TPU v7x, 256 devices: a whole 4x4x8 slice. The times are simulated.
256 devices in a mesh: ctx: 32 (over x, y, core), head: 8 (over z).
Axes of the slice: x: 4, y: 4, z: 8, core: 2. Of those that a mesh axis runs over, the one named last changes fastest.
Arguments:
- mixer_input: bfloat16 [4096, 16384], P('ctx', 'head'), may hold values from -1200 to 1200
- gate: bfloat16 [4096, 16384], P('ctx', 'head'), may hold values from -6 to 6
- in_b: bfloat16 [4096, 2048], P('ctx', 'head'), may hold values from -6 to 6
- in_c: bfloat16 [4096, 2048], P('ctx', 'head'), may hold values from -0.375 to 0.375
- step_size: float32 [256, 4096], P('head', 'ctx'), may hold values from 0.5 to 2
- log_decay: float32 [256, 4096], P('head', 'ctx'), may hold values from -0.7 to 0
- skip_gain: float32 [256], P('head'), may hold values from 1 to 4
- norm_gain: float32 [16384], P('head'), may hold values from 0.5 to 1.5
- query_weight: bfloat16 [8, 2048, 1024], P('head'), may hold values from -0.125 to 0.125
- keys: bfloat16 [4096, 1024], P('ctx', 'head'), may hold values from -500 to 500
- values: bfloat16 [4096, 1024], P('ctx', 'head'), may hold values from -6 to 6
- doc_lengths: int32 [16], replicated, may hold values from 1 to 2176, 4096 in all
Outputs:
- mixer_out: bfloat16 [4096, 16384], P('ctx', 'head')
- attn_out: bfloat16 [4096, 8192], P('ctx', 'head')
Inputs may be any that keep to these rules, and one draw needn't show every extreme that they name: `doc_lengths`: the documents lie end to end in token order, sum to 4096 tokens, and the longest has exactly 2176 tokens.
All inputs are finite; a program needn't handle non-finite values.
Results may differ from a plain program's by a relative error of at most 0.0151.
The roundings to bfloat16 on the way count: a program that leaves them out, or rounds other values in their place, can miss the bound.
Values may be sent and summed in bfloat16 or wider, within the bound.
No kernel may reach another device: no remote copies, remote signals or barrier semaphores. Data moves between devices by JAX's collectives and lax.ppermute only.
A program may use at most 192 MiB of HBM per device.

v0:
```python
import jax
import jax.numpy as jnp
from jax import lax
from jax.sharding import PartitionSpec as P

MIXER_HEADS = 256
HEAD_DIM = 64
STATE = 256
GROUPS = 8
QHEADS = 64
ATT_DIM = 128


EPSILON = 1e-05
NEG_FILL = -1e30
BLOCK_ROWS = 1024


def prefix(part, axis, combine, identity):
    place = lax.axis_index(axis)
    gathered = jax.tree.map(lambda a: lax.all_gather(a, axis), part)
    state = jax.tree.map(lambda a, e: jnp.zeros_like(a) + jnp.asarray(e, a.dtype), part, identity)

    def one(turn, state):
        return combine(
            state, jax.tree.map(lambda a: lax.dynamic_index_in_dim(a, turn, 0, False), gathered)
        )

    return lax.fori_loop(0, place, one, state)


def segment_ids(positions, doc_lengths):
    doc_starts = jnp.cumsum(doc_lengths) - doc_lengths
    hits = (doc_starts[None, :] <= positions[:, None]).astype(jnp.int32)
    return jnp.sum(hits, axis=1) - 1


def combine_states(earlier, later):
    decay_early, state_early = earlier
    decay_late, state_late = later
    return (decay_early * decay_late, decay_late[:, :, None, None] * state_early + state_late)


def shards(
    mixer_input,
    gate,
    in_b,
    in_c,
    step_size,
    log_decay,
    skip_gain,
    norm_gain,
    query_weight,
    keys,
    values,
    doc_lengths,
):
    highest = lax.Precision.HIGHEST
    tok_rows = mixer_input.shape[0]
    groups_dev = query_weight.shape[0]
    heads_dev = step_size.shape[0]
    head_group = heads_dev // groups_dev
    query_group = QHEADS // GROUPS
    shard_index = lax.axis_index("ctx")
    first_pos = shard_index * tok_rows
    row_index = jnp.arange(tok_rows, dtype=jnp.int32)
    own_pos = first_pos + row_index
    own_docs = segment_ids(own_pos, doc_lengths)
    prev_doc = segment_ids(jnp.reshape(first_pos - 1, (1,)), doc_lengths)[0]
    input_f32 = mixer_input.reshape(tok_rows, groups_dev, head_group, HEAD_DIM).astype(jnp.float32)
    state_in = in_b.reshape(tok_rows, groups_dev, STATE)
    state_out = in_c.reshape(tok_rows, groups_dev, STATE)
    upper_ones = (row_index[:, None] <= row_index[None, :]).astype(jnp.float32)
    cum_decay = jnp.dot(log_decay, upper_ones, precision=highest).reshape(
        groups_dev, head_group, tok_rows
    )
    step_rows = step_size.reshape(groups_dev, head_group, tok_rows)
    last_doc = (own_docs == own_docs[-1]).astype(jnp.float32)
    end_weight = jnp.exp(cum_decay[:, :, -1:] - cum_decay) * last_doc[None, None, :] * step_rows
    weighted = input_f32 * jnp.transpose(end_weight, (2, 0, 1))[..., None]
    local_state = jnp.einsum(
        "sgn,sgjp->gjnp", state_in.astype(jnp.float32), weighted, precision=highest
    )
    carry_mask = (own_docs == prev_doc).astype(jnp.float32)
    block_decay = jnp.exp(cum_decay[:, :, -1]) * carry_mask[-1]
    identity = (jnp.ones_like(block_decay), jnp.zeros_like(local_state))
    scanned = prefix((block_decay, local_state), "ctx", combine_states, identity)
    incoming = scanned[1]
    same_doc = (own_docs[:, None] == own_docs[None, :]) & (row_index[:, None] >= row_index[None, :])
    log_gap = cum_decay[:, :, :, None] - cum_decay[:, :, None, :]
    decay_matrix = jnp.exp(jnp.where(same_doc[None, None], log_gap, -jnp.inf))
    pair_products = jnp.einsum(
        "tgn,sgn->gts", state_out, state_in, preferred_element_type=jnp.float32
    )
    mixing = pair_products[:, None] * decay_matrix * step_rows[:, :, None, :]
    local_out = jnp.einsum("gjts,sgjp->tgjp", mixing, input_f32, precision=highest)
    carry_weight = jnp.exp(cum_decay) * carry_mask[None, None, :]
    carried_out = (
        jnp.einsum("tgn,gjnp->tgjp", state_out.astype(jnp.float32), incoming, precision=highest)
        * jnp.transpose(carry_weight, (2, 0, 1))[..., None]
    )
    skip_rows = skip_gain.reshape(groups_dev, head_group)[None, :, :, None] * input_f32
    mixer_full = (local_out + carried_out + skip_rows).reshape(tok_rows, -1)
    gated = mixer_full * jax.nn.silu(gate.astype(jnp.float32))
    square_local = jnp.sum(gated * gated, axis=1)
    square_sum = lax.psum(square_local, "head")
    mixer_out = (
        gated
        * lax.rsqrt(square_sum / (MIXER_HEADS * HEAD_DIM) + EPSILON)[:, None]
        * norm_gain[None, :]
    ).astype(jnp.bfloat16)
    query = jnp.einsum(
        "tgf,gfo->tgo",
        mixer_out.reshape(tok_rows, groups_dev, -1),
        query_weight,
        preferred_element_type=jnp.float32,
    )
    query = query.astype(jnp.bfloat16).reshape(tok_rows, groups_dev, query_group, ATT_DIM)

    def make_visit(query_rows, query_pos):
        query_docs = segment_ids(query_pos, doc_lengths)

        def attend_block(carried, key_rows, value_rows, offset):
            key_count = key_rows.shape[0]
            key_pos = offset + jnp.arange(key_count, dtype=jnp.int32)
            key_docs = segment_ids(key_pos, doc_lengths)
            visible = (query_docs[:, None] == key_docs[None, :]) & (
                key_pos[None, :] <= query_pos[:, None]
            )
            key_heads = key_rows.reshape(key_count, groups_dev, ATT_DIM)
            value_heads = value_rows.reshape(key_count, groups_dev, ATT_DIM)
            scores = jnp.einsum(
                "tgqa,rga->gqtr", query_rows, key_heads, preferred_element_type=jnp.float32
            ) * ATT_DIM ** (-0.5)
            scores = jnp.where(visible[None, None], scores, NEG_FILL)
            best_old, total_old, accum_old = carried
            best_new = jnp.maximum(best_old, jnp.max(scores, axis=-1))
            weights = jnp.where(visible[None, None], jnp.exp(scores - best_new[..., None]), 0.0)
            rescale = jnp.exp(best_old - best_new)
            total_new = total_old * rescale + jnp.sum(weights, axis=-1)
            accum_new = accum_old * rescale[..., None] + jnp.einsum(
                "gqtr,rga->gqta",
                weights.astype(jnp.bfloat16),
                value_heads,
                preferred_element_type=jnp.float32,
            )
            return (best_new, total_new, accum_new)

        def attend_piece(carried, key_rows, value_rows):
            key_count = key_rows.shape[0]
            block_count = key_count // BLOCK_ROWS
            key_blocks = key_rows.reshape(block_count, BLOCK_ROWS, -1)
            value_blocks = value_rows.reshape(block_count, BLOCK_ROWS, -1)

            def block_turn(inner, scan_item):
                key_part, value_part, block_index = scan_item
                return (attend_block(inner, key_part, value_part, block_index * BLOCK_ROWS), None)

            carried, _ = lax.scan(
                block_turn,
                carried,
                (key_blocks, value_blocks, jnp.arange(block_count, dtype=jnp.int32)),
            )
            return carried

        def visit(carried, key_rows, value_rows, offset):
            return attend_piece(carried, key_rows, value_rows)

        return visit

    initial = (
        jnp.full((groups_dev, query_group, tok_rows), NEG_FILL, jnp.float32),
        jnp.zeros((groups_dev, query_group, tok_rows), jnp.float32),
        jnp.zeros((groups_dev, query_group, tok_rows, ATT_DIM), jnp.float32),
    )
    visit_chosen = make_visit(query, own_pos)
    final_carry = visit_chosen(
        initial,
        lax.all_gather(keys, "ctx", axis=0, tiled=True),
        lax.all_gather(values, "ctx", axis=0, tiled=True),
        jnp.int32(0),
    )
    _, score_total, accum = final_carry
    attended = accum / score_total[..., None]
    attn_out = jnp.transpose(attended, (2, 0, 1, 3)).reshape(tok_rows, -1).astype(jnp.bfloat16)
    return (mixer_out, attn_out)


def solution(mesh):
    return jax.shard_map(
        shards,
        mesh=mesh,
        in_specs=(
            P("ctx", "head"),
            P("ctx", "head"),
            P("ctx", "head"),
            P("ctx", "head"),
            P("head", "ctx"),
            P("head", "ctx"),
            P("head"),
            P("head"),
            P("head", None, None),
            P("ctx", "head"),
            P("ctx", "head"),
            P(),
        ),
        out_specs=(P("ctx", "head"), P("ctx", "head")),
        check_vma=False,
    )
```

profile of v0, /device:TPU:31, one launch (start us, length us, event | category | flops | bytes accessed | tf_op | source)
XLA Modules:
  0.0 646.1 jit_solution(614431955727706993)
XLA Ops:
  20.1 19.1 %all-gather = f32[32,32,1]{1,2,0:T(1,128)S(1)} all-gather(f32[1,32,1]{1,2,0:T(1,128)S(1)} %get-tuple-element.350), channel_id=2, replica_groups=mesh['ctx'=32,'head'=8] {'ctx'}, dimensions={0}, use_global_device_ids=true | all-gather | bytes 4224 | tf_op jit(solution)/shard_map/all_gather | solution.py:21
  39.5 186.4 %all-gather.10.cloned.1.call-done = f32[32,32,256,64]{2,3,1,0:T(8,128)} async-done(((f32[1,32,256,64]{2,3,1,0:T(8,128)}), f32[32,32,256,64]{2,3,1,0:T(8,128)}) %all-gather.10.cloned.1.call-update) | async-done | bytes 67108880 | tf_op jit(solution)/shard_map/all_gather | solution.py:21
  228.3 340.6 %while.29 = (s32[]{:T(128)}, f32[1,32,256,64]{3,2,1,0:T(8,128)}, s32[]{:T(128)}, f32[32,1,32]{2,1,0:T(1,128)S(1)}, f32[32,1,32,256,64]{3,4,2,0,1:T(8,128)}, /*index=5*/s32[]{:T(128)}, s32[]{:T(128)}, s32[]{:T(128)}) while((s32[]{:T(128)}, f32[1,32,256,64]{3,2,1,0:T(8,128)}, s32[]{:T(128)}, f32[32,1,32]{2,1,0:T(1,128)S(1)}, ...), condition=%wide.region_4.5_spmd, body=%wide.region_3.4_spmd.sunk | while | flops 1048581 | bytes 14680575 | solution.py:29
  230.0 2.7 copy.85
  232.8 6.5 %bitcast_add_fusion.4 = f32[1,32,256,64]{3,2,1,0:T(8,128)} fusion(f32[1,1,32,256,64]{4,3,2,1,0:T(8,128)} %copy.85, f32[1,32,256,64]{3,2,1,0:T(8,128)} %get-tuple-element.469, f32[32]{0:T(128)S(1)} %dynamic-slice_bitcast_fusion.2), kind=kLoop, calls=%fused_computation.1.clone.1 | loop fusion | flops 1048576 | bytes 6291584 | tf_op jit(solution)/shard_map/while/body/add | solution.py:41
  241.0 2.7 copy.85
  243.8 6.5 %bitcast_add_fusion.4 = f32[1,32,256,64]{3,2,1,0:T(8,128)} fusion(f32[1,1,32,256,64]{4,3,2,1,0:T(8,128)} %copy.85, f32[1,32,256,64]{3,2,1,0:T(8,128)} %get-tuple-element.469, f32[32]{0:T(128)S(1)} %dynamic-slice_bitcast_fusion.2), kind=kLoop, calls=%fused_computation.1.clone.1 | loop fusion | flops 1048576 | bytes 6291584 | tf_op jit(solution)/shard_map/while/body/add | solution.py:41
  252.0 2.7 copy.85
  254.8 6.5 %bitcast_add_fusion.4 = f32[1,32,256,64]{3,2,1,0:T(8,128)} fusion(f32[1,1,32,256,64]{4,3,2,1,0:T(8,128)} %copy.85, f32[1,32,256,64]{3,2,1,0:T(8,128)} %get-tuple-element.469, f32[32]{0:T(128)S(1)} %dynamic-slice_bitcast_fusion.2), kind=kLoop, calls=%fused_computation.1.clone.1 | loop fusion | flops 1048576 | bytes 6291584 | tf_op jit(solution)/shard_map/while/body/add | solution.py:41
  263.0 2.7 copy.85
  265.7 6.5 %bitcast_add_fusion.4 = f32[1,32,256,64]{3,2,1,0:T(8,128)} fusion(f32[1,1,32,256,64]{4,3,2,1,0:T(8,128)} %copy.85, f32[1,32,256,64]{3,2,1,0:T(8,128)} %get-tuple-element.469, f32[32]{0:T(128)S(1)} %dynamic-slice_bitcast_fusion.2), kind=kLoop, calls=%fused_computation.1.clone.1 | loop fusion | flops 1048576 | bytes 6291584 | tf_op jit(solution)/shard_map/while/body/add | solution.py:41
  274.0 2.7 copy.85
  276.8 6.5 %bitcast_add_fusion.4 = f32[1,32,256,64]{3,2,1,0:T(8,128)} fusion(f32[1,1,32,256,64]{4,3,2,1,0:T(8,128)} %copy.85, f32[1,32,256,64]{3,2,1,0:T(8,128)} %get-tuple-element.469, f32[32]{0:T(128)S(1)} %dynamic-slice_bitcast_fusion.2), kind=kLoop, calls=%fused_computation.1.clone.1 | loop fusion | flops 1048576 | bytes 6291584 | tf_op jit(solution)/shard_map/while/body/add | solution.py:41
  285.0 2.7 copy.85
  287.8 6.5 %bitcast_add_fusion.4 = f32[1,32,256,64]{3,2,1,0:T(8,128)} fusion(f32[1,1,32,256,64]{4,3,2,1,0:T(8,128)} %copy.85, f32[1,32,256,64]{3,2,1,0:T(8,128)} %get-tuple-element.469, f32[32]{0:T(128)S(1)} %dynamic-slice_bitcast_fusion.2), kind=kLoop, calls=%fused_computation.1.clone.1 | loop fusion | flops 1048576 | bytes 6291584 | tf_op jit(solution)/shard_map/while/body/add | solution.py:41
  296.0 2.7 copy.85
  298.8 6.5 %bitcast_add_fusion.4 = f32[1,32,256,64]{3,2,1,0:T(8,128)} fusion(f32[1,1,32,256,64]{4,3,2,1,0:T(8,128)} %copy.85, f32[1,32,256,64]{3,2,1,0:T(8,128)} %get-tuple-element.469, f32[32]{0:T(128)S(1)} %dynamic-slice_bitcast_fusion.2), kind=kLoop, calls=%fused_computation.1.clone.1 | loop fusion | flops 1048576 | bytes 6291584 | tf_op jit(solution)/shard_map/while/body/add | solution.py:41
  307.0 2.7 copy.85
  309.7 6.5 %bitcast_add_fusion.4 = f32[1,32,256,64]{3,2,1,0:T(8,128)} fusion(f32[1,1,32,256,64]{4,3,2,1,0:T(8,128)} %copy.85, f32[1,32,256,64]{3,2,1,0:T(8,128)} %get-tuple-element.469, f32[32]{0:T(128)S(1)} %dynamic-slice_bitcast_fusion.2), kind=kLoop, calls=%fused_computation.1.clone.1 | loop fusion | flops 1048576 | bytes 6291584 | tf_op jit(solution)/shard_map/while/body/add | solution.py:41
  318.0 2.7 copy.85
  320.7 6.5 %bitcast_add_fusion.4 = f32[1,32,256,64]{3,2,1,0:T(8,128)} fusion(f32[1,1,32,256,64]{4,3,2,1,0:T(8,128)} %copy.85, f32[1,32,256,64]{3,2,1,0:T(8,128)} %get-tuple-element.469, f32[32]{0:T(128)S(1)} %dynamic-slice_bitcast_fusion.2), kind=kLoop, calls=%fused_computation.1.clone.1 | loop fusion | flops 1048576 | bytes 6291584 | tf_op jit(solution)/shard_map/while/body/add | solution.py:41
  329.0 2.7 copy.85
  331.7 6.5 %bitcast_add_fusion.4 = f32[1,32,256,64]{3,2,1,0:T(8,128)} fusion(f32[1,1,32,256,64]{4,3,2,1,0:T(8,128)} %copy.85, f32[1,32,256,64]{3,2,1,0:T(8,128)} %get-tuple-element.469, f32[32]{0:T(128)S(1)} %dynamic-slice_bitcast_fusion.2), kind=kLoop, calls=%fused_computation.1.clone.1 | loop fusion | flops 1048576 | bytes 6291584 | tf_op jit(solution)/shard_map/while/body/add | solution.py:41
  342.7 6.5 %bitcast_add_fusion.4 = f32[1,32,256,64]{3,2,1,0:T(8,128)} fusion(f32[1,1,32,256,64]{4,3,2,1,0:T(8,128)} %copy.85, f32[1,32,256,64]{3,2,1,0:T(8,128)} %get-tuple-element.469, f32[32]{0:T(128)S(1)} %dynamic-slice_bitcast_fusion.2), kind=kLoop, calls=%fused_computation.1.clone.1 | loop fusion | flops 1048576 | bytes 6291584 | tf_op jit(solution)/shard_map/while/body/add | solution.py:41
  351.0 2.7 copy.85
  353.7 6.5 %bitcast_add_fusion.4 = f32[1,32,256,64]{3,2,1,0:T(8,128)} fusion(f32[1,1,32,256,64]{4,3,2,1,0:T(8,128)} %copy.85, f32[1,32,256,64]{3,2,1,0:T(8,128)} %get-tuple-element.469, f32[32]{0:T(128)S(1)} %dynamic-slice_bitcast_fusion.2), kind=kLoop, calls=%fused_computation.1.clone.1 | loop fusion | flops 1048576 | bytes 6291584 | tf_op jit(solution)/shard_map/while/body/add | solution.py:41
  362.0 2.7 copy.85
  364.7 6.5 %bitcast_add_fusion.4 = f32[1,32,256,64]{3,2,1,0:T(8,128)} fusion(f32[1,1,32,256,64]{4,3,2,1,0:T(8,128)} %copy.85, f32[1,32,256,64]{3,2,1,0:T(8,128)} %get-tuple-element.469, f32[32]{0:T(128)S(1)} %dynamic-slice_bitcast_fusion.2), kind=kLoop, calls=%fused_computation.1.clone.1 | loop fusion | flops 1048576 | bytes 6291584 | tf_op jit(solution)/shard_map/while/body/add | solution.py:41
  372.9 2.7 copy.85
  375.7 6.5 %bitcast_add_fusion.4 = f32[1,32,256,64]{3,2,1,0:T(8,128)} fusion(f32[1,1,32,256,64]{4,3,2,1,0:T(8,128)} %copy.85, f32[1,32,256,64]{3,2,1,0:T(8,128)} %get-tuple-element.469, f32[32]{0:T(128)S(1)} %dynamic-slice_bitcast_fusion.2), kind=kLoop, calls=%fused_computation.1.clone.1 | loop fusion | flops 1048576 | bytes 6291584 | tf_op jit(solution)/shard_map/while/body/add | solution.py:41
  386.7 6.5 %bitcast_add_fusion.4 = f32[1,32,256,64]{3,2,1,0:T(8,128)} fusion(f32[1,1,32,256,64]{4,3,2,1,0:T(8,128)} %copy.85, f32[1,32,256,64]{3,2,1,0:T(8,128)} %get-tuple-element.469, f32[32]{0:T(128)S(1)} %dynamic-slice_bitcast_fusion.2), kind=kLoop, calls=%fused_computation.1.clone.1 | loop fusion | flops 1048576 | bytes 6291584 | tf_op jit(solution)/shard_map/while/body/add | solution.py:41
  397.6 6.5 %bitcast_add_fusion.4 = f32[1,32,256,64]{3,2,1,0:T(8,128)} fusion(f32[1,1,32,256,64]{4,3,2,1,0:T(8,128)} %copy.85, f32[1,32,256,64]{3,2,1,0:T(8,128)} %get-tuple-element.469, f32[32]{0:T(128)S(1)} %dynamic-slice_bitcast_fusion.2), kind=kLoop, calls=%fused_computation.1.clone.1 | loop fusion | flops 1048576 | bytes 6291584 | tf_op jit(solution)/shard_map/while/body/add | solution.py:41
  408.6 6.5 %bitcast_add_fusion.4 = f32[1,32,256,64]{3,2,1,0:T(8,128)} fusion(f32[1,1,32,256,64]{4,3,2,1,0:T(8,128)} %copy.85, f32[1,32,256,64]{3,2,1,0:T(8,128)} %get-tuple-element.469, f32[32]{0:T(128)S(1)} %dynamic-slice_bitcast_fusion.2), kind=kLoop, calls=%fused_computation.1.clone.1 | loop fusion | flops 1048576 | bytes 6291584 | tf_op jit(solution)/shard_map/while/body/add | solution.py:41
  419.6 6.5 %bitcast_add_fusion.4 = f32[1,32,256,64]{3,2,1,0:T(8,128)} fusion(f32[1,1,32,256,64]{4,3,2,1,0:T(8,128)} %copy.85, f32[1,32,256,64]{3,2,1,0:T(8,128)} %get-tuple-element.469, f32[32]{0:T(128)S(1)} %dynamic-slice_bitcast_fusion.2), kind=kLoop, calls=%fused_computation.1.clone.1 | loop fusion | flops 1048576 | bytes 6291584 | tf_op jit(solution)/shard_map/while/body/add | solution.py:41
  430.6 6.5 %bitcast_add_fusion.4 = f32[1,32,256,64]{3,2,1,0:T(8,128)} fusion(f32[1,1,32,256,64]{4,3,2,1,0:T(8,128)} %copy.85, f32[1,32,256,64]{3,2,1,0:T(8,128)} %get-tuple-element.469, f32[32]{0:T(128)S(1)} %dynamic-slice_bitcast_fusion.2), kind=kLoop, calls=%fused_computation.1.clone.1 | loop fusion | flops 1048576 | bytes 6291584 | tf_op jit(solution)/shard_map/while/body/add | solution.py:41
  441.6 6.5 %bitcast_add_fusion.4 = f32[1,32,256,64]{3,2,1,0:T(8,128)} fusion(f32[1,1,32,256,64]{4,3,2,1,0:T(8,128)} %copy.85, f32[1,32,256,64]{3,2,1,0:T(8,128)} %get-tuple-element.469, f32[32]{0:T(128)S(1)} %dynamic-slice_bitcast_fusion.2), kind=kLoop, calls=%fused_computation.1.clone.1 | loop fusion | flops 1048576 | bytes 6291584 | tf_op jit(solution)/shard_map/while/body/add | solution.py:41
  452.6 6.5 %bitcast_add_fusion.4 = f32[1,32,256,64]{3,2,1,0:T(8,128)} fusion(f32[1,1,32,256,64]{4,3,2,1,0:T(8,128)} %copy.85, f32[1,32,256,64]{3,2,1,0:T(8,128)} %get-tuple-element.469, f32[32]{0:T(128)S(1)} %dynamic-slice_bitcast_fusion.2), kind=kLoop, calls=%fused_computation.1.clone.1 | loop fusion | flops 1048576 | bytes 6291584 | tf_op jit(solution)/shard_map/while/body/add | solution.py:41
  460.8 2.7 copy.85
  463.5 6.5 %bitcast_add_fusion.4 = f32[1,32,256,64]{3,2,1,0:T(8,128)} fusion(f32[1,1,32,256,64]{4,3,2,1,0:T(8,128)} %copy.85, f32[1,32,256,64]{3,2,1,0:T(8,128)} %get-tuple-element.469, f32[32]{0:T(128)S(1)} %dynamic-slice_bitcast_fusion.2), kind=kLoop, calls=%fused_computation.1.clone.1 | loop fusion | flops 1048576 | bytes 6291584 | tf_op jit(solution)/shard_map/while/body/add | solution.py:41
  471.8 2.7 copy.85
  474.5 6.5 %bitcast_add_fusion.4 = f32[1,32,256,64]{3,2,1,0:T(8,128)} fusion(f32[1,1,32,256,64]{4,3,2,1,0:T(8,128)} %copy.85, f32[1,32,256,64]{3,2,1,0:T(8,128)} %get-tuple-element.469, f32[32]{0:T(128)S(1)} %dynamic-slice_bitcast_fusion.2), kind=kLoop, calls=%fused_computation.1.clone.1 | loop fusion | flops 1048576 | bytes 6291584 | tf_op jit(solution)/shard_map/while/body/add | solution.py:41
  482.8 2.7 copy.85
  485.5 6.5 %bitcast_add_fusion.4 = f32[1,32,256,64]{3,2,1,0:T(8,128)} fusion(f32[1,1,32,256,64]{4,3,2,1,0:T(8,128)} %copy.85, f32[1,32,256,64]{3,2,1,0:T(8,128)} %get-tuple-element.469, f32[32]{0:T(128)S(1)} %dynamic-slice_bitcast_fusion.2), kind=kLoop, calls=%fused_computation.1.clone.1 | loop fusion | flops 1048576 | bytes 6291584 | tf_op jit(solution)/shard_map/while/body/add | solution.py:41
  496.5 6.5 %bitcast_add_fusion.4 = f32[1,32,256,64]{3,2,1,0:T(8,128)} fusion(f32[1,1,32,256,64]{4,3,2,1,0:T(8,128)} %copy.85, f32[1,32,256,64]{3,2,1,0:T(8,128)} %get-tuple-element.469, f32[32]{0:T(128)S(1)} %dynamic-slice_bitcast_fusion.2), kind=kLoop, calls=%fused_computation.1.clone.1 | loop fusion | flops 1048576 | bytes 6291584 | tf_op jit(solution)/shard_map/while/body/add | solution.py:41
  507.5 6.5 %bitcast_add_fusion.4 = f32[1,32,256,64]{3,2,1,0:T(8,128)} fusion(f32[1,1,32,256,64]{4,3,2,1,0:T(8,128)} %copy.85, f32[1,32,256,64]{3,2,1,0:T(8,128)} %get-tuple-element.469, f32[32]{0:T(128)S(1)} %dynamic-slice_bitcast_fusion.2), kind=kLoop, calls=%fused_computation.1.clone.1 | loop fusion | flops 1048576 | bytes 6291584 | tf_op jit(solution)/shard_map/while/body/add | solution.py:41
  518.5 6.5 %bitcast_add_fusion.4 = f32[1,32,256,64]{3,2,1,0:T(8,128)} fusion(f32[1,1,32,256,64]{4,3,2,1,0:T(8,128)} %copy.85, f32[1,32,256,64]{3,2,1,0:T(8,128)} %get-tuple-element.469, f32[32]{0:T(128)S(1)} %dynamic-slice_bitcast_fusion.2), kind=kLoop, calls=%fused_computation.1.clone.1 | loop fusion | flops 1048576 | bytes 6291584 | tf_op jit(solution)/shard_map/while/body/add | solution.py:41
  529.4 6.5 %bitcast_add_fusion.4 = f32[1,32,256,64]{3,2,1,0:T(8,128)} fusion(f32[1,1,32,256,64]{4,3,2,1,0:T(8,128)} %copy.85, f32[1,32,256,64]{3,2,1,0:T(8,128)} %get-tuple-element.469, f32[32]{0:T(128)S(1)} %dynamic-slice_bitcast_fusion.2), kind=kLoop, calls=%fused_computation.1.clone.1 | loop fusion | flops 1048576 | bytes 6291584 | tf_op jit(solution)/shard_map/while/body/add | solution.py:41
  540.4 6.5 %bitcast_add_fusion.4 = f32[1,32,256,64]{3,2,1,0:T(8,128)} fusion(f32[1,1,32,256,64]{4,3,2,1,0:T(8,128)} %copy.85, f32[1,32,256,64]{3,2,1,0:T(8,128)} %get-tuple-element.469, f32[32]{0:T(128)S(1)} %dynamic-slice_bitcast_fusion.2), kind=kLoop, calls=%fused_computation.1.clone.1 | loop fusion | flops 1048576 | bytes 6291584 | tf_op jit(solution)/shard_map/while/body/add | solution.py:41
  551.4 6.5 %bitcast_add_fusion.4 = f32[1,32,256,64]{3,2,1,0:T(8,128)} fusion(f32[1,1,32,256,64]{4,3,2,1,0:T(8,128)} %copy.85, f32[1,32,256,64]{3,2,1,0:T(8,128)} %get-tuple-element.469, f32[32]{0:T(128)S(1)} %dynamic-slice_bitcast_fusion.2), kind=kLoop, calls=%fused_computation.1.clone.1 | loop fusion | flops 1048576 | bytes 6291584 | tf_op jit(solution)/shard_map/while/body/add | solution.py:41
  559.6 2.7 copy.85
  562.4 6.5 %bitcast_add_fusion.4 = f32[1,32,256,64]{3,2,1,0:T(8,128)} fusion(f32[1,1,32,256,64]{4,3,2,1,0:T(8,128)} %copy.85, f32[1,32,256,64]{3,2,1,0:T(8,128)} %get-tuple-element.469, f32[32]{0:T(128)S(1)} %dynamic-slice_bitcast_fusion.2), kind=kLoop, calls=%fused_computation.1.clone.1 | loop fusion | flops 1048576 | bytes 6291584 | tf_op jit(solution)/shard_map/while/body/add | solution.py:41
  568.9 5.7 fusion.49
  574.6 3.6 fusion.46
  580.2 13.9 %psum.7 = f32[128]{0:T(128)S(1)} all-reduce(f32[128]{0:T(128)S(1)} %multiply_reduce_fusion), channel_id=1, replica_groups=mesh['ctx'=32,'head'=8] {'head'}, use_global_device_ids=true, to_apply=%region_6.7 | all-reduce | flops 128 | bytes 1024 | tf_op jit(solution)/shard_map/psum | solution.py:106
  594.5 3.1 fusion.55
  597.7 40.7 %while.30 = (s32[]{:T(128)}, f32[1,8,128]{2,1,0:T(8,128)S(1)}, f32[1,8,128]{2,1,0:T(8,128)S(1)}, f32[1,8,128,128]{3,2,1,0:T(8,128)S(1)}, s32[128]{0:T(128)S(1)},...) while((s32[]{:T(128)}, f32[1,8,128]{2,1,0:T(8,128)S(1)}, ...), condition=%wide.region_11.12_spmd.clone, body=%wide.region_7.11_spmd.clone.sunk | while | flops 551345280 | bytes 31816460 | solution.py:159
  599.4 3.6 fusion.92
  603.1 3.8 fusion.95
  609.6 3.6 fusion.92
  613.3 3.8 fusion.95
  619.8 3.6 fusion.92
  623.4 3.8 fusion.95
  630.0 3.6 fusion.92
  633.6 3.8 fusion.95
  (181 shorter events, 119.3 us)
Async XLA Ops:
  7.2 9.0 %copy-start = (bf16[128,256]{1,0:T(8,128)(2,1)S(1)}, bf16[128,256]{1,0:T(8,128)(2,1)}, u32[]{:S(2)}) copy-start(bf16[128,256]{1,0:T(8,128)(2,1)} %param.18) | copy-start | bytes 196612
  7.2 218.7 %all-gather.10.cloned.1.call-start = ((), (), s32[]{:S(2)}) async-start(), calls=%async_computation.2 | async-start | bytes 69206016 | tf_op jit(solution)/shard_map/all_gather | solution.py:21
  14.7 24.6 %copy-start.4 = (bf16[128,256]{1,0:T(8,128)(2,1)S(1)}, bf16[128,256]{1,0:T(8,128)(2,1)}, u32[]{:S(2)}) copy-start(bf16[128,256]{1,0:T(8,128)(2,1)} %param.19) | copy-start | bytes 196612
  18.5 579.1 %all-gather.6.cloned.1.call-start = ((), (), s32[]{:S(2)}) async-start(), calls=%async_computation | async-start | bytes 1081344 | tf_op jit(solution)/shard_map/all_gather | solution.py:179
  19.2 578.4 %all-gather.8.cloned.1.call-start = ((), (), s32[]{:S(2)}) async-start(), calls=%async_computation.1 | async-start | bytes 1081344 | tf_op jit(solution)/shard_map/all_gather | solution.py:180
  568.9 5.7 copy-start.5
  568.9 5.7 copy-start.7
  574.5 5.2 copy-start.3
  574.6 19.5 %copy-start.6 = (f32[2048]{0:T(1024)S(1)}, f32[2048]{0:T(1024)}, u32[]{:S(2)}) copy-start(f32[2048]{0:T(1024)} %param.23) | copy-start | bytes 24580
  594.4 3.2 copy-start.2
  603.1 3.8 copy-start.1
  613.2 3.8 copy-start.1
  623.4 3.8 copy-start.1
  633.6 3.8 copy-start.1
Sparse Core Ops, SparseCore 0:
  18.6 207.1 all-gather.9
  228.4 46.6 all-gather.5
  277.6 47.1 all-gather.7
where the time goes:
time: 648 us; the launch traced here: 646 us
  other arithmetic  211 us (33%)
  waiting for transfers between devices  188 us (29%)
  local copies, waits for them, and re-layouts  151 us (23%)
  matrix products  45.3 us (7%)
  blocking collectives  33 us (5%)
  between operations  14.7 us (2%)
    add x31, other arithmetic, combine_states(): decay_late[:, :, None, None] * state_early + state_late  201 us
    all_gather x1, waiting for transfers between devices, prefix(): gathered = jax.tree.map(lambda a: lax.all_gather(a, axis), part)  186 us
    dynamic_slice x62, local copies, waits for them, and re-layouts, one(): lax.dynamic_index_in_dim(a, turn, 0, False)  139 us
    all_gather x1, blocking collectives, prefix(): gathered = jax.tree.map(lambda a: lax.all_gather(a, axis), part)  19.1 us
    dot_general x4, matrix products, attend_block(): jnp.einsum('gqtr,rga->gqta', weights.astype(jnp.bfloat16), value_heads, p...  15 us
    dot_general x4, matrix products, attend_block(): jnp.einsum('tgqa,rga->gqtr', query_rows, key_heads, preferred_element_typ...  14.6 us
    psum x1, blocking collectives, shards(): square_sum = lax.psum(square_local, 'head')  13.9 us
  transfers between devices with their start and end apart: 3, of which 1 were waited for; matrix products, arithmetic and copies ran while one was open for 55% of the time, Pallas kernels for 0%

commit v1 on v0

--- a/solution.py
+++ b/solution.py
@@ -16,29 +16,10 @@
 BLOCK_ROWS = 1024
 
 
-def prefix(part, axis, combine, identity):
-    place = lax.axis_index(axis)
-    gathered = jax.tree.map(lambda a: lax.all_gather(a, axis), part)
-    state = jax.tree.map(lambda a, e: jnp.zeros_like(a) + jnp.asarray(e, a.dtype), part, identity)
-
-    def one(turn, state):
-        return combine(
-            state, jax.tree.map(lambda a: lax.dynamic_index_in_dim(a, turn, 0, False), gathered)
-        )
-
-    return lax.fori_loop(0, place, one, state)
-
-
 def segment_ids(positions, doc_lengths):
     doc_starts = jnp.cumsum(doc_lengths) - doc_lengths
     hits = (doc_starts[None, :] <= positions[:, None]).astype(jnp.int32)
     return jnp.sum(hits, axis=1) - 1
-
-
-def combine_states(earlier, later):
-    decay_early, state_early = earlier
-    decay_late, state_late = later
-    return (decay_early * decay_late, decay_late[:, :, None, None] * state_early + state_late)
 
 
 def shards(
@@ -82,10 +63,27 @@
         "sgn,sgjp->gjnp", state_in.astype(jnp.float32), weighted, precision=highest
     )
     carry_mask = (own_docs == prev_doc).astype(jnp.float32)
-    block_decay = jnp.exp(cum_decay[:, :, -1]) * carry_mask[-1]
-    identity = (jnp.ones_like(block_decay), jnp.zeros_like(local_state))
-    scanned = prefix((block_decay, local_state), "ctx", combine_states, identity)
-    incoming = scanned[1]
+    ctx_count = lax.axis_size("ctx")
+    owned = heads_dev // ctx_count
+    block_log = jnp.where(carry_mask[-1] > 0, cum_decay[:, :, -1], -jnp.inf).reshape(heads_dev)
+    all_log = lax.all_gather(block_log, "ctx")
+    mine_log = lax.dynamic_slice_in_dim(all_log, shard_index * owned, owned, 1)
+    block_row = jnp.arange(ctx_count, dtype=jnp.int32)
+    between = (block_row[None, :, None] < block_row[None, None, :]) & (
+        block_row[None, None, :] < block_row[:, None, None]
+    )
+    log_span = jnp.sum(
+        jnp.where(between[None], jnp.transpose(mine_log)[:, None, None, :], 0.0), axis=-1
+    )
+    earlier = block_row[:, None] > block_row[None, :]
+    transfer = jnp.where(earlier[None], jnp.exp(log_span), 0.0)
+    states_mine = lax.all_to_all(
+        local_state.reshape(heads_dev, STATE * HEAD_DIM), "ctx", 0, 0, tiled=True
+    ).reshape(ctx_count, owned, STATE * HEAD_DIM)
+    incoming_mine = jnp.einsum("kcd,dkf->ckf", transfer, states_mine, precision=highest)
+    incoming = lax.all_to_all(incoming_mine, "ctx", 0, 0, tiled=True).reshape(
+        groups_dev, head_group, STATE, HEAD_DIM
+    )
     same_doc = (own_docs[:, None] == own_docs[None, :]) & (row_index[:, None] >= row_index[None, :])
     log_gap = cum_decay[:, :, :, None] - cum_decay[:, :, None, :]
     decay_matrix = jnp.exp(jnp.where(same_doc[None, None], log_gap, -jnp.inf))

time: 648 us -> 204 us (0.31)
  the two profiles are of different devices: /device:TPU:31 before, /device:TPU:4 now
where the time goes in v1:
time: 204 us; the launch traced here: 202 us
  blocking collectives  59.7 us (29%)
  matrix products  47.4 us (23%)
  waiting for transfers between devices  22.7 us (11%)
  local copies, waits for them, and re-layouts  22.3 us (11%)
  other arithmetic  17.3 us (8%)
  between operations  15.6 us (8%)
  starting transfers between devices  14 us (7%)
  loops' own time  2.88 us (1%)
    all_gather x1, blocking collectives, shards(): all_log = lax.all_gather(block_log, 'ctx')  39.3 us
    all_to_all x1, waiting for transfers between devices, shards(): lax.all_to_all(incoming_mine, 'ctx', 0, 0, tiled=True)  21.5 us
    psum x1, blocking collectives, shards(): square_sum = lax.psum(square_local, 'head')  20.4 us
    dot_general x4, matrix products, attend_block(): jnp.einsum('gqtr,rga->gqta', weights.astype(jnp.bfloat16), value_heads, p...  15 us
    dot_general x4, matrix products, attend_block(): jnp.einsum('tgqa,rga->gqtr', query_rows, key_heads, preferred_element_typ...  14.6 us
    all_to_all x1, starting transfers between devices, shards(): lax.all_to_all(local_state.reshape(heads_dev, STATE * HEAD_DIM), 'ctx', 0...  7.6 us
    all_to_all x1, other arithmetic, shards(): lax.all_to_all(incoming_mine, 'ctx', 0, 0, tiled=True)  6.75 us
    all_to_all x1, starting transfers between devices, shards(): lax.all_to_all(incoming_mine, 'ctx', 0, 0, tiled=True)  6.11 us
  transfers between devices with their start and end apart: 4, of which 1 were waited for; matrix products, arithmetic and copies ran while one was open for 16% of the time, Pallas kernels for 0%

profile of v1, /device:TPU:4, one launch (start us, length us, event | category | flops | bytes accessed | tf_op | source)
XLA Modules:
  0.0 202.0 jit_solution(15854381399884146402)
XLA Ops:
  7.2 0.8 copy.46
  8.0 0.1 reduce.11
  8.1 1.3 fusion.67
  9.4 0.1 convert_reduce_fusion.1
  9.5 0.7 slice.11
  10.8 0.7 compare_convert_fusion
  11.5 0.6 slice.12
  12.1 0.8 fusion.63
  12.9 1.3 copy.47
  15.0 0.2 slice_select_fusion
  15.1 0.8 multiply_bitcast_fusion
  16.0 1.0 convolution_bitcast_fusion.1
  17.0 2.7 %copy.49 = f32[1,32,256,64]{3,2,1,0:T(8,128)} copy(f32[1,32,256,64]{2,3,1,0:T(8,128)S(1)} %convolution_bitcast_fusion.1) | data formatting | bytes 4194304 | tf_op jit(solution)/shard_map/sgn,sgjp->gjnp/transpose | solution.py:62
  19.7 5.5 %all_to_all.12 = f32[32,1,16384]{2,1,0:T(1,128)} reshape(f32[1,32,256,64]{3,2,1,0:T(8,128)} %copy.49) | data formatting | bytes 4194304 | tf_op jit(solution)/shard_map/all_to_all | solution.py:80
  25.2 7.6 %all-to-all-start = ((f32[32,1,16384]{2,1,0:T(1,128)}), f32[32,1,16384]{2,1,0:T(1,128)S(1)}, u32[]{:S(2)}, u32[]{:S(2)}) async-start(f32[32,1,16384]{2,1,0:T(1,128)} %all_to_all.12), calls=%async_computation | async-start | bytes 4194304 | tf_op jit(solution)/shard_map/all_to_all | solution.py:80
  32.8 0.7 all-gather.4.cloned.1.call-update
  33.6 39.3 %all-gather = f32[32,32,1]{1,2,0:T(1,128)S(1)} all-gather(f32[1,32,1]{1,2,0:T(1,128)S(1)} %copy.51), channel_id=2, replica_groups=mesh['ctx'=32,'head'=8] {'ctx'}, dimensions={0}, use_global_device_ids=true | all-gather | bytes 4224 | tf_op jit(solution)/shard_map/all_gather | solution.py:69
  72.9 0.5 dynamic-slice_reduce_fusion
  73.4 0.2 select_reduce_fusion
  73.6 3.2 %convolution_bitcast_fusion = f32[32,1,16384]{2,0,1:T(8,128)S(1)} fusion(f32[32,1,16384]{2,1,0:T(1,128)S(1)} %all-to-all-done, f32[32,32]{1,0:T(8,128)S(1)} %select_reduce_fusion), kind=kOutput, calls=%fused_computation.33 | convolution fusion | flops 201328640 | bytes 4198400 | tf_op jit(solution)/shard_map/kcd,dkf->ckf/dot_general | solution.py:83
  76.9 3.5 %copy.52 = f32[32,1,16384]{2,1,0:T(1,128)} copy(f32[32,1,16384]{2,0,1:T(8,128)S(1)} %convolution_bitcast_fusion) | data formatting | bytes 4194304 | tf_op jit(solution)/shard_map/kcd,dkf->ckf/transpose | solution.py:83
  80.3 6.1 %all-to-all-start.1 = ((f32[32,1,16384]{2,1,0:T(1,128)}), f32[32,1,16384]{2,1,0:T(1,128)}, u32[]{:S(2)}, u32[]{:S(2)}) async-start(f32[32,1,16384]{2,1,0:T(1,128)} %copy.52), calls=%async_computation.1 | async-start | bytes 4194304 | tf_op jit(solution)/shard_map/all_to_all | solution.py:84
  86.4 0.2 all-gather.6.cloned.1.call-start
  86.7 0.5 all-gather.6.cloned.1.call-update
  87.2 0.1 fusion.70
  87.3 0.1 fusion.62
  87.5 3.5 %fusion.37 = f32[128,1,32,64]{0,3,2,1:T(8,128)} fusion(bf16[128,32,64]{0,2,1:T(8,128)(2,1)S(1)} %bitcast.188, f32[32,128]{1,0:T(8,128)S(1)} %copy-done.5, f32[32,128]{1,0:T(8,128)S(1)} %bitcast.199, f32[128,128]{1,0:T(8,128)S(1)} %fusion.70, pred[128,128]{1,0:T(8,128)(4,1)S(1)} %fusion.62), kind=kOutput, calls=%fused_computation.45 | convolution fusion | flops 404750336 | bytes 1687552 | tf_op jit(solution)/shard_map/gjts,sgjp->tgjp/dot_general | solution.py:94
  91.0 21.5 %all-to-all-done.1 = f32[32,1,16384]{2,1,0:T(1,128)} async-done(((f32[32,1,16384]{2,1,0:T(1,128)}), f32[32,1,16384]{2,1,0:T(1,128)}, u32[]{:S(2)}, u32[]{:S(2)}) %all-to-all-start.1) | async-done | bytes 2097184 | tf_op jit(solution)/shard_map/all_to_all | solution.py:84
  112.5 6.8 %reduce.14 = f32[32,16384]{1,0:T(8,128)S(1)} reduce(f32[32,1,16384]{2,1,0:T(1,128)} %all-to-all-done.1, f32[]{:T(128)} %constant.96), dimensions={1}, to_apply=%all_to_all.11.reduce_sub_computation | reduce | bytes 4194308 | tf_op jit(solution)/shard_map/all_to_all | solution.py:84
  119.3 3.0 %reshape.495 = f32[32,256,64]{2,1,0:T(8,128)} reshape(f32[32,16384]{1,0:T(8,128)S(1)} %reduce.14) | data formatting | bytes 4194304 | tf_op jit(solution)/shard_map/reshape.61
  122.3 6.0 %fusion.42 = f32[128,1,32,64]{0,3,2,1:T(8,128)S(1)} fusion(f32[128,1,32,64]{0,3,2,1:T(8,128)} %fusion.37, f32[32,256,64]{2,1,0:T(8,128)} %reshape.495, f32[32]{0:T(128)S(1)} %copy-done.7, f32[128,32]{0,1:T(8,128)S(1)} %get-tuple-element.256, bf16[128,256]{1,0:T(8,128)(2,1)S(1)} %copy-done.4, bf16[128,1,32,64]{0,3,2,1:T(8,128)(2,1)S(1)} %bitcast.189), kind=kOutput, calls=%fused_computation.49 | convolution fusion | flops 806617088 | bytes 4800640 | tf_op jit(solution)/shard_map/tgn,gjnp->tgjp/dot_general | solution.py:97
  128.3 0.3 copy.54
  128.7 0.4 multiply_reduce_fusion
  129.1 20.4 %psum.7 = f32[128]{0:T(128)S(1)} all-reduce(f32[128]{0:T(128)S(1)} %multiply_reduce_fusion), channel_id=1, replica_groups=mesh['ctx'=32,'head'=8] {'head'}, use_global_device_ids=true, to_apply=%region_5.6 | all-reduce | flops 128 | bytes 1024 | tf_op jit(solution)/shard_map/psum | solution.py:104
  149.5 0.4 multiply_convert_fusion
  149.9 3.1 %fusion.46 = bf16[1,16,8,8,128]{4,3,2,1,0:T(8,128)(2,1)S(1)} fusion(bf16[128,2048]{1,0:T(8,128)(2,1)S(1)} %multiply_convert_fusion, bf16[1,2048,1024]{2,1,0:T(8,128)(2,1)} %param.22), kind=kOutput, calls=%fused_computation.53 | convolution fusion | flops 537001984 | bytes 4980736 | tf_op jit(solution)/shard_map/tgf,gfo->tgo/dot_general | solution.py:110
  153.2 40.8 %while.17 = (s32[]{:T(128)}, f32[1,8,128]{2,1,0:T(8,128)S(1)}, f32[1,8,128]{2,1,0:T(8,128)S(1)}, f32[1,8,128,128]{3,2,1,0:T(8,128)S(1)}, s32[128]{0:T(128)S(1)},...) while((s32[]{:T(128)}, f32[1,8,128]{2,1,0:T(8,128)S(1)}, ...), condition=%wide.region_10.11_spmd.clone, body=%wide.region_6.10_spmd.clone.sunk | while | flops 551345280 | bytes 31816460 | solution.py:157
  153.2 0.6 dynamic_slice.42
  154.4 0.1 convert_reduce_fusion.3
  154.6 0.3 compare_and_fusion.2
  154.9 3.6 %fusion.86 = (f32[8,128]{1,0:T(8,128)S(1)}, f32[1024,128,8]{1,0,2:T(8,128)}) fusion(pred[128,1024]{0,1:T(8,128)(4,1)S(1)} %compare_and_fusion.2, bf16[128,1,8,128]{3,0,2,1:T(8,128)(2,1)S(1)} %get-tuple-element.375, bf16[4,1024,128]{2,1,0:T(8,128)(2,1)} %get-tuple-element.374, s32[]{:T(128)} %get-tuple-element.353), kind=kOutput, calls=%fused_computation.3.clone.1 | convolution fusion | flops 271580160 | bytes 4854272 | tf_op jit(solution)/shard_map/while/body/eval_jaxpr/tgqa,rga->gqtr/dot_general | solution.py:130
  158.6 3.8 %fusion.89 = f32[1,8,128,128]{3,2,1,0:T(8,128)S(1)} fusion(f32[1024,128,8]{1,0,2:T(8,128)} %get-tuple-element.337, f32[8,128]{1,0:T(8,128)S(1)} %bitcast.193, pred[128,1024]{0,1:T(8,128)(4,1)S(1)} %compare_and_fusion.2, f32[1,8,128,128]{3,2,1,0:T(8,128)S(1)} %get-tuple-element.356, bf16[4,1024,128]{2,1,0:T(8,128)(2,1)} %get-tuple-element.376, ...), kind=kOutput, calls=%fused_computation.10.clone.1 | convolution fusion | flops 274071552 | bytes 5644801 | tf_op jit(solution)/shard_map/while/body/eval_jaxpr/gqtr,rga->gqta/dot_general | solution.py:139
  162.3 1.0 fusion.88
  163.4 0.6 dynamic_slice.42
  164.6 0.1 convert_reduce_fusion.3
  164.8 0.3 compare_and_fusion.2
  165.1 3.6 %fusion.86 = (f32[8,128]{1,0:T(8,128)S(1)}, f32[1024,128,8]{1,0,2:T(8,128)}) fusion(pred[128,1024]{0,1:T(8,128)(4,1)S(1)} %compare_and_fusion.2, bf16[128,1,8,128]{3,0,2,1:T(8,128)(2,1)S(1)} %get-tuple-element.375, bf16[4,1024,128]{2,1,0:T(8,128)(2,1)} %get-tuple-element.374, s32[]{:T(128)} %get-tuple-element.353), kind=kOutput, calls=%fused_computation.3.clone.1 | convolution fusion | flops 271580160 | bytes 4854272 | tf_op jit(solution)/shard_map/while/body/eval_jaxpr/tgqa,rga->gqtr/dot_general | solution.py:130
  168.8 3.8 %fusion.89 = f32[1,8,128,128]{3,2,1,0:T(8,128)S(1)} fusion(f32[1024,128,8]{1,0,2:T(8,128)} %get-tuple-element.337, f32[8,128]{1,0:T(8,128)S(1)} %bitcast.193, pred[128,1024]{0,1:T(8,128)(4,1)S(1)} %compare_and_fusion.2, f32[1,8,128,128]{3,2,1,0:T(8,128)S(1)} %get-tuple-element.356, bf16[4,1024,128]{2,1,0:T(8,128)(2,1)} %get-tuple-element.376, ...), kind=kOutput, calls=%fused_computation.10.clone.1 | convolution fusion | flops 274071552 | bytes 5644801 | tf_op jit(solution)/shard_map/while/body/eval_jaxpr/gqtr,rga->gqta/dot_general | solution.py:139
  172.5 1.0 fusion.88
  173.6 0.6 dynamic_slice.42
  174.8 0.1 convert_reduce_fusion.3
  175.0 0.3 compare_and_fusion.2
  175.3 3.6 %fusion.86 = (f32[8,128]{1,0:T(8,128)S(1)}, f32[1024,128,8]{1,0,2:T(8,128)}) fusion(pred[128,1024]{0,1:T(8,128)(4,1)S(1)} %compare_and_fusion.2, bf16[128,1,8,128]{3,0,2,1:T(8,128)(2,1)S(1)} %get-tuple-element.375, bf16[4,1024,128]{2,1,0:T(8,128)(2,1)} %get-tuple-element.374, s32[]{:T(128)} %get-tuple-element.353), kind=kOutput, calls=%fused_computation.3.clone.1 | convolution fusion | flops 271580160 | bytes 4854272 | tf_op jit(solution)/shard_map/while/body/eval_jaxpr/tgqa,rga->gqtr/dot_general | solution.py:130
  179.0 3.8 %fusion.89 = f32[1,8,128,128]{3,2,1,0:T(8,128)S(1)} fusion(f32[1024,128,8]{1,0,2:T(8,128)} %get-tuple-element.337, f32[8,128]{1,0:T(8,128)S(1)} %bitcast.193, pred[128,1024]{0,1:T(8,128)(4,1)S(1)} %compare_and_fusion.2, f32[1,8,128,128]{3,2,1,0:T(8,128)S(1)} %get-tuple-element.356, bf16[4,1024,128]{2,1,0:T(8,128)(2,1)} %get-tuple-element.376, ...), kind=kOutput, calls=%fused_computation.10.clone.1 | convolution fusion | flops 274071552 | bytes 5644801 | tf_op jit(solution)/shard_map/while/body/eval_jaxpr/gqtr,rga->gqta/dot_general | solution.py:139
  182.7 1.0 fusion.88
  183.8 0.6 dynamic_slice.42
  185.0 0.1 convert_reduce_fusion.3
  185.2 0.3 compare_and_fusion.2
  185.5 3.6 %fusion.86 = (f32[8,128]{1,0:T(8,128)S(1)}, f32[1024,128,8]{1,0,2:T(8,128)}) fusion(pred[128,1024]{0,1:T(8,128)(4,1)S(1)} %compare_and_fusion.2, bf16[128,1,8,128]{3,0,2,1:T(8,128)(2,1)S(1)} %get-tuple-element.375, bf16[4,1024,128]{2,1,0:T(8,128)(2,1)} %get-tuple-element.374, s32[]{:T(128)} %get-tuple-element.353), kind=kOutput, calls=%fused_computation.3.clone.1 | convolution fusion | flops 271580160 | bytes 4854272 | tf_op jit(solution)/shard_map/while/body/eval_jaxpr/tgqa,rga->gqtr/dot_general | solution.py:130
  189.2 3.8 %fusion.89 = f32[1,8,128,128]{3,2,1,0:T(8,128)S(1)} fusion(f32[1024,128,8]{1,0,2:T(8,128)} %get-tuple-element.337, f32[8,128]{1,0:T(8,128)S(1)} %bitcast.193, pred[128,1024]{0,1:T(8,128)(4,1)S(1)} %compare_and_fusion.2, f32[1,8,128,128]{3,2,1,0:T(8,128)S(1)} %get-tuple-element.356, bf16[4,1024,128]{2,1,0:T(8,128)(2,1)} %get-tuple-element.376, ...), kind=kOutput, calls=%fused_computation.10.clone.1 | convolution fusion | flops 274071552 | bytes 5644801 | tf_op jit(solution)/shard_map/while/body/eval_jaxpr/gqtr,rga->gqta/dot_general | solution.py:139
  192.9 1.0 fusion.88
  194.0 0.2 fusion.59
  194.2 0.2 copy.56
  194.4 0.8 copy.68
  (62 shorter events, 0.5 us)
Async XLA Ops:
  7.2 8.9 %copy-start = (bf16[128,256]{1,0:T(8,128)(2,1)S(1)}, bf16[128,256]{1,0:T(8,128)(2,1)}, u32[]{:S(2)}) copy-start(bf16[128,256]{1,0:T(8,128)(2,1)} %param.16) | copy-start | bytes 196612
  25.2 48.4 %all-to-all-start = ((f32[32,1,16384]{2,1,0:T(1,128)}), f32[32,1,16384]{2,1,0:T(1,128)S(1)}, u32[]{:S(2)}, u32[]{:S(2)}) async-start(f32[32,1,16384]{2,1,0:T(1,128)} %all_to_all.12), calls=%async_computation | async-start | bytes 4194304 | tf_op jit(solution)/shard_map/all_to_all | solution.py:80
  32.8 120.3 %all-gather.4.cloned.1.call-start = ((), (), s32[]{:S(2)}) async-start(), calls=%async_computation.2 | async-start | bytes 1081344 | tf_op jit(solution)/shard_map/all_gather | solution.py:177
  76.8 10.3 %copy-start.4 = (bf16[128,256]{1,0:T(8,128)(2,1)S(1)}, bf16[128,256]{1,0:T(8,128)(2,1)}, u32[]{:S(2)}) copy-start(bf16[128,256]{1,0:T(8,128)(2,1)} %param.17) | copy-start | bytes 196612
  76.9 10.6 %copy-start.5 = (f32[32,128]{1,0:T(8,128)S(1)}, f32[32,128]{1,0:T(8,128)}, u32[]{:S(2)}) copy-start(f32[32,128]{1,0:T(8,128)} %param.18) | copy-start | bytes 49156
  80.3 32.2 %all-to-all-start.1 = ((f32[32,1,16384]{2,1,0:T(1,128)}), f32[32,1,16384]{2,1,0:T(1,128)}, u32[]{:S(2)}, u32[]{:S(2)}) async-start(f32[32,1,16384]{2,1,0:T(1,128)} %copy.52), calls=%async_computation.1 | async-start | bytes 4194304 | tf_op jit(solution)/shard_map/all_to_all | solution.py:84
  86.4 66.7 %all-gather.6.cloned.1.call-start = ((), (), s32[]{:S(2)}) async-start(), calls=%async_computation.3 | async-start | bytes 1081344 | tf_op jit(solution)/shard_map/all_gather | solution.py:178
  119.3 3.0 %copy-start.7 = (f32[32]{0:T(128)S(1)}, f32[32]{0:T(128)}, u32[]{:S(2)}) copy-start(f32[32]{0:T(128)} %param.20) | copy-start | bytes 388
  122.3 6.4 %copy-start.3 = (bf16[128,2048]{1,0:T(8,128)(2,1)S(1)}, bf16[128,2048]{1,0:T(8,128)(2,1)}, u32[]{:S(2)}) copy-start(bf16[128,2048]{1,0:T(8,128)(2,1)} %param.15) | copy-start | bytes 1572868
  122.3 27.3 %copy-start.6 = (f32[2048]{0:T(1024)S(1)}, f32[2048]{0:T(1024)}, u32[]{:S(2)}) copy-start(f32[2048]{0:T(1024)} %param.21) | copy-start | bytes 24580
  149.9 3.2 %copy-start.2 = (bf16[128,2048]{1,0:T(8,128)(2,1)}, bf16[128,2048]{1,0:T(8,128)(2,1)S(1)}, u32[]{:S(2)}) copy-start(bf16[128,2048]{1,0:T(8,128)(2,1)S(1)} %multiply_convert_fusion) | copy-start | bytes 1572868
  158.6 3.8 %copy-start.1 = (f32[1024,128,8]{1,0,2:T(8,128)S(1)}, f32[1024,128,8]{1,0,2:T(8,128)}, u32[]{:S(2)}) copy-start(f32[1024,128,8]{1,0,2:T(8,128)} %get-tuple-element.337) | copy-start | bytes 12582916 | tf_op jit(solution)/shard_map/while
  168.8 3.8 %copy-start.1 = (f32[1024,128,8]{1,0,2:T(8,128)S(1)}, f32[1024,128,8]{1,0,2:T(8,128)}, u32[]{:S(2)}) copy-start(f32[1024,128,8]{1,0,2:T(8,128)} %get-tuple-element.337) | copy-start | bytes 12582916 | tf_op jit(solution)/shard_map/while
  179.0 3.8 %copy-start.1 = (f32[1024,128,8]{1,0,2:T(8,128)S(1)}, f32[1024,128,8]{1,0,2:T(8,128)}, u32[]{:S(2)}) copy-start(f32[1024,128,8]{1,0,2:T(8,128)} %get-tuple-element.337) | copy-start | bytes 12582916 | tf_op jit(solution)/shard_map/while
  189.1 3.8 %copy-start.1 = (f32[1024,128,8]{1,0,2:T(8,128)S(1)}, f32[1024,128,8]{1,0,2:T(8,128)}, u32[]{:S(2)}) copy-start(f32[1024,128,8]{1,0,2:T(8,128)} %get-tuple-element.337) | copy-start | bytes 12582916 | tf_op jit(solution)/shard_map/while
Sparse Core Ops, SparseCore 0:
  36.2 54.1 all-gather.3
  92.9 51.1 all-gather.5

commit v2 on v1

--- a/solution.py
+++ b/solution.py
@@ -66,8 +66,17 @@
     ctx_count = lax.axis_size("ctx")
     owned = heads_dev // ctx_count
     block_log = jnp.where(carry_mask[-1] > 0, cum_decay[:, :, -1], -jnp.inf).reshape(heads_dev)
-    all_log = lax.all_gather(block_log, "ctx")
-    mine_log = lax.dynamic_slice_in_dim(all_log, shard_index * owned, owned, 1)
+    lane_rows = 8
+    state_cols = STATE * HEAD_DIM // lane_rows
+    log_cols = jnp.broadcast_to(block_log[:, None, None], (heads_dev, lane_rows, 128))
+    payload = jnp.concatenate(
+        [local_state.reshape(heads_dev, lane_rows, state_cols), log_cols], axis=2
+    )
+    gathered = lax.all_to_all(payload, "ctx", 0, 0, tiled=True).reshape(
+        ctx_count, owned, lane_rows, state_cols + 128
+    )
+    states_mine = gathered[:, :, :, :state_cols]
+    mine_log = gathered[:, :, 0, state_cols]
     block_row = jnp.arange(ctx_count, dtype=jnp.int32)
     between = (block_row[None, :, None] < block_row[None, None, :]) & (
         block_row[None, None, :] < block_row[:, None, None]
@@ -77,13 +86,10 @@
     )
     earlier = block_row[:, None] > block_row[None, :]
     transfer = jnp.where(earlier[None], jnp.exp(log_span), 0.0)
-    states_mine = lax.all_to_all(
-        local_state.reshape(heads_dev, STATE * HEAD_DIM), "ctx", 0, 0, tiled=True
-    ).reshape(ctx_count, owned, STATE * HEAD_DIM)
-    incoming_mine = jnp.einsum("kcd,dkf->ckf", transfer, states_mine, precision=highest)
-    incoming = lax.all_to_all(incoming_mine, "ctx", 0, 0, tiled=True).reshape(
-        groups_dev, head_group, STATE, HEAD_DIM
-    )
+    incoming_mine = jnp.einsum("kcd,dkrf->ckrf", transfer, states_mine, precision=highest)
+    incoming = lax.all_to_all(
+        incoming_mine.reshape(ctx_count * owned, lane_rows, state_cols), "ctx", 0, 0, tiled=True
+    ).reshape(groups_dev, head_group, STATE, HEAD_DIM)
     same_doc = (own_docs[:, None] == own_docs[None, :]) & (row_index[:, None] >= row_index[None, :])
     log_gap = cum_decay[:, :, :, None] - cum_decay[:, :, None, :]
     decay_matrix = jnp.exp(jnp.where(same_doc[None, None], log_gap, -jnp.inf))

time: 204 us -> 204 us (level)
  waiting for transfers between devices: 22.7 us -> 69.7 us
  blocking collectives: 59.7 us -> 20.8 us
  other arithmetic: 17.3 us -> 11.9 us
  local copies, waits for them, and re-layouts: 22.3 us -> 19.7 us
    all_gather x1 -> x0, blocking collectives: 39.3 us -> none  [shards(): all_log = lax.all_gather(block_log, 'ctx')]
    all_to_all x2, waiting for transfers between devices: 21.5 us -> 49.4 us  [the longest x1 26.8 us: shards(): lax.all_to_all(payload, 'ctx', 0, 0, tiled=True)]
    all_gather x1, waiting for transfers between devices: 0.02 us -> 19.1 us  [shards(): lax.all_gather(values, 'ctx', axis=0, tiled=True)]
    all_to_all x1 -> x0, other arithmetic: 6.75 us -> none  [shards(): lax.all_to_all(incoming_mine, 'ctx', 0, 0, tiled=True)]
    reshape x0 -> x2, local copies, waits for them, and re-layouts: none -> 6.17 us  [the longest x1 3.6 us: shards(): local_state.reshape(heads_dev, lane_rows, state_cols)]
    all_to_all x1, local copies, waits for them, and re-layouts: 5.46 us -> 0.43 us  [shards(): lax.all_to_all(payload, 'ctx', 0, 0, tiled=True)]
    transpose x1 -> x0, local copies, waits for them, and re-layouts: 3.45 us -> none  [shards(): jnp.einsum('kcd,dkf->ckf', transfer, states_mine, precision=highest)]
  transfers between devices with their start and end apart: 4 -> 4, of which waited for: 1 -> 3; matrix products, arithmetic and copies ran while one was open for 16% -> 11% of each run, Pallas kernels for 0% -> 0%
where the time goes in v2:
time: 204 us; the launch traced here: 201 us
  waiting for transfers between devices  69.7 us (34%)
  matrix products  46.1 us (23%)
  blocking collectives  20.8 us (10%)
  local copies, waits for them, and re-layouts  19.7 us (10%)
  between operations  15.6 us (8%)
  starting transfers between devices  14.8 us (7%)
  other arithmetic  11.9 us (6%)
  loops' own time  2.63 us (1%)
    all_to_all x1, waiting for transfers between devices, shards(): lax.all_to_all(payload, 'ctx', 0, 0, tiled=True)  26.8 us
    all_to_all x1, waiting for transfers between devices, shards(): lax.all_to_all(incoming_mine.reshape(ctx_count * owned, lane_rows, state_...  22.6 us
    psum x1, blocking collectives, shards(): square_sum = lax.psum(square_local, 'head')  20.8 us
    all_gather x1, waiting for transfers between devices, shards(): lax.all_gather(values, 'ctx', axis=0, tiled=True)  19.1 us
    dot_general x4, matrix products, attend_block(): jnp.einsum('gqtr,rga->gqta', weights.astype(jnp.bfloat16), value_heads, p...  15 us
    dot_general x4, matrix products, attend_block(): jnp.einsum('tgqa,rga->gqtr', query_rows, key_heads, preferred_element_typ...  14.6 us
    all_to_all x1, starting transfers between devices, shards(): lax.all_to_all(payload, 'ctx', 0, 0, tiled=True)  7.59 us
    all_to_all x1, starting transfers between devices, shards(): lax.all_to_all(incoming_mine.reshape(ctx_count * owned, lane_rows, state_...  6.96 us
  transfers between devices with their start and end apart: 4, of which 3 were waited for; matrix products, arithmetic and copies ran while one was open for 11% of the time, Pallas kernels for 0%

profile of v2, /device:TPU:4, one launch (start us, length us, event | category | flops | bytes accessed | tf_op | source)
XLA Modules:
  0.0 201.3 jit_solution(6079622498042372984)
XLA Ops:
  7.2 0.8 copy.46
  8.0 0.1 reduce.11
  8.1 1.3 fusion.65
  9.4 0.1 convert_reduce_fusion.1
  9.5 0.7 slice.17
  10.8 0.8 fusion.61
  11.7 0.2 slice_reduce_fusion.1
  11.9 1.3 copy.47
  13.2 0.7 compare_convert_fusion.2
  13.9 0.6 slice.18
  14.5 0.8 multiply_bitcast_fusion
  15.4 1.0 convolution_bitcast_fusion.1
  16.4 2.7 %copy.49 = f32[1,32,256,64]{3,2,1,0:T(8,128)} copy(f32[1,32,256,64]{2,3,1,0:T(8,128)S(1)} %convolution_bitcast_fusion.1) | data formatting | bytes 4194304 | tf_op jit(solution)/shard_map/sgn,sgjp->gjnp/transpose | solution.py:62
  19.1 3.6 %reshape.489 = f32[32,8,2048]{2,1,0:T(8,128)S(1)} reshape(f32[1,32,256,64]{3,2,1,0:T(8,128)} %copy.49) | data formatting | bytes 4194304 | tf_op jit(solution)/shard_map/reshape | solution.py:73
  23.3 0.1 broadcast_in_dim.116
  23.4 1.6 pad_maximum_fusion
  25.0 7.6 %all-to-all-start = ((f32[32,8,2176]{2,1,0:T(8,128)}), f32[32,8,2176]{2,1,0:T(8,128)S(1)}, u32[]{:S(2)}, u32[]{:S(2)}) async-start(f32[32,8,2176]{2,1,0:T(8,128)} %pad_maximum_fusion), calls=%async_computation | async-start | bytes 4456448 | tf_op jit(solution)/shard_map/all_to_all | solution.py:75
  32.6 0.7 all-gather.3.cloned.1.call-update
  33.3 26.8 %all-to-all-done = f32[32,8,2176]{2,1,0:T(8,128)S(1)} async-done(((f32[32,8,2176]{2,1,0:T(8,128)}), f32[32,8,2176]{2,1,0:T(8,128)S(1)}, u32[]{:S(2)}, u32[]{:S(2)}) %all-to-all-start) | async-done | bytes 2228256 | tf_op jit(solution)/shard_map/all_to_all | solution.py:75
  60.1 0.4 copy.63
  60.5 0.1 slice_reduce_fusion
  60.6 0.2 select_reduce_fusion
  60.9 1.9 convolution_bitcast_fusion
  62.8 2.6 %copy.51 = f32[32,8,2048]{2,1,0:T(8,128)} copy(f32[32,8,2048]{2,0,1:T(8,128)S(1)} %convolution_bitcast_fusion) | data formatting | bytes 4194304 | tf_op jit(solution)/shard_map/reshape | solution.py:91
  65.4 7.0 %all-to-all-start.1 = ((f32[32,8,2048]{2,1,0:T(8,128)}), f32[32,8,2048]{2,1,0:T(8,128)S(1)}, u32[]{:S(2)}, u32[]{:S(2)}) async-start(f32[32,8,2048]{2,1,0:T(8,128)} %copy.51), calls=%async_computation.1 | async-start | bytes 4194304 | tf_op jit(solution)/shard_map/all_to_all | solution.py:90
  72.4 0.2 all-gather.5.cloned.1.call-start
  72.6 0.5 all-gather.5.cloned.1.call-update
  73.1 0.1 fusion.68
  73.2 0.1 fusion.60
  73.4 3.6 %fusion.35 = f32[128,1,32,64]{0,3,2,1:T(8,128)} fusion(bf16[128,32,64]{0,2,1:T(8,128)(2,1)S(1)} %bitcast.197, f32[32,128]{1,0:T(8,128)S(1)} %copy-done.6, f32[32,128]{1,0:T(8,128)S(1)} %bitcast.208, f32[128,128]{1,0:T(8,128)S(1)} %fusion.68, pred[128,128]{1,0:T(8,128)(4,1)S(1)} %fusion.60), kind=kOutput, calls=%fused_computation.46 | convolution fusion | flops 404750336 | bytes 1687552 | tf_op jit(solution)/shard_map/gjts,sgjp->tgjp/dot_general | solution.py:100
  77.0 22.6 %all-to-all-done.1 = f32[32,8,2048]{2,1,0:T(8,128)S(1)} async-done(((f32[32,8,2048]{2,1,0:T(8,128)}), f32[32,8,2048]{2,1,0:T(8,128)S(1)}, u32[]{:S(2)}, u32[]{:S(2)}) %all-to-all-start.1) | async-done | bytes 2097184 | tf_op jit(solution)/shard_map/all_to_all | solution.py:90
  99.6 3.0 %reshape.493 = f32[32,256,64]{2,1,0:T(8,128)} reshape(f32[32,8,2048]{2,1,0:T(8,128)S(1)} %all-to-all-done.1) | data formatting | bytes 4194304 | tf_op jit(solution)/shard_map/reshape.62
  102.6 6.0 %fusion.40 = f32[128,1,32,64]{0,3,2,1:T(8,128)S(1)} fusion(f32[128,1,32,64]{0,3,2,1:T(8,128)} %fusion.35, f32[32,256,64]{2,1,0:T(8,128)} %reshape.493, f32[32]{0:T(128)S(1)} %copy-done.8, f32[128,32]{0,1:T(8,128)S(1)} %get-tuple-element.256, bf16[128,256]{1,0:T(8,128)(2,1)S(1)} %copy-done.5, bf16[128,1,32,64]{0,3,2,1:T(8,128)(2,1)S(1)} %bitcast.198), kind=kOutput, calls=%fused_computation.50 | convolution fusion | flops 806617088 | bytes 4800640 | tf_op jit(solution)/shard_map/tgn,gjnp->tgjp/dot_general | solution.py:103
  108.6 0.3 copy.53
  109.0 0.4 multiply_reduce_fusion
  109.4 20.8 %psum.7 = f32[128]{0:T(128)S(1)} all-reduce(f32[128]{0:T(128)S(1)} %multiply_reduce_fusion), channel_id=1, replica_groups=mesh['ctx'=32,'head'=8] {'head'}, use_global_device_ids=true, to_apply=%region_5.6 | all-reduce | flops 128 | bytes 1024 | tf_op jit(solution)/shard_map/psum | solution.py:110
  130.3 0.4 multiply_convert_fusion
  130.7 3.1 %fusion.44 = bf16[1,16,8,8,128]{4,3,2,1,0:T(8,128)(2,1)S(1)} fusion(bf16[128,2048]{1,0:T(8,128)(2,1)S(1)} %multiply_convert_fusion, bf16[1,2048,1024]{2,1,0:T(8,128)(2,1)} %param.22), kind=kOutput, calls=%fused_computation.54 | convolution fusion | flops 537001984 | bytes 4980736 | tf_op jit(solution)/shard_map/tgf,gfo->tgo/dot_general | solution.py:116
  133.8 19.1 %all-gather.5.cloned.1.call-done = bf16[4096,128]{1,0:T(8,128)(2,1)} async-done(((bf16[128,128]{1,0:T(8,128)(2,1)}), bf16[4096,128]{1,0:T(8,128)(2,1)}) %all-gather.5.cloned.1.call-update) | async-done | bytes 1048592 | tf_op jit(solution)/shard_map/all_gather | solution.py:184
  152.9 40.4 %while.17 = (s32[]{:T(128)}, f32[1,8,128]{2,1,0:T(8,128)S(1)}, f32[1,8,128]{2,1,0:T(8,128)S(1)}, f32[1,8,128,128]{3,2,1,0:T(8,128)S(1)}, s32[128]{0:T(128)S(1)},...) while((s32[]{:T(128)}, f32[1,8,128]{2,1,0:T(8,128)S(1)}, ...), condition=%wide.region_10.11_spmd.clone, body=%wide.region_6.10_spmd.clone.sunk | while | flops 551345280 | bytes 31816460 | solution.py:163
  152.9 0.6 dynamic_slice.38
  154.1 0.1 convert_reduce_fusion.3
  154.2 0.3 compare_and_fusion.2
  154.5 3.6 %fusion.84 = (f32[8,128]{1,0:T(8,128)S(1)}, f32[1024,128,8]{1,0,2:T(8,128)}) fusion(pred[128,1024]{0,1:T(8,128)(4,1)S(1)} %compare_and_fusion.2, bf16[128,1,8,128]{3,0,2,1:T(8,128)(2,1)S(1)} %get-tuple-element.373, bf16[4,1024,128]{2,1,0:T(8,128)(2,1)} %get-tuple-element.372, s32[]{:T(128)} %get-tuple-element.351), kind=kOutput, calls=%fused_computation.3.clone.1 | convolution fusion | flops 271580160 | bytes 4854272 | tf_op jit(solution)/shard_map/while/body/eval_jaxpr/tgqa,rga->gqtr/dot_general | solution.py:136
  158.2 3.8 %fusion.87 = f32[1,8,128,128]{3,2,1,0:T(8,128)S(1)} fusion(f32[1024,128,8]{1,0,2:T(8,128)} %get-tuple-element.335, f32[8,128]{1,0:T(8,128)S(1)} %bitcast.202, pred[128,1024]{0,1:T(8,128)(4,1)S(1)} %compare_and_fusion.2, f32[1,8,128,128]{3,2,1,0:T(8,128)S(1)} %get-tuple-element.354, bf16[4,1024,128]{2,1,0:T(8,128)(2,1)} %get-tuple-element.374, ...), kind=kOutput, calls=%fused_computation.10.clone.1 | convolution fusion | flops 274071552 | bytes 5644801 | tf_op jit(solution)/shard_map/while/body/eval_jaxpr/gqtr,rga->gqta/dot_general | solution.py:145
  162.0 1.0 fusion.86
  163.0 0.6 dynamic_slice.38
  164.3 0.3 compare_and_fusion.2
  164.7 3.6 %fusion.84 = (f32[8,128]{1,0:T(8,128)S(1)}, f32[1024,128,8]{1,0,2:T(8,128)}) fusion(pred[128,1024]{0,1:T(8,128)(4,1)S(1)} %compare_and_fusion.2, bf16[128,1,8,128]{3,0,2,1:T(8,128)(2,1)S(1)} %get-tuple-element.373, bf16[4,1024,128]{2,1,0:T(8,128)(2,1)} %get-tuple-element.372, s32[]{:T(128)} %get-tuple-element.351), kind=kOutput, calls=%fused_computation.3.clone.1 | convolution fusion | flops 271580160 | bytes 4854272 | tf_op jit(solution)/shard_map/while/body/eval_jaxpr/tgqa,rga->gqtr/dot_general | solution.py:136
  168.3 3.8 %fusion.87 = f32[1,8,128,128]{3,2,1,0:T(8,128)S(1)} fusion(f32[1024,128,8]{1,0,2:T(8,128)} %get-tuple-element.335, f32[8,128]{1,0:T(8,128)S(1)} %bitcast.202, pred[128,1024]{0,1:T(8,128)(4,1)S(1)} %compare_and_fusion.2, f32[1,8,128,128]{3,2,1,0:T(8,128)S(1)} %get-tuple-element.354, bf16[4,1024,128]{2,1,0:T(8,128)(2,1)} %get-tuple-element.374, ...), kind=kOutput, calls=%fused_computation.10.clone.1 | convolution fusion | flops 274071552 | bytes 5644801 | tf_op jit(solution)/shard_map/while/body/eval_jaxpr/gqtr,rga->gqta/dot_general | solution.py:145
  172.1 1.0 fusion.86
  173.1 0.6 dynamic_slice.38
  174.4 0.3 compare_and_fusion.2
  174.8 3.6 %fusion.84 = (f32[8,128]{1,0:T(8,128)S(1)}, f32[1024,128,8]{1,0,2:T(8,128)}) fusion(pred[128,1024]{0,1:T(8,128)(4,1)S(1)} %compare_and_fusion.2, bf16[128,1,8,128]{3,0,2,1:T(8,128)(2,1)S(1)} %get-tuple-element.373, bf16[4,1024,128]{2,1,0:T(8,128)(2,1)} %get-tuple-element.372, s32[]{:T(128)} %get-tuple-element.351), kind=kOutput, calls=%fused_computation.3.clone.1 | convolution fusion | flops 271580160 | bytes 4854272 | tf_op jit(solution)/shard_map/while/body/eval_jaxpr/tgqa,rga->gqtr/dot_general | solution.py:136
  178.4 3.8 %fusion.87 = f32[1,8,128,128]{3,2,1,0:T(8,128)S(1)} fusion(f32[1024,128,8]{1,0,2:T(8,128)} %get-tuple-element.335, f32[8,128]{1,0:T(8,128)S(1)} %bitcast.202, pred[128,1024]{0,1:T(8,128)(4,1)S(1)} %compare_and_fusion.2, f32[1,8,128,128]{3,2,1,0:T(8,128)S(1)} %get-tuple-element.354, bf16[4,1024,128]{2,1,0:T(8,128)(2,1)} %get-tuple-element.374, ...), kind=kOutput, calls=%fused_computation.10.clone.1 | convolution fusion | flops 274071552 | bytes 5644801 | tf_op jit(solution)/shard_map/while/body/eval_jaxpr/gqtr,rga->gqta/dot_general | solution.py:145
  182.2 1.0 fusion.86
  183.2 0.6 dynamic_slice.38
  184.5 0.3 compare_and_fusion.2
  184.9 3.6 %fusion.84 = (f32[8,128]{1,0:T(8,128)S(1)}, f32[1024,128,8]{1,0,2:T(8,128)}) fusion(pred[128,1024]{0,1:T(8,128)(4,1)S(1)} %compare_and_fusion.2, bf16[128,1,8,128]{3,0,2,1:T(8,128)(2,1)S(1)} %get-tuple-element.373, bf16[4,1024,128]{2,1,0:T(8,128)(2,1)} %get-tuple-element.372, s32[]{:T(128)} %get-tuple-element.351), kind=kOutput, calls=%fused_computation.3.clone.1 | convolution fusion | flops 271580160 | bytes 4854272 | tf_op jit(solution)/shard_map/while/body/eval_jaxpr/tgqa,rga->gqtr/dot_general | solution.py:136
  188.5 3.8 %fusion.87 = f32[1,8,128,128]{3,2,1,0:T(8,128)S(1)} fusion(f32[1024,128,8]{1,0,2:T(8,128)} %get-tuple-element.335, f32[8,128]{1,0:T(8,128)S(1)} %bitcast.202, pred[128,1024]{0,1:T(8,128)(4,1)S(1)} %compare_and_fusion.2, f32[1,8,128,128]{3,2,1,0:T(8,128)S(1)} %get-tuple-element.354, bf16[4,1024,128]{2,1,0:T(8,128)(2,1)} %get-tuple-element.374, ...), kind=kOutput, calls=%fused_computation.10.clone.1 | convolution fusion | flops 274071552 | bytes 5644801 | tf_op jit(solution)/shard_map/while/body/eval_jaxpr/gqtr,rga->gqta/dot_general | solution.py:145
  192.3 1.0 fusion.86
  193.4 0.2 fusion.57
  193.6 0.2 copy.55
  193.8 0.8 copy.64
  (65 shorter events, 0.7 us)
Async XLA Ops:
  7.2 8.2 %copy-start = (bf16[128,256]{1,0:T(8,128)(2,1)S(1)}, bf16[128,256]{1,0:T(8,128)(2,1)}, u32[]{:S(2)}) copy-start(bf16[128,256]{1,0:T(8,128)(2,1)} %param.16) | copy-start | bytes 196612
  25.0 35.1 %all-to-all-start = ((f32[32,8,2176]{2,1,0:T(8,128)}), f32[32,8,2176]{2,1,0:T(8,128)S(1)}, u32[]{:S(2)}, u32[]{:S(2)}) async-start(f32[32,8,2176]{2,1,0:T(8,128)} %pad_maximum_fusion), calls=%async_computation | async-start | bytes 4456448 | tf_op jit(solution)/shard_map/all_to_all | solution.py:75
  32.6 101.2 %all-gather.3.cloned.1.call-start = ((), (), s32[]{:S(2)}) async-start(), calls=%async_computation.2 | async-start | bytes 1081344 | tf_op jit(solution)/shard_map/all_gather | solution.py:183
  62.8 10.3 %copy-start.5 = (bf16[128,256]{1,0:T(8,128)(2,1)S(1)}, bf16[128,256]{1,0:T(8,128)(2,1)}, u32[]{:S(2)}) copy-start(bf16[128,256]{1,0:T(8,128)(2,1)} %param.17) | copy-start | bytes 196612
  62.8 10.6 %copy-start.6 = (f32[32,128]{1,0:T(8,128)S(1)}, f32[32,128]{1,0:T(8,128)}, u32[]{:S(2)}) copy-start(f32[32,128]{1,0:T(8,128)} %param.18) | copy-start | bytes 49156
  65.4 34.2 %all-to-all-start.1 = ((f32[32,8,2048]{2,1,0:T(8,128)}), f32[32,8,2048]{2,1,0:T(8,128)S(1)}, u32[]{:S(2)}, u32[]{:S(2)}) async-start(f32[32,8,2048]{2,1,0:T(8,128)} %copy.51), calls=%async_computation.1 | async-start | bytes 4194304 | tf_op jit(solution)/shard_map/all_to_all | solution.py:90
  72.4 80.5 %all-gather.5.cloned.1.call-start = ((), (), s32[]{:S(2)}) async-start(), calls=%async_computation.3 | async-start | bytes 1081344 | tf_op jit(solution)/shard_map/all_gather | solution.py:184
  73.4 29.2 %copy-start.8 = (f32[32]{0:T(128)S(1)}, f32[32]{0:T(128)}, u32[]{:S(2)}) copy-start(f32[32]{0:T(128)} %param.20) | copy-start | bytes 388
  102.6 6.4 %copy-start.3 = (bf16[128,2048]{1,0:T(8,128)(2,1)S(1)}, bf16[128,2048]{1,0:T(8,128)(2,1)}, u32[]{:S(2)}) copy-start(bf16[128,2048]{1,0:T(8,128)(2,1)} %param.15) | copy-start | bytes 1572868
  102.6 27.7 %copy-start.7 = (f32[2048]{0:T(1024)S(1)}, f32[2048]{0:T(1024)}, u32[]{:S(2)}) copy-start(f32[2048]{0:T(1024)} %param.21) | copy-start | bytes 24580
  109.4 43.5 %copy-start.4 = (f32[1,8,128,128]{3,2,1,0:T(8,128)S(1)}, f32[1,8,128,128]{3,2,1,0:T(8,128)}, u32[]{:S(2)}) copy-start(f32[1,8,128,128]{3,2,1,0:T(8,128)} %custom-call.2) | copy-start | bytes 1572868
  130.6 22.3 %copy-start.2 = (bf16[128,2048]{1,0:T(8,128)(2,1)}, bf16[128,2048]{1,0:T(8,128)(2,1)S(1)}, u32[]{:S(2)}) copy-start(bf16[128,2048]{1,0:T(8,128)(2,1)S(1)} %multiply_convert_fusion) | copy-start | bytes 1572868
  158.2 3.8 %copy-start.1 = (f32[1024,128,8]{1,0,2:T(8,128)S(1)}, f32[1024,128,8]{1,0,2:T(8,128)}, u32[]{:S(2)}) copy-start(f32[1024,128,8]{1,0,2:T(8,128)} %get-tuple-element.335) | copy-start | bytes 12582916 | tf_op jit(solution)/shard_map/while
  168.3 3.8 %copy-start.1 = (f32[1024,128,8]{1,0,2:T(8,128)S(1)}, f32[1024,128,8]{1,0,2:T(8,128)}, u32[]{:S(2)}) copy-start(f32[1024,128,8]{1,0,2:T(8,128)} %get-tuple-element.335) | copy-start | bytes 12582916 | tf_op jit(solution)/shard_map/while
  178.4 3.8 %copy-start.1 = (f32[1024,128,8]{1,0,2:T(8,128)S(1)}, f32[1024,128,8]{1,0,2:T(8,128)}, u32[]{:S(2)}) copy-start(f32[1024,128,8]{1,0,2:T(8,128)} %get-tuple-element.335) | copy-start | bytes 12582916 | tf_op jit(solution)/shard_map/while
  188.5 3.8 %copy-start.1 = (f32[1024,128,8]{1,0,2:T(8,128)S(1)}, f32[1024,128,8]{1,0,2:T(8,128)}, u32[]{:S(2)}) copy-start(f32[1024,128,8]{1,0,2:T(8,128)} %get-tuple-element.335) | copy-start | bytes 12582916 | tf_op jit(solution)/shard_map/while
Sparse Core Ops, SparseCore 0:
  36.0 66.0 all-gather.2
  104.6 48.2 all-gather.4

commit v3 on v2

--- a/solution.py
+++ b/solution.py
@@ -13,7 +13,7 @@
 
 EPSILON = 1e-05
 NEG_FILL = -1e30
-BLOCK_ROWS = 1024
+KEY_CHUNK = 256
 
 
 def segment_ids(positions, doc_lengths):
@@ -150,25 +150,15 @@
             )
             return (best_new, total_new, accum_new)
 
-        def attend_piece(carried, key_rows, value_rows):
-            key_count = key_rows.shape[0]
-            block_count = key_count // BLOCK_ROWS
-            key_blocks = key_rows.reshape(block_count, BLOCK_ROWS, -1)
-            value_blocks = value_rows.reshape(block_count, BLOCK_ROWS, -1)
-
-            def block_turn(inner, scan_item):
-                key_part, value_part, block_index = scan_item
-                return (attend_block(inner, key_part, value_part, block_index * BLOCK_ROWS), None)
-
-            carried, _ = lax.scan(
-                block_turn,
-                carried,
-                (key_blocks, value_blocks, jnp.arange(block_count, dtype=jnp.int32)),
-            )
-            return carried
-
-        def visit(carried, key_rows, value_rows, offset):
-            return attend_piece(carried, key_rows, value_rows)
+        def visit(carried, kv_rows, first_chunk, chunk_count):
+            def chunk_turn(turn, inner):
+                offset = (first_chunk + turn) * KEY_CHUNK
+                piece = lax.dynamic_slice_in_dim(kv_rows, offset, KEY_CHUNK, 0)
+                key_part = piece[:, :, :ATT_DIM].reshape(KEY_CHUNK, -1)
+                value_part = piece[:, :, ATT_DIM:].reshape(KEY_CHUNK, -1)
+                return attend_block(inner, key_part, value_part, offset)
+
+            return lax.fori_loop(0, chunk_count, chunk_turn, carried)
 
         return visit
 
@@ -177,13 +167,20 @@
         jnp.zeros((groups_dev, query_group, tok_rows), jnp.float32),
         jnp.zeros((groups_dev, query_group, tok_rows, ATT_DIM), jnp.float32),
     )
+    kv_local = jnp.concatenate(
+        [
+            keys.reshape(tok_rows, groups_dev, ATT_DIM),
+            values.reshape(tok_rows, groups_dev, ATT_DIM),
+        ],
+        axis=2,
+    )
+    kv_all = lax.all_gather(kv_local, "ctx", axis=0, tiled=True)
+    doc_starts = jnp.cumsum(doc_lengths) - doc_lengths
+    earliest = doc_starts[own_docs[0]]
+    first_chunk = earliest // KEY_CHUNK
+    last_chunk = (first_pos + tok_rows - 1) // KEY_CHUNK
     visit_chosen = make_visit(query, own_pos)
-    final_carry = visit_chosen(
-        initial,
-        lax.all_gather(keys, "ctx", axis=0, tiled=True),
-        lax.all_gather(values, "ctx", axis=0, tiled=True),
-        jnp.int32(0),
-    )
+    final_carry = visit_chosen(initial, kv_all, first_chunk, last_chunk - first_chunk + 1)
     _, score_total, accum = final_carry
     attended = accum / score_total[..., None]
     attn_out = jnp.transpose(attended, (2, 0, 1, 3)).reshape(tok_rows, -1).astype(jnp.bfloat16)

time: 204 us -> 175 us (0.86)
  the two profiles are of different devices: /device:TPU:4 before, /device:TPU:22 now
where the time goes in v3:
time: 175 us; the launch traced here: 171 us
  waiting for transfers between devices  46.6 us (27%)
  matrix products  38.9 us (22%)
  blocking collectives  20.3 us (12%)
  between operations  20.2 us (12%)
  local copies, waits for them, and re-layouts  18.7 us (11%)
  starting transfers between devices  15.2 us (9%)
  other arithmetic  10.7 us (6%)
    all_to_all x1, waiting for transfers between devices, shards(): lax.all_to_all(payload, 'ctx', 0, 0, tiled=True)  26.4 us
    psum x1, blocking collectives, shards(): square_sum = lax.psum(square_local, 'head')  20.3 us
    all_to_all x1, waiting for transfers between devices, shards(): lax.all_to_all(incoming_mine.reshape(ctx_count * owned, lane_rows, state_...  20.2 us
    dot_general x9, matrix products, attend_block(): jnp.einsum('gqtr,rga->gqta', weights.astype(jnp.bfloat16), value_heads, p...  12 us
    dot_general x9, matrix products, attend_block(): jnp.einsum('tgqa,rga->gqtr', query_rows, key_heads, preferred_element_typ...  10.4 us
    all_to_all x1, starting transfers between devices, shards(): lax.all_to_all(incoming_mine.reshape(ctx_count * owned, lane_rows, state_...  7.59 us
    all_to_all x1, starting transfers between devices, shards(): lax.all_to_all(payload, 'ctx', 0, 0, tiled=True)  7.54 us
    dot_general x1, matrix products, shards(): jnp.einsum('tgn,gjnp->tgjp', state_out.astype(jnp.float32), incoming, pre...  5.97 us
  transfers between devices with their start and end apart: 3, of which 2 were waited for; matrix products, arithmetic and copies ran while one was open for 14% of the time, Pallas kernels for 0%

profile of v3, /device:TPU:22, one launch (start us, length us, event | category | flops | bytes accessed | tf_op | source)
XLA Modules:
  0.0 171.3 jit_solution(8321625258652463838)
XLA Ops:
  7.2 0.8 copy.46
  8.1 1.3 fusion.55
  9.5 0.7 fusion.59
  10.8 0.8 fusion.51
  11.7 0.2 slice_reduce_fusion.1
  11.9 1.3 copy.47
  13.2 0.7 compare_convert_fusion.2
  13.9 0.6 slice.33
  14.5 0.8 multiply_bitcast_fusion
  15.4 1.0 convolution_bitcast_fusion.2
  16.4 2.7 %copy.49 = f32[1,32,256,64]{3,2,1,0:T(8,128)} copy(f32[1,32,256,64]{2,3,1,0:T(8,128)S(1)} %convolution_bitcast_fusion.2) | data formatting | bytes 4194304 | tf_op jit(solution)/shard_map/sgn,sgjp->gjnp/transpose | solution.py:62
  19.1 3.6 %reshape.481 = f32[32,8,2048]{2,1,0:T(8,128)S(1)} reshape(f32[1,32,256,64]{3,2,1,0:T(8,128)} %copy.49) | data formatting | bytes 4194304 | tf_op jit(solution)/shard_map/reshape | solution.py:73
  23.4 1.6 pad_maximum_fusion
  25.0 7.5 %all-to-all-start = ((f32[32,8,2176]{2,1,0:T(8,128)}), f32[32,8,2176]{2,1,0:T(8,128)S(1)}, u32[]{:S(2)}, u32[]{:S(2)}) async-start(f32[32,8,2176]{2,1,0:T(8,128)} %pad_maximum_fusion), calls=%async_computation | async-start | bytes 4456448 | tf_op jit(solution)/shard_map/all_to_all | solution.py:75
  32.6 0.6 pad_maximum_fusion.1
  33.3 26.4 %all-to-all-done = f32[32,8,2176]{2,1,0:T(8,128)S(1)} async-done(((f32[32,8,2176]{2,1,0:T(8,128)}), f32[32,8,2176]{2,1,0:T(8,128)S(1)}, u32[]{:S(2)}, u32[]{:S(2)}) %all-to-all-start) | async-done | bytes 2228256 | tf_op jit(solution)/shard_map/all_to_all | solution.py:75
  59.6 0.4 copy.63
  60.2 0.2 select_reduce_fusion
  60.4 1.9 %convolution_bitcast_fusion.1 = f32[32,8,2048]{2,0,1:T(8,128)S(1)} fusion(f32[32,1,8,2176]{3,0,2,1:T(8,128)S(1)} %bitcast.172, f32[32,32]{1,0:T(8,128)S(1)} %select_reduce_fusion), kind=kOutput, calls=%fused_computation.30 | convolution fusion | flops 201328640 | bytes 4210688 | tf_op jit(solution)/shard_map/kcd,dkrf->ckrf/dot_general | solution.py:89
  62.3 2.6 %copy.51 = f32[32,8,2048]{2,1,0:T(8,128)} copy(f32[32,8,2048]{2,0,1:T(8,128)S(1)} %convolution_bitcast_fusion.1) | data formatting | bytes 4194304 | tf_op jit(solution)/shard_map/reshape | solution.py:91
  64.9 7.6 %all-to-all-start.1 = ((f32[32,8,2048]{2,1,0:T(8,128)}), f32[32,8,2048]{2,1,0:T(8,128)S(1)}, u32[]{:S(2)}, u32[]{:S(2)}) async-start(f32[32,8,2048]{2,1,0:T(8,128)} %copy.51), calls=%async_computation.1 | async-start | bytes 4194304 | tf_op jit(solution)/shard_map/all_to_all | solution.py:90
  74.5 0.6 dynamic_slice.9
  77.9 3.6 %fusion.25 = f32[128,1,32,64]{0,3,2,1:T(8,128)} fusion(bf16[128,32,64]{0,2,1:T(8,128)(2,1)S(1)} %bitcast.173, f32[32,128]{1,0:T(8,128)S(1)} %copy-done.6, f32[32,128]{1,0:T(8,128)S(1)} %bitcast.183, f32[128,128]{1,0:T(8,128)S(1)} %fusion.60, pred[128,128]{1,0:T(8,128)(4,1)S(1)} %fusion.50), kind=kOutput, calls=%fused_computation.41 | convolution fusion | flops 404750336 | bytes 1687552 | tf_op jit(solution)/shard_map/gjts,sgjp->tgjp/dot_general | solution.py:100
  81.5 20.2 %all-to-all-done.1 = f32[32,8,2048]{2,1,0:T(8,128)S(1)} async-done(((f32[32,8,2048]{2,1,0:T(8,128)}), f32[32,8,2048]{2,1,0:T(8,128)S(1)}, u32[]{:S(2)}, u32[]{:S(2)}) %all-to-all-start.1) | async-done | bytes 2097184 | tf_op jit(solution)/shard_map/all_to_all | solution.py:90
  101.7 3.0 %reshape.485 = f32[32,256,64]{2,1,0:T(8,128)} reshape(f32[32,8,2048]{2,1,0:T(8,128)S(1)} %all-to-all-done.1) | data formatting | bytes 4194304 | tf_op jit(solution)/shard_map/reshape.58
  104.7 6.0 %fusion.30 = f32[128,1,32,64]{0,3,2,1:T(8,128)S(1)} fusion(f32[128,1,32,64]{0,3,2,1:T(8,128)} %fusion.25, f32[32,256,64]{2,1,0:T(8,128)} %reshape.485, f32[32]{0:T(128)S(1)} %copy-done.8, f32[128,32]{0,1:T(8,128)S(1)} %get-tuple-element.246, bf16[128,256]{1,0:T(8,128)(2,1)S(1)} %copy-done.3, bf16[128,1,32,64]{0,3,2,1:T(8,128)(2,1)S(1)} %bitcast.174), kind=kOutput, calls=%fused_computation.45 | convolution fusion | flops 806617088 | bytes 4800640 | tf_op jit(solution)/shard_map/tgn,gjnp->tgjp/dot_general | solution.py:103
  110.7 0.3 copy.53
  111.0 0.7 copy-done.2
  111.7 0.4 multiply_reduce_fusion
  112.1 20.3 %psum.7 = f32[128]{0:T(128)S(1)} all-reduce(f32[128]{0:T(128)S(1)} %multiply_reduce_fusion), channel_id=1, replica_groups=mesh['ctx'=32,'head'=8] {'head'}, use_global_device_ids=true, to_apply=%region_5.6 | all-reduce | flops 128 | bytes 1024 | tf_op jit(solution)/shard_map/psum | solution.py:110
  132.4 0.4 multiply_convert_fusion
  132.8 3.1 %fusion.34 = bf16[1,16,8,8,128]{4,3,2,1,0:T(8,128)(2,1)S(1)} fusion(bf16[128,2048]{1,0:T(8,128)(2,1)S(1)} %multiply_convert_fusion, bf16[1,2048,1024]{2,1,0:T(8,128)(2,1)} %param.22), kind=kOutput, calls=%fused_computation.49 | convolution fusion | flops 537001984 | bytes 4980736 | tf_op jit(solution)/shard_map/tgf,gfo->tgo/dot_general | solution.py:116
  136.1 27.2 %while.17 = (s32[]{:T(128)}, f32[1,8,128]{2,1,0:T(8,128)S(1)}, f32[1,8,128]{2,1,0:T(8,128)S(1)}, f32[1,8,128,128]{3,2,1,0:T(8,128)S(1)}, s32[]{:T(128)}, /*index...) while((s32[]{:T(128)}, f32[1,8,128]{2,1,0:T(8,128)S(1)}, ...), condition=%wide.region_10.11_spmd.clone, body=%wide.region_6.10_spmd.clone.sunk | while | flops 136953216 | bytes 4793135 | solution.py:161
  136.2 0.1 compare_and_fusion.2
  136.4 1.1 fusion.74
  137.5 1.3 fusion.77
  138.9 0.2 fusion.76
  139.4 1.1 fusion.74
  140.6 1.3 fusion.77
  141.9 0.2 fusion.76
  142.4 1.2 fusion.74
  143.6 1.3 fusion.77
  144.9 0.2 fusion.76
  145.4 1.2 fusion.74
  146.6 1.3 fusion.77
  148.0 0.2 fusion.76
  148.5 1.2 fusion.74
  149.6 1.3 fusion.77
  151.0 0.2 fusion.76
  151.5 1.2 fusion.74
  152.7 1.3 fusion.77
  154.0 0.2 fusion.76
  154.5 1.2 fusion.74
  155.7 1.3 fusion.77
  157.0 0.2 fusion.76
  157.5 1.2 fusion.74
  158.7 1.3 fusion.77
  160.0 0.2 fusion.76
  160.6 1.2 fusion.74
  161.7 1.3 fusion.77
  163.1 0.2 fusion.76
  163.3 0.2 fusion.47
  163.5 0.2 copy.55
  163.7 0.8 copy.64
  (108 shorter events, 3.2 us)
Async XLA Ops:
  7.2 8.2 %copy-start = (bf16[128,256]{1,0:T(8,128)(2,1)S(1)}, bf16[128,256]{1,0:T(8,128)(2,1)}, u32[]{:S(2)}) copy-start(bf16[128,256]{1,0:T(8,128)(2,1)} %param.16) | copy-start | bytes 196612
  25.0 7.6 %copy-start.4 = (bf16[128,128]{1,0:T(8,128)(2,1)S(1)}, bf16[128,128]{1,0:T(8,128)(2,1)}, u32[]{:S(2)}) copy-start(bf16[128,128]{1,0:T(8,128)(2,1)} %param.24) | copy-start | bytes 98308
  25.0 7.6 %copy-start.5 = (bf16[128,128]{1,0:T(8,128)(2,1)S(1)}, bf16[128,128]{1,0:T(8,128)(2,1)}, u32[]{:S(2)}) copy-start(bf16[128,128]{1,0:T(8,128)(2,1)} %param.23) | copy-start | bytes 98308
  25.0 34.7 %all-to-all-start = ((f32[32,8,2176]{2,1,0:T(8,128)}), f32[32,8,2176]{2,1,0:T(8,128)S(1)}, u32[]{:S(2)}, u32[]{:S(2)}) async-start(f32[32,8,2176]{2,1,0:T(8,128)} %pad_maximum_fusion), calls=%async_computation | async-start | bytes 4456448 | tf_op jit(solution)/shard_map/all_to_all | solution.py:75
  32.5 103.5 %all-gather.2.cloned.1.call-start = ((), (), s32[]{:S(2)}) async-start(), calls=%async_computation.2 | async-start | bytes 2162688 | tf_op jit(solution)/shard_map/all_gather | solution.py:177
  64.9 12.8 %copy-start.3 = (bf16[128,256]{1,0:T(8,128)(2,1)S(1)}, bf16[128,256]{1,0:T(8,128)(2,1)}, u32[]{:S(2)}) copy-start(bf16[128,256]{1,0:T(8,128)(2,1)} %param.17) | copy-start | bytes 196612
  64.9 13.0 %copy-start.6 = (f32[32,128]{1,0:T(8,128)S(1)}, f32[32,128]{1,0:T(8,128)}, u32[]{:S(2)}) copy-start(f32[32,128]{1,0:T(8,128)} %param.18) | copy-start | bytes 49156
  64.9 36.8 %all-to-all-start.1 = ((f32[32,8,2048]{2,1,0:T(8,128)}), f32[32,8,2048]{2,1,0:T(8,128)S(1)}, u32[]{:S(2)}, u32[]{:S(2)}) async-start(f32[32,8,2048]{2,1,0:T(8,128)} %copy.51), calls=%async_computation.1 | async-start | bytes 4194304 | tf_op jit(solution)/shard_map/all_to_all | solution.py:90
  81.5 23.2 %copy-start.8 = (f32[32]{0:T(128)S(1)}, f32[32]{0:T(128)}, u32[]{:S(2)}) copy-start(f32[32]{0:T(128)} %param.20) | copy-start | bytes 388
  110.6 1.0 copy-start.2
  110.7 21.7 %copy-start.7 = (f32[2048]{0:T(1024)S(1)}, f32[2048]{0:T(1024)}, u32[]{:S(2)}) copy-start(f32[2048]{0:T(1024)} %param.21) | copy-start | bytes 24580
  132.8 3.2 %copy-start.1 = (bf16[128,2048]{1,0:T(8,128)(2,1)}, bf16[128,2048]{1,0:T(8,128)(2,1)S(1)}, u32[]{:S(2)}) copy-start(bf16[128,2048]{1,0:T(8,128)(2,1)S(1)} %multiply_convert_fusion) | copy-start | bytes 1572868
Sparse Core Ops, SparseCore 0:
  36.5 66.8 all-gather.1

commit v4 on v3

--- a/solution.py
+++ b/solution.py
@@ -60,23 +60,19 @@
     end_weight = jnp.exp(cum_decay[:, :, -1:] - cum_decay) * last_doc[None, None, :] * step_rows
     weighted = input_f32 * jnp.transpose(end_weight, (2, 0, 1))[..., None]
     local_state = jnp.einsum(
-        "sgn,sgjp->gjnp", state_in.astype(jnp.float32), weighted, precision=highest
+        "sgjp,sgn->gjpn", weighted, state_in.astype(jnp.float32), precision=highest
     )
     carry_mask = (own_docs == prev_doc).astype(jnp.float32)
     ctx_count = lax.axis_size("ctx")
     owned = heads_dev // ctx_count
     block_log = jnp.where(carry_mask[-1] > 0, cum_decay[:, :, -1], -jnp.inf).reshape(heads_dev)
-    lane_rows = 8
-    state_cols = STATE * HEAD_DIM // lane_rows
-    log_cols = jnp.broadcast_to(block_log[:, None, None], (heads_dev, lane_rows, 128))
-    payload = jnp.concatenate(
-        [local_state.reshape(heads_dev, lane_rows, state_cols), log_cols], axis=2
-    )
+    log_rows = jnp.broadcast_to(block_log[:, None, None], (heads_dev, 8, STATE))
+    payload = jnp.concatenate([local_state.reshape(heads_dev, HEAD_DIM, STATE), log_rows], axis=1)
     gathered = lax.all_to_all(payload, "ctx", 0, 0, tiled=True).reshape(
-        ctx_count, owned, lane_rows, state_cols + 128
-    )
-    states_mine = gathered[:, :, :, :state_cols]
-    mine_log = gathered[:, :, 0, state_cols]
+        ctx_count, owned, HEAD_DIM + 8, STATE
+    )
+    states_mine = gathered[:, :, :HEAD_DIM, :]
+    mine_log = gathered[:, :, HEAD_DIM, 0]
     block_row = jnp.arange(ctx_count, dtype=jnp.int32)
     between = (block_row[None, :, None] < block_row[None, None, :]) & (
         block_row[None, None, :] < block_row[:, None, None]
@@ -86,10 +82,10 @@
     )
     earlier = block_row[:, None] > block_row[None, :]
     transfer = jnp.where(earlier[None], jnp.exp(log_span), 0.0)
-    incoming_mine = jnp.einsum("kcd,dkrf->ckrf", transfer, states_mine, precision=highest)
+    incoming_mine = jnp.einsum("kcd,dkpn->ckpn", transfer, states_mine, precision=highest)
     incoming = lax.all_to_all(
-        incoming_mine.reshape(ctx_count * owned, lane_rows, state_cols), "ctx", 0, 0, tiled=True
-    ).reshape(groups_dev, head_group, STATE, HEAD_DIM)
+        incoming_mine.reshape(ctx_count * owned, HEAD_DIM, STATE), "ctx", 0, 0, tiled=True
+    ).reshape(groups_dev, head_group, HEAD_DIM, STATE)
     same_doc = (own_docs[:, None] == own_docs[None, :]) & (row_index[:, None] >= row_index[None, :])
     log_gap = cum_decay[:, :, :, None] - cum_decay[:, :, None, :]
     decay_matrix = jnp.exp(jnp.where(same_doc[None, None], log_gap, -jnp.inf))
@@ -100,7 +96,7 @@
     local_out = jnp.einsum("gjts,sgjp->tgjp", mixing, input_f32, precision=highest)
     carry_weight = jnp.exp(cum_decay) * carry_mask[None, None, :]
     carried_out = (
-        jnp.einsum("tgn,gjnp->tgjp", state_out.astype(jnp.float32), incoming, precision=highest)
+        jnp.einsum("tgn,gjpn->tgjp", state_out.astype(jnp.float32), incoming, precision=highest)
         * jnp.transpose(carry_weight, (2, 0, 1))[..., None]
     )
     skip_rows = skip_gain.reshape(groups_dev, head_group)[None, :, :, None] * input_f32

time: 175 us -> 164 us (0.937)
  the two profiles are of different devices: /device:TPU:22 before, /device:TPU:30 now
where the time goes in v4:
time: 164 us; the launch traced here: 163 us
  waiting for transfers between devices  48.1 us (29%)
  matrix products  37.5 us (23%)
  blocking collectives  20.4 us (12%)
  between operations  20.2 us (12%)
  starting transfers between devices  15.1 us (9%)
  other arithmetic  10.6 us (6%)
  local copies, waits for them, and re-layouts  9.93 us (6%)
    all_to_all x1, waiting for transfers between devices, shards(): lax.all_to_all(payload, 'ctx', 0, 0, tiled=True)  27.9 us
    psum x1, blocking collectives, shards(): square_sum = lax.psum(square_local, 'head')  20.4 us
    all_to_all x1, waiting for transfers between devices, shards(): lax.all_to_all(incoming_mine.reshape(ctx_count * owned, HEAD_DIM, STATE),...  20.2 us
    dot_general x9, matrix products, attend_block(): jnp.einsum('gqtr,rga->gqta', weights.astype(jnp.bfloat16), value_heads, p...  12 us
    dot_general x9, matrix products, attend_block(): jnp.einsum('tgqa,rga->gqtr', query_rows, key_heads, preferred_element_typ...  10.4 us
    all_to_all x1, starting transfers between devices, shards(): lax.all_to_all(incoming_mine.reshape(ctx_count * owned, HEAD_DIM, STATE),...  7.63 us
    all_to_all x1, starting transfers between devices, shards(): lax.all_to_all(payload, 'ctx', 0, 0, tiled=True)  7.44 us
    dot_general x1, matrix products, shards(): jnp.einsum('gjts,sgjp->tgjp', mixing, input_f32, precision=highest)  3.55 us
  transfers between devices with their start and end apart: 3, of which 2 were waited for; matrix products, arithmetic and copies ran while one was open for 13% of the time, Pallas kernels for 0%

profile of v4, /device:TPU:30, one launch (start us, length us, event | category | flops | bytes accessed | tf_op | source)
XLA Modules:
  0.0 162.6 jit_solution(1307695073874066572)
XLA Ops:
  7.2 0.8 copy.44
  8.1 1.3 fusion.61
  9.5 0.6 fusion.65
  10.7 0.8 fusion.57
  11.6 0.2 slice_reduce_fusion.1
  11.8 1.3 copy.45
  13.1 0.6 compare_convert_fusion.2
  13.7 0.6 slice.33
  14.9 0.8 multiply_bitcast_fusion
  15.8 1.0 fusion.54
  16.9 1.6 pad_maximum_fusion
  18.5 7.4 %all-to-all-start = ((f32[32,72,256]{2,1,0:T(8,128)}), f32[32,72,256]{2,1,0:T(8,128)S(1)}, u32[]{:S(2)}, u32[]{:S(2)}) async-start(f32[32,72,256]{2,1,0:T(8,128)} %pad_maximum_fusion), calls=%async_computation | async-start | bytes 4718592 | tf_op jit(solution)/shard_map/all_to_all | solution.py:71
  26.0 0.6 pad_maximum_fusion.1
  26.7 27.9 %all-to-all-done = f32[32,72,256]{2,1,0:T(8,128)S(1)} async-done(((f32[32,72,256]{2,1,0:T(8,128)}), f32[32,72,256]{2,1,0:T(8,128)S(1)}, u32[]{:S(2)}, u32[]{:S(2)}) %all-to-all-start) | async-done | bytes 2359328 | tf_op jit(solution)/shard_map/all_to_all | solution.py:71
  54.6 0.3 slice_reduce_fusion
  54.9 0.2 slice_bitcast_fusion
  55.1 0.2 select_reduce_fusion
  55.4 3.2 %fusion.27 = f32[32,64,256]{2,0,1:T(8,128)S(1)} fusion(f32[32,64,256]{2,1,0:T(8,128)S(1)} %slice_bitcast_fusion, f32[32,32]{1,0:T(8,128)S(1)} %select_reduce_fusion), kind=kOutput, calls=%fused_computation.40 | convolution fusion | flops 201328640 | bytes 4198400 | tf_op jit(solution)/shard_map/kcd,dkpn->ckpn/dot_general | solution.py:85
  58.6 2.5 %copy.48 = f32[32,64,256]{2,1,0:T(8,128)} copy(f32[32,64,256]{2,0,1:T(8,128)S(1)} %fusion.27) | data formatting | bytes 4194304 | tf_op jit(solution)/shard_map/reshape | solution.py:87
  61.1 7.6 %all-to-all-start.1 = ((f32[32,64,256]{2,1,0:T(8,128)}), f32[32,64,256]{2,1,0:T(8,128)S(1)}, u32[]{:S(2)}, u32[]{:S(2)}) async-start(f32[32,64,256]{2,1,0:T(8,128)} %copy.48), calls=%async_computation.1 | async-start | bytes 4194304 | tf_op jit(solution)/shard_map/all_to_all | solution.py:86
  70.7 0.6 dynamic_slice.9
  74.2 3.5 %fusion.30 = f32[128,1,32,64]{0,3,2,1:T(8,128)} fusion(bf16[128,32,64]{0,2,1:T(8,128)(2,1)S(1)} %bitcast.164, f32[32,128]{1,0:T(8,128)S(1)} %copy-done.6, f32[32,128]{1,0:T(8,128)S(1)} %bitcast.174, f32[128,128]{1,0:T(8,128)S(1)} %fusion.66, pred[128,128]{1,0:T(8,128)(4,1)S(1)} %fusion.56), kind=kOutput, calls=%fused_computation.41 | convolution fusion | flops 404750336 | bytes 1687552 | tf_op jit(solution)/shard_map/gjts,sgjp->tgjp/dot_general | solution.py:96
  77.7 20.2 %all-to-all-done.1 = f32[32,64,256]{2,1,0:T(8,128)S(1)} async-done(((f32[32,64,256]{2,1,0:T(8,128)}), f32[32,64,256]{2,1,0:T(8,128)S(1)}, u32[]{:S(2)}, u32[]{:S(2)}) %all-to-all-start.1) | async-done | bytes 2097184 | tf_op jit(solution)/shard_map/all_to_all | solution.py:86
  97.9 3.3 %fusion.35 = f32[128,1,32,64]{0,3,2,1:T(8,128)} fusion(f32[128,1,32,64]{0,3,2,1:T(8,128)} %fusion.30, f32[32,64,256]{2,1,0:T(8,128)S(1)} %all-to-all-done.1, f32[32]{0:T(128)S(1)} %copy-done.8, f32[128,32]{0,1:T(8,128)S(1)} %get-tuple-element.246, bf16[128,256]{1,0:T(8,128)(2,1)S(1)} %copy-done.3, bf16[128,1,32,64]{0,3,2,1:T(8,128)(2,1)S(1)} %bitcast.165), kind=kOutput, calls=%fused_computation.45 | convolution fusion | flops 806617088 | bytes 4800640 | tf_op jit(solution)/shard_map/tgn,gjpn->tgjp/dot_general | solution.py:99
  101.2 1.6 copy.49
  102.9 0.4 multiply_reduce_fusion
  103.3 20.4 %psum.7 = f32[128]{0:T(128)S(1)} all-reduce(f32[128]{0:T(128)S(1)} %multiply_reduce_fusion), channel_id=1, replica_groups=mesh['ctx'=32,'head'=8] {'head'}, use_global_device_ids=true, to_apply=%region_5.6 | all-reduce | flops 128 | bytes 1024 | tf_op jit(solution)/shard_map/psum | solution.py:106
  123.7 0.4 multiply_convert_fusion
  124.1 3.1 %fusion.39 = bf16[1,16,8,8,128]{4,3,2,1,0:T(8,128)(2,1)S(1)} fusion(bf16[128,2048]{1,0:T(8,128)(2,1)S(1)} %multiply_convert_fusion, bf16[1,2048,1024]{2,1,0:T(8,128)(2,1)} %param.22), kind=kOutput, calls=%fused_computation.49 | convolution fusion | flops 537001984 | bytes 4980736 | tf_op jit(solution)/shard_map/tgf,gfo->tgo/dot_general | solution.py:112
  127.4 27.2 %while.17 = (s32[]{:T(128)}, f32[1,8,128]{2,1,0:T(8,128)S(1)}, f32[1,8,128]{2,1,0:T(8,128)S(1)}, f32[1,8,128,128]{3,2,1,0:T(8,128)S(1)}, s32[]{:T(128)}, /*index...) while((s32[]{:T(128)}, f32[1,8,128]{2,1,0:T(8,128)S(1)}, ...), condition=%wide.region_10.11_spmd.clone, body=%wide.region_6.10_spmd.clone.sunk | while | flops 136953216 | bytes 4793135 | solution.py:157
  127.5 0.1 compare_and_fusion.2
  127.7 1.2 fusion.80
  128.8 1.3 fusion.83
  130.2 0.2 fusion.82
  130.5 0.1 compare_and_fusion.2
  130.7 1.2 fusion.80
  131.9 1.3 fusion.83
  133.2 0.2 fusion.82
  133.7 1.2 fusion.80
  134.9 1.3 fusion.83
  136.2 0.2 fusion.82
  136.6 0.1 compare_and_fusion.2
  136.7 1.2 fusion.80
  137.9 1.3 fusion.83
  139.2 0.2 fusion.82
  139.6 0.1 compare_and_fusion.2
  139.8 1.2 fusion.80
  140.9 1.3 fusion.83
  142.3 0.2 fusion.82
  142.8 1.2 fusion.80
  143.9 1.3 fusion.83
  145.3 0.2 fusion.82
  145.8 1.2 fusion.80
  147.0 1.3 fusion.83
  148.3 0.2 fusion.82
  148.8 1.2 fusion.80
  150.0 1.3 fusion.83
  151.3 0.2 fusion.82
  151.8 1.2 fusion.80
  153.0 1.3 fusion.83
  154.4 0.2 fusion.82
  154.6 0.2 fusion.52
  154.8 0.2 copy.51
  155.0 0.8 copy.61
  (105 shorter events, 2.7 us)
Async XLA Ops:
  7.2 8.7 %copy-start = (bf16[128,256]{1,0:T(8,128)(2,1)S(1)}, bf16[128,256]{1,0:T(8,128)(2,1)}, u32[]{:S(2)}) copy-start(bf16[128,256]{1,0:T(8,128)(2,1)} %param.16) | copy-start | bytes 196612
  18.5 7.5 %copy-start.4 = (bf16[128,128]{1,0:T(8,128)(2,1)S(1)}, bf16[128,128]{1,0:T(8,128)(2,1)}, u32[]{:S(2)}) copy-start(bf16[128,128]{1,0:T(8,128)(2,1)} %param.24) | copy-start | bytes 98308
  18.5 7.5 %copy-start.5 = (bf16[128,128]{1,0:T(8,128)(2,1)S(1)}, bf16[128,128]{1,0:T(8,128)(2,1)}, u32[]{:S(2)}) copy-start(bf16[128,128]{1,0:T(8,128)(2,1)} %param.23) | copy-start | bytes 98308
  18.5 36.1 %all-to-all-start = ((f32[32,72,256]{2,1,0:T(8,128)}), f32[32,72,256]{2,1,0:T(8,128)S(1)}, u32[]{:S(2)}, u32[]{:S(2)}) async-start(f32[32,72,256]{2,1,0:T(8,128)} %pad_maximum_fusion), calls=%async_computation | async-start | bytes 4718592 | tf_op jit(solution)/shard_map/all_to_all | solution.py:71
  25.9 101.4 %all-gather.2.cloned.1.call-start = ((), (), s32[]{:S(2)}) async-start(), calls=%async_computation.2 | async-start | bytes 2162688 | tf_op jit(solution)/shard_map/all_gather | solution.py:173
  61.1 12.9 %copy-start.3 = (bf16[128,256]{1,0:T(8,128)(2,1)S(1)}, bf16[128,256]{1,0:T(8,128)(2,1)}, u32[]{:S(2)}) copy-start(bf16[128,256]{1,0:T(8,128)(2,1)} %param.17) | copy-start | bytes 196612
  61.1 13.0 %copy-start.6 = (f32[32,128]{1,0:T(8,128)S(1)}, f32[32,128]{1,0:T(8,128)}, u32[]{:S(2)}) copy-start(f32[32,128]{1,0:T(8,128)} %param.18) | copy-start | bytes 49156
  61.1 36.8 %all-to-all-start.1 = ((f32[32,64,256]{2,1,0:T(8,128)}), f32[32,64,256]{2,1,0:T(8,128)S(1)}, u32[]{:S(2)}, u32[]{:S(2)}) async-start(f32[32,64,256]{2,1,0:T(8,128)} %copy.48), calls=%async_computation.1 | async-start | bytes 4194304 | tf_op jit(solution)/shard_map/all_to_all | solution.py:86
  73.9 24.1 %copy-start.8 = (f32[32]{0:T(128)S(1)}, f32[32]{0:T(128)}, u32[]{:S(2)}) copy-start(f32[32]{0:T(128)} %param.20) | copy-start | bytes 388
  101.2 1.6 %copy-start.2 = (bf16[128,2048]{1,0:T(8,128)(2,1)S(1)}, bf16[128,2048]{1,0:T(8,128)(2,1)}, u32[]{:S(2)}) copy-start(bf16[128,2048]{1,0:T(8,128)(2,1)} %param.15) | copy-start | bytes 1572868
  101.2 22.4 %copy-start.7 = (f32[2048]{0:T(1024)S(1)}, f32[2048]{0:T(1024)}, u32[]{:S(2)}) copy-start(f32[2048]{0:T(1024)} %param.21) | copy-start | bytes 24580
  124.1 3.2 %copy-start.1 = (bf16[128,2048]{1,0:T(8,128)(2,1)}, bf16[128,2048]{1,0:T(8,128)(2,1)S(1)}, u32[]{:S(2)}) copy-start(bf16[128,2048]{1,0:T(8,128)(2,1)S(1)} %multiply_convert_fusion) | copy-start | bytes 1572868
Sparse Core Ops, SparseCore 0:
  29.9 69.2 all-gather.1

commit v5 on v4

--- a/solution.py
+++ b/solution.py
@@ -103,7 +103,14 @@
     mixer_full = (local_out + carried_out + skip_rows).reshape(tok_rows, -1)
     gated = mixer_full * jax.nn.silu(gate.astype(jnp.float32))
     square_local = jnp.sum(gated * gated, axis=1)
-    square_sum = lax.psum(square_local, "head")
+    head_count = lax.axis_size("head")
+    square_sum = square_local
+    for shift in range(1, head_count):
+        square_sum = square_sum + lax.ppermute(
+            square_local,
+            "head",
+            [(source, (source + shift) % head_count) for source in range(head_count)],
+        )
     mixer_out = (
         gated
         * lax.rsqrt(square_sum / (MIXER_HEADS * HEAD_DIM) + EPSILON)[:, None]

time: 164 us -> 168 us (1.024)
  the two profiles are of different devices: /device:TPU:30 before, /device:TPU:6 now
where the time goes in v5:
time: 168 us; the launch traced here: 167 us
  waiting for transfers between devices  50.9 us (30%)
  matrix products  40 us (24%)
  starting transfers between devices  33.7 us (20%)
  between operations  20.2 us (12%)
  other arithmetic  11 us (7%)
  local copies, waits for them, and re-layouts  9.98 us (6%)
    all_to_all x1, waiting for transfers between devices, shards(): lax.all_to_all(payload, 'ctx', 0, 0, tiled=True)  28.1 us
    all_to_all x1, waiting for transfers between devices, shards(): lax.all_to_all(incoming_mine.reshape(ctx_count * owned, HEAD_DIM, STATE),...  20.3 us
    ppermute x7, starting transfers between devices, shards(): lax.ppermute(square_local, 'head', [(source, (source + shift) % head_coun...  18.6 us
    dot_general x10, matrix products, attend_block(): jnp.einsum('gqtr,rga->gqta', weights.astype(jnp.bfloat16), value_heads, p...  13.3 us
    dot_general x10, matrix products, attend_block(): jnp.einsum('tgqa,rga->gqtr', query_rows, key_heads, preferred_element_typ...  11.5 us
    all_to_all x1, starting transfers between devices, shards(): lax.all_to_all(payload, 'ctx', 0, 0, tiled=True)  7.74 us
    all_to_all x1, starting transfers between devices, shards(): lax.all_to_all(incoming_mine.reshape(ctx_count * owned, HEAD_DIM, STATE),...  7.38 us
    dot_general x1, matrix products, shards(): jnp.einsum('gjts,sgjp->tgjp', mixing, input_f32, precision=highest)  3.54 us
  transfers between devices with their start and end apart: 10, of which 4 were waited for; matrix products, arithmetic and copies ran while one was open for 12% of the time, Pallas kernels for 0%

profile of v5, /device:TPU:6, one launch (start us, length us, event | category | flops | bytes accessed | tf_op | source)
XLA Modules:
  0.0 166.7 jit_solution(15230764750014686643)
XLA Ops:
  7.2 0.8 copy.44
  8.1 1.3 fusion.61
  9.5 0.6 fusion.65
  10.7 0.8 fusion.57
  11.6 0.2 slice_reduce_fusion.1
  11.8 1.3 copy.45
  13.1 0.6 compare_convert_fusion.2
  13.7 0.6 slice.33
  14.9 0.8 multiply_bitcast_fusion
  15.8 1.0 fusion.54
  16.9 1.6 pad_maximum_fusion
  18.5 7.7 %all-to-all-start = ((f32[32,72,256]{2,1,0:T(8,128)}), f32[32,72,256]{2,1,0:T(8,128)S(1)}, u32[]{:S(2)}, u32[]{:S(2)}) async-start(f32[32,72,256]{2,1,0:T(8,128)} %pad_maximum_fusion), calls=%async_computation | async-start | bytes 4718592 | tf_op jit(solution)/shard_map/all_to_all | solution.py:71
  26.3 0.6 pad_maximum_fusion.1
  27.0 28.1 %all-to-all-done = f32[32,72,256]{2,1,0:T(8,128)S(1)} async-done(((f32[32,72,256]{2,1,0:T(8,128)}), f32[32,72,256]{2,1,0:T(8,128)S(1)}, u32[]{:S(2)}, u32[]{:S(2)}) %all-to-all-start) | async-done | bytes 2359328 | tf_op jit(solution)/shard_map/all_to_all | solution.py:71
  55.1 0.3 slice_reduce_fusion
  55.5 0.2 slice_bitcast_fusion
  55.7 0.2 select_reduce_fusion
  55.9 3.2 %fusion.27 = f32[32,64,256]{2,0,1:T(8,128)S(1)} fusion(f32[32,64,256]{2,1,0:T(8,128)S(1)} %slice_bitcast_fusion, f32[32,32]{1,0:T(8,128)S(1)} %select_reduce_fusion), kind=kOutput, calls=%fused_computation.40 | convolution fusion | flops 201328640 | bytes 4198400 | tf_op jit(solution)/shard_map/kcd,dkpn->ckpn/dot_general | solution.py:85
  59.1 2.6 %copy.48 = f32[32,64,256]{2,1,0:T(8,128)} copy(f32[32,64,256]{2,0,1:T(8,128)S(1)} %fusion.27) | data formatting | bytes 4194304 | tf_op jit(solution)/shard_map/reshape | solution.py:87
  61.7 7.4 %all-to-all-start.1 = ((f32[32,64,256]{2,1,0:T(8,128)}), f32[32,64,256]{2,1,0:T(8,128)S(1)}, u32[]{:S(2)}, u32[]{:S(2)}) async-start(f32[32,64,256]{2,1,0:T(8,128)} %copy.48), calls=%async_computation.1 | async-start | bytes 4194304 | tf_op jit(solution)/shard_map/all_to_all | solution.py:86
  71.0 0.6 dynamic_slice.9
  74.5 3.5 %fusion.30 = f32[128,1,32,64]{0,3,2,1:T(8,128)} fusion(bf16[128,32,64]{0,2,1:T(8,128)(2,1)S(1)} %bitcast.164, f32[32,128]{1,0:T(8,128)S(1)} %copy-done.6, f32[32,128]{1,0:T(8,128)S(1)} %bitcast.174, f32[128,128]{1,0:T(8,128)S(1)} %fusion.66, pred[128,128]{1,0:T(8,128)(4,1)S(1)} %fusion.56), kind=kOutput, calls=%fused_computation.41 | convolution fusion | flops 404750336 | bytes 1687552 | tf_op jit(solution)/shard_map/gjts,sgjp->tgjp/dot_general | solution.py:96
  78.1 20.3 %all-to-all-done.1 = f32[32,64,256]{2,1,0:T(8,128)S(1)} async-done(((f32[32,64,256]{2,1,0:T(8,128)}), f32[32,64,256]{2,1,0:T(8,128)S(1)}, u32[]{:S(2)}, u32[]{:S(2)}) %all-to-all-start.1) | async-done | bytes 2097184 | tf_op jit(solution)/shard_map/all_to_all | solution.py:86
  98.3 3.3 %fusion.35 = f32[128,1,32,64]{0,3,2,1:T(8,128)} fusion(f32[128,1,32,64]{0,3,2,1:T(8,128)} %fusion.30, f32[32,64,256]{2,1,0:T(8,128)S(1)} %all-to-all-done.1, f32[32]{0:T(128)S(1)} %copy-done.8, f32[128,32]{0,1:T(8,128)S(1)} %get-tuple-element.246, bf16[128,256]{1,0:T(8,128)(2,1)S(1)} %copy-done.3, bf16[128,1,32,64]{0,3,2,1:T(8,128)(2,1)S(1)} %bitcast.165), kind=kOutput, calls=%fused_computation.45 | convolution fusion | flops 806617088 | bytes 4800640 | tf_op jit(solution)/shard_map/tgn,gjpn->tgjp/dot_general | solution.py:99
  101.6 1.6 copy.49
  103.2 0.4 multiply_reduce_fusion
  103.7 2.1 %collective-permute-start = (f32[128]{0:T(128)S(1)}, f32[128]{0:T(128)S(1)}, u32[]{:S(2)}, u32[]{:S(2)}) collective-permute-start(f32[128]{0:T(128)S(1)} %multiply_reduce_fusion), channel_id=1, source_target_pairs={{0,1},{1,2},{2,3},{3,4},{4,5},{5,6},{6,7},{7,0},{8,9},{9,10},{10,1... | collective-permute-start | bytes 1544 | tf_op jit(solution)/shard_map/ppermute | solution.py:109
  105.7 3.3 %collective-permute-start.1 = (f32[128]{0:T(128)S(1)}, f32[128]{0:T(128)S(1)}, u32[]{:S(2)}, u32[]{:S(2)}) collective-permute-start(f32[128]{0:T(128)S(1)} %multiply_reduce_fusion), channel_id=1, source_target_pairs={{0,2},{1,3},{2,4},{3,5},{4,6},{5,7},{6,0},{7,1},{8,10},{9,11},{10,... | collective-permute-start | bytes 1544 | tf_op jit(solution)/shard_map/ppermute | solution.py:109
  109.0 4.1 %collective-permute-start.2 = (f32[128]{0:T(128)S(1)}, f32[128]{0:T(128)S(1)}, u32[]{:S(2)}, u32[]{:S(2)}) collective-permute-start(f32[128]{0:T(128)S(1)} %multiply_reduce_fusion), channel_id=1, source_target_pairs={{0,3},{1,4},{2,5},{3,6},{4,7},{5,0},{6,1},{7,2},{8,11},{9,12},{10,... | collective-permute-start | bytes 1544 | tf_op jit(solution)/shard_map/ppermute | solution.py:109
  113.1 1.0 collective-permute-start.3
  114.1 5.0 %collective-permute-start.4 = (f32[128]{0:T(128)S(1)}, f32[128]{0:T(128)S(1)}, u32[]{:S(2)}, u32[]{:S(2)}) collective-permute-start(f32[128]{0:T(128)S(1)} %multiply_reduce_fusion), channel_id=1, source_target_pairs={{0,5},{1,6},{2,7},{3,0},{4,1},{5,2},{6,3},{7,4},{8,13},{9,14},{10,... | collective-permute-start | bytes 1544 | tf_op jit(solution)/shard_map/ppermute | solution.py:109
  119.2 2.0 %collective-permute-start.5 = (f32[128]{0:T(128)S(1)}, f32[128]{0:T(128)S(1)}, u32[]{:S(2)}, u32[]{:S(2)}) collective-permute-start(f32[128]{0:T(128)S(1)} %multiply_reduce_fusion), channel_id=1, source_target_pairs={{0,6},{1,7},{2,0},{3,1},{4,2},{5,3},{6,4},{7,5},{8,14},{9,15},{10,... | collective-permute-start | bytes 1544 | tf_op jit(solution)/shard_map/ppermute | solution.py:109
  121.2 1.1 collective-permute-start.6
  122.3 1.4 collective-permute-done.5
  123.6 1.1 collective-permute-done.6
  124.8 0.4 multiply_convert_fusion
  125.2 3.1 %fusion.39 = bf16[1,16,8,8,128]{4,3,2,1,0:T(8,128)(2,1)S(1)} fusion(bf16[128,2048]{1,0:T(8,128)(2,1)S(1)} %multiply_convert_fusion, bf16[1,2048,1024]{2,1,0:T(8,128)(2,1)} %param.22), kind=kOutput, calls=%fused_computation.49 | convolution fusion | flops 537001984 | bytes 4980736 | tf_op jit(solution)/shard_map/tgf,gfo->tgo/dot_general | solution.py:119
  128.5 30.2 %while.17 = (s32[]{:T(128)}, f32[1,8,128]{2,1,0:T(8,128)S(1)}, f32[1,8,128]{2,1,0:T(8,128)S(1)}, f32[1,8,128,128]{3,2,1,0:T(8,128)S(1)}, s32[]{:T(128)}, /*index...) while((s32[]{:T(128)}, f32[1,8,128]{2,1,0:T(8,128)S(1)}, ...), condition=%wide.region_9.10_spmd.clone, body=%wide.region_5.9_spmd.clone.sunk | while | flops 136953216 | bytes 4793135 | solution.py:164
  128.7 1.1 fusion.80
  129.9 1.3 fusion.83
  131.3 0.2 fusion.82
  131.8 1.1 fusion.80
  132.9 1.3 fusion.83
  134.3 0.2 fusion.82
  134.8 1.1 fusion.80
  136.0 1.3 fusion.83
  137.3 0.2 fusion.82
  137.8 1.1 fusion.80
  139.0 1.3 fusion.83
  140.3 0.2 fusion.82
  140.8 1.1 fusion.80
  142.0 1.3 fusion.83
  143.9 1.1 fusion.80
  145.0 1.3 fusion.83
  146.9 1.1 fusion.80
  148.1 1.3 fusion.83
  149.9 1.1 fusion.80
  151.1 1.3 fusion.83
  152.9 1.1 fusion.80
  154.1 1.3 fusion.83
  155.9 1.1 fusion.80
  157.1 1.3 fusion.83
  158.7 0.2 fusion.52
  159.1 0.8 copy.61
  (129 shorter events, 4.8 us)
Async XLA Ops:
  7.2 8.7 %copy-start = (bf16[128,256]{1,0:T(8,128)(2,1)S(1)}, bf16[128,256]{1,0:T(8,128)(2,1)}, u32[]{:S(2)}) copy-start(bf16[128,256]{1,0:T(8,128)(2,1)} %param.16) | copy-start | bytes 196612
  18.5 7.8 %copy-start.4 = (bf16[128,128]{1,0:T(8,128)(2,1)S(1)}, bf16[128,128]{1,0:T(8,128)(2,1)}, u32[]{:S(2)}) copy-start(bf16[128,128]{1,0:T(8,128)(2,1)} %param.24) | copy-start | bytes 98308
  18.5 7.8 %copy-start.5 = (bf16[128,128]{1,0:T(8,128)(2,1)S(1)}, bf16[128,128]{1,0:T(8,128)(2,1)}, u32[]{:S(2)}) copy-start(bf16[128,128]{1,0:T(8,128)(2,1)} %param.23) | copy-start | bytes 98308
  18.5 36.6 %all-to-all-start = ((f32[32,72,256]{2,1,0:T(8,128)}), f32[32,72,256]{2,1,0:T(8,128)S(1)}, u32[]{:S(2)}, u32[]{:S(2)}) async-start(f32[32,72,256]{2,1,0:T(8,128)} %pad_maximum_fusion), calls=%async_computation | async-start | bytes 4718592 | tf_op jit(solution)/shard_map/all_to_all | solution.py:71
  26.2 102.1 %all-gather.2.cloned.1.call-start = ((), (), s32[]{:S(2)}) async-start(), calls=%async_computation.2 | async-start | bytes 2162688 | tf_op jit(solution)/shard_map/all_gather | solution.py:180
  61.7 12.6 %copy-start.3 = (bf16[128,256]{1,0:T(8,128)(2,1)S(1)}, bf16[128,256]{1,0:T(8,128)(2,1)}, u32[]{:S(2)}) copy-start(bf16[128,256]{1,0:T(8,128)(2,1)} %param.17) | copy-start | bytes 196612
  61.7 12.8 %copy-start.6 = (f32[32,128]{1,0:T(8,128)S(1)}, f32[32,128]{1,0:T(8,128)}, u32[]{:S(2)}) copy-start(f32[32,128]{1,0:T(8,128)} %param.18) | copy-start | bytes 49156
  61.7 36.6 %all-to-all-start.1 = ((f32[32,64,256]{2,1,0:T(8,128)}), f32[32,64,256]{2,1,0:T(8,128)S(1)}, u32[]{:S(2)}, u32[]{:S(2)}) async-start(f32[32,64,256]{2,1,0:T(8,128)} %copy.48), calls=%async_computation.1 | async-start | bytes 4194304 | tf_op jit(solution)/shard_map/all_to_all | solution.py:86
  71.6 26.7 %copy-start.8 = (f32[32]{0:T(128)S(1)}, f32[32]{0:T(128)}, u32[]{:S(2)}) copy-start(f32[32]{0:T(128)} %param.20) | copy-start | bytes 388
  101.6 1.6 copy-start.2
  101.6 23.1 %copy-start.7 = (f32[2048]{0:T(1024)S(1)}, f32[2048]{0:T(1024)}, u32[]{:S(2)}) copy-start(f32[2048]{0:T(1024)} %param.21) | copy-start | bytes 24580
  103.7 15.5 %collective-permute-start = (f32[128]{0:T(128)S(1)}, f32[128]{0:T(128)S(1)}, u32[]{:S(2)}, u32[]{:S(2)}) collective-permute-start(f32[128]{0:T(128)S(1)} %multiply_reduce_fusion), channel_id=1, source_target_pairs={{0,1},{1,2},{2,3},{3,4},{4,5},{5,6},{6,7},{7,0},{8,9},{9,10},{10,1... | collective-permute-start | bytes 1544 | tf_op jit(solution)/shard_map/ppermute | solution.py:109
  105.7 15.4 %collective-permute-start.1 = (f32[128]{0:T(128)S(1)}, f32[128]{0:T(128)S(1)}, u32[]{:S(2)}, u32[]{:S(2)}) collective-permute-start(f32[128]{0:T(128)S(1)} %multiply_reduce_fusion), channel_id=1, source_target_pairs={{0,2},{1,3},{2,4},{3,5},{4,6},{5,7},{6,0},{7,1},{8,10},{9,11},{10,... | collective-permute-start | bytes 1544 | tf_op jit(solution)/shard_map/ppermute | solution.py:109
  109.0 13.2 %collective-permute-start.2 = (f32[128]{0:T(128)S(1)}, f32[128]{0:T(128)S(1)}, u32[]{:S(2)}, u32[]{:S(2)}) collective-permute-start(f32[128]{0:T(128)S(1)} %multiply_reduce_fusion), channel_id=1, source_target_pairs={{0,3},{1,4},{2,5},{3,6},{4,7},{5,0},{6,1},{7,2},{8,11},{9,12},{10,... | collective-permute-start | bytes 1544 | tf_op jit(solution)/shard_map/ppermute | solution.py:109
  113.1 9.1 %collective-permute-start.3 = (f32[128]{0:T(128)S(1)}, f32[128]{0:T(128)S(1)}, u32[]{:S(2)}, u32[]{:S(2)}) collective-permute-start(f32[128]{0:T(128)S(1)} %multiply_reduce_fusion), channel_id=1, source_target_pairs={{0,4},{1,5},{2,6},{3,7},{4,0},{5,1},{6,2},{7,3},{8,12},{9,13},{10,... | collective-permute-start | bytes 1544 | tf_op jit(solution)/shard_map/ppermute | solution.py:109
  114.1 8.1 %collective-permute-start.4 = (f32[128]{0:T(128)S(1)}, f32[128]{0:T(128)S(1)}, u32[]{:S(2)}, u32[]{:S(2)}) collective-permute-start(f32[128]{0:T(128)S(1)} %multiply_reduce_fusion), channel_id=1, source_target_pairs={{0,5},{1,6},{2,7},{3,0},{4,1},{5,2},{6,3},{7,4},{8,13},{9,14},{10,... | collective-permute-start | bytes 1544 | tf_op jit(solution)/shard_map/ppermute | solution.py:109
  119.2 4.4 %collective-permute-start.5 = (f32[128]{0:T(128)S(1)}, f32[128]{0:T(128)S(1)}, u32[]{:S(2)}, u32[]{:S(2)}) collective-permute-start(f32[128]{0:T(128)S(1)} %multiply_reduce_fusion), channel_id=1, source_target_pairs={{0,6},{1,7},{2,0},{3,1},{4,2},{5,3},{6,4},{7,5},{8,14},{9,15},{10,... | collective-permute-start | bytes 1544 | tf_op jit(solution)/shard_map/ppermute | solution.py:109
  121.2 3.5 %collective-permute-start.6 = (f32[128]{0:T(128)S(1)}, f32[128]{0:T(128)S(1)}, u32[]{:S(2)}, u32[]{:S(2)}) collective-permute-start(f32[128]{0:T(128)S(1)} %multiply_reduce_fusion), channel_id=1, source_target_pairs={{0,7},{1,0},{2,1},{3,2},{4,3},{5,4},{6,5},{7,6},{8,15},{9,8},{10,9... | collective-permute-start | bytes 1544 | tf_op jit(solution)/shard_map/ppermute | solution.py:109
  125.1 3.2 %copy-start.1 = (bf16[128,2048]{1,0:T(8,128)(2,1)}, bf16[128,2048]{1,0:T(8,128)(2,1)S(1)}, u32[]{:S(2)}) copy-start(bf16[128,2048]{1,0:T(8,128)(2,1)S(1)} %multiply_convert_fusion) | copy-start | bytes 1572868
Sparse Core Ops, SparseCore 0:
  30.2 70.9 all-gather.1

commit v6 on v4

--- a/solution.py
+++ b/solution.py
@@ -2,6 +2,8 @@
 import jax.numpy as jnp
 from jax import lax
 from jax.sharding import PartitionSpec as P
+from jax.experimental import pallas as pl
+from jax.experimental.pallas import tpu as pltpu
 
 MIXER_HEADS = 256
 HEAD_DIM = 64
@@ -20,6 +22,64 @@
     doc_starts = jnp.cumsum(doc_lengths) - doc_lengths
     hits = (doc_starts[None, :] <= positions[:, None]).astype(jnp.int32)
     return jnp.sum(hits, axis=1) - 1
+
+
+def attention_kernel(chunk_ref, query_ref, kv_ref, low_ref, high_ref, out_ref):
+    rows = query_ref.shape[0]
+    query_rows = query_ref[...]
+    low = low_ref[...]
+    high = high_ref[...]
+
+    def chunk_turn(turn, carried):
+        best_old, total_old, accum_old = carried
+        start = pl.multiple_of((chunk_ref[0] + turn) * KEY_CHUNK, KEY_CHUNK)
+        piece = kv_ref[pl.ds(start, KEY_CHUNK), :]
+        key_part = piece[:, :ATT_DIM]
+        value_part = piece[:, ATT_DIM:]
+        scores = lax.dot_general(
+            query_rows, key_part, (((1,), (1,)), ((), ())), preferred_element_type=jnp.float32
+        ) * ATT_DIM ** (-0.5)
+        key_pos = start + lax.broadcasted_iota(jnp.int32, (rows, KEY_CHUNK), 1)
+        visible = (key_pos >= low) & (key_pos <= high)
+        scores = jnp.where(visible, scores, NEG_FILL)
+        best_new = jnp.maximum(best_old, jnp.max(scores, axis=1, keepdims=True))
+        weights = jnp.where(visible, jnp.exp(scores - best_new), 0.0)
+        rescale = jnp.exp(best_old - best_new)
+        total_new = total_old * rescale + jnp.sum(weights, axis=1, keepdims=True)
+        accum_new = accum_old * rescale + jnp.dot(
+            weights.astype(jnp.bfloat16), value_part, preferred_element_type=jnp.float32
+        )
+        return (best_new, total_new, accum_new)
+
+    initial = (
+        jnp.full((rows, 1), NEG_FILL, jnp.float32),
+        jnp.zeros((rows, 1), jnp.float32),
+        jnp.zeros((rows, ATT_DIM), jnp.float32),
+    )
+    _, total, accum = lax.fori_loop(0, chunk_ref[1], chunk_turn, initial)
+    out_ref[...] = (accum / total).astype(out_ref.dtype)
+
+
+def flash_attention(query_flat, kv_rows, low, high, first_chunk, chunk_count):
+    rows, width = query_flat.shape
+    heads = width // ATT_DIM
+    chunk_info = jnp.stack([first_chunk, chunk_count]).astype(jnp.int32)
+    grid_spec = pltpu.PrefetchScalarGridSpec(
+        num_scalar_prefetch=1,
+        grid=(heads,),
+        in_specs=[
+            pl.BlockSpec((rows, ATT_DIM), lambda i, info: (0, i)),
+            pl.BlockSpec(kv_rows.shape, lambda i, info: (0, 0)),
+            pl.BlockSpec((rows, 1), lambda i, info: (0, 0)),
+            pl.BlockSpec((rows, 1), lambda i, info: (0, 0)),
+        ],
+        out_specs=pl.BlockSpec((rows, ATT_DIM), lambda i, info: (0, i)),
+    )
+    return pl.pallas_call(
+        attention_kernel,
+        grid_spec=grid_spec,
+        out_shape=jax.ShapeDtypeStruct((rows, width), jnp.bfloat16),
+    )(chunk_info, query_flat, kv_rows, low, high)
 
 
 def shards(
@@ -117,52 +177,6 @@
     )
     query = query.astype(jnp.bfloat16).reshape(tok_rows, groups_dev, query_group, ATT_DIM)
 
-    def make_visit(query_rows, query_pos):
-        query_docs = segment_ids(query_pos, doc_lengths)
-
-        def attend_block(carried, key_rows, value_rows, offset):
-            key_count = key_rows.shape[0]
-            key_pos = offset + jnp.arange(key_count, dtype=jnp.int32)
-            key_docs = segment_ids(key_pos, doc_lengths)
-            visible = (query_docs[:, None] == key_docs[None, :]) & (
-                key_pos[None, :] <= query_pos[:, None]
-            )
-            key_heads = key_rows.reshape(key_count, groups_dev, ATT_DIM)
-            value_heads = value_rows.reshape(key_count, groups_dev, ATT_DIM)
-            scores = jnp.einsum(
-                "tgqa,rga->gqtr", query_rows, key_heads, preferred_element_type=jnp.float32
-            ) * ATT_DIM ** (-0.5)
-            scores = jnp.where(visible[None, None], scores, NEG_FILL)
-            best_old, total_old, accum_old = carried
-            best_new = jnp.maximum(best_old, jnp.max(scores, axis=-1))
-            weights = jnp.where(visible[None, None], jnp.exp(scores - best_new[..., None]), 0.0)
-            rescale = jnp.exp(best_old - best_new)
-            total_new = total_old * rescale + jnp.sum(weights, axis=-1)
-            accum_new = accum_old * rescale[..., None] + jnp.einsum(
-                "gqtr,rga->gqta",
-                weights.astype(jnp.bfloat16),
-                value_heads,
-                preferred_element_type=jnp.float32,
-            )
-            return (best_new, total_new, accum_new)
-
-        def visit(carried, kv_rows, first_chunk, chunk_count):
-            def chunk_turn(turn, inner):
-                offset = (first_chunk + turn) * KEY_CHUNK
-                piece = lax.dynamic_slice_in_dim(kv_rows, offset, KEY_CHUNK, 0)
-                key_part = piece[:, :, :ATT_DIM].reshape(KEY_CHUNK, -1)
-                value_part = piece[:, :, ATT_DIM:].reshape(KEY_CHUNK, -1)
-                return attend_block(inner, key_part, value_part, offset)
-
-            return lax.fori_loop(0, chunk_count, chunk_turn, carried)
-
-        return visit
-
-    initial = (
-        jnp.full((groups_dev, query_group, tok_rows), NEG_FILL, jnp.float32),
-        jnp.zeros((groups_dev, query_group, tok_rows), jnp.float32),
-        jnp.zeros((groups_dev, query_group, tok_rows, ATT_DIM), jnp.float32),
-    )
     kv_local = jnp.concatenate(
         [
             keys.reshape(tok_rows, groups_dev, ATT_DIM),
@@ -172,14 +186,22 @@
     )
     kv_all = lax.all_gather(kv_local, "ctx", axis=0, tiled=True)
     doc_starts = jnp.cumsum(doc_lengths) - doc_lengths
-    earliest = doc_starts[own_docs[0]]
-    first_chunk = earliest // KEY_CHUNK
+    row_low = doc_starts[own_docs]
+    first_chunk = row_low[0] // KEY_CHUNK
     last_chunk = (first_pos + tok_rows - 1) // KEY_CHUNK
-    visit_chosen = make_visit(query, own_pos)
-    final_carry = visit_chosen(initial, kv_all, first_chunk, last_chunk - first_chunk + 1)
-    _, score_total, accum = final_carry
-    attended = accum / score_total[..., None]
-    attn_out = jnp.transpose(attended, (2, 0, 1, 3)).reshape(tok_rows, -1).astype(jnp.bfloat16)
+    group_outs = []
+    for group in range(groups_dev):
+        group_outs.append(
+            flash_attention(
+                query[:, group].reshape(tok_rows, query_group * ATT_DIM),
+                kv_all[:, group],
+                row_low[:, None],
+                own_pos[:, None],
+                first_chunk,
+                last_chunk - first_chunk + 1,
+            )
+        )
+    attn_out = jnp.concatenate(group_outs, axis=1)
     return (mixer_out, attn_out)
 
 

time: 164 us -> 180 us (1.098)
  the two profiles are of different devices: /device:TPU:30 before, /device:TPU:28 now
where the time goes in v6:
time: 180 us
  waiting for transfers between devices  50.6 us (28%)
  Pallas kernels  35.1 us (20%)
  blocking collectives  20.5 us (11%)
  other arithmetic  17.6 us (10%)
  matrix products  15.8 us (9%)
  between operations  15.7 us (9%)
  starting transfers between devices  15.1 us (8%)
  local copies, waits for them, and re-layouts  9.74 us (5%)
    pallas_call x1, Pallas kernels, flash_attention(): pl.pallas_call(attention_kernel, grid_spec=grid_spec, out_shape=jax.Shape...  35.1 us
    all_to_all x1, waiting for transfers between devices, shards(): lax.all_to_all(payload, 'ctx', 0, 0, tiled=True)  27.8 us
    all_to_all x1, waiting for transfers between devices, shards(): lax.all_to_all(incoming_mine.reshape(ctx_count * owned, HEAD_DIM, STATE),...  22.8 us
    psum x1, blocking collectives, shards(): square_sum = lax.psum(square_local, 'head')  20.5 us
    gather x1, other arithmetic, shards(): row_low = doc_starts[own_docs]  9.95 us
    all_to_all x1, starting transfers between devices, shards(): lax.all_to_all(incoming_mine.reshape(ctx_count * owned, HEAD_DIM, STATE),...  7.68 us
    all_to_all x1, starting transfers between devices, shards(): lax.all_to_all(payload, 'ctx', 0, 0, tiled=True)  7.41 us
    dot_general x1, matrix products, shards(): jnp.einsum('tgf,gfo->tgo', mixer_out.reshape(tok_rows, groups_dev, -1), q...  3.8 us
  transfers between devices with their start and end apart: 3, of which 2 were waited for; matrix products, arithmetic and copies ran while one was open for 12% of the time, Pallas kernels for 0%

profile of v6, /device:TPU:28, one launch (start us, length us, event | category | flops | bytes accessed | tf_op | source)
XLA Modules:
  0.0 180.2 jit_solution(4682409101827869315)
XLA Ops:
  7.2 0.0 copy-start
  7.2 0.8 copy.37
  8.0 0.1 reduce.3
  8.1 1.3 fusion.40
  9.4 0.7 fusion.44
  10.1 0.1 convert_reduce_fusion
  10.2 9.9 %bitcast_select_fusion.10 = (s32[128]{0:T(128)S(1)}, s32[128]{0:T(128)S(1)}) fusion(s32[128]{0:T(128)S(1)} %convert_reduce_fusion, s32[]{:T(128)} %bitcast.51, s32[]{:T(128)} %bitcast.52, s32[]{:T(128)} %bitcast.53, s32[]{:T(128)} %bitcast.54, s32[]{:T(128)} %bitcast.55, s32[]{:T(128)} %bitcast.57, s32[]{:T(128)} %bitcast.56, s32[]{:T(128)} %bitcast.34, ...), kind=kLoop, calls=%fused_computation.65 | loop fusion | flops 4352 | bytes 1600 | tf_op jit(solution)/shard_map/gather | solution.py:189
  20.2 0.6 slice.20
  21.4 0.8 fusion.36
  22.3 0.2 slice_reduce_fusion.1
  22.5 1.3 copy.38
  23.8 0.7 compare_convert_fusion.2
  24.4 0.6 slice.21
  25.7 0.8 multiply_bitcast_fusion
  26.5 0.1 bitcast_multiply_fusion
  26.6 0.0 copy-done
  26.6 1.0 fusion.33
  27.6 0.1 broadcast_in_dim.37
  27.7 1.6 pad_maximum_fusion
  29.2 0.0 copy-start.4
  29.2 0.0 copy-start.5
  29.2 7.4 %all-to-all-start = ((f32[32,72,256]{2,1,0:T(8,128)}), f32[32,72,256]{2,1,0:T(8,128)S(1)}, u32[]{:S(2)}, u32[]{:S(2)}) async-start(f32[32,72,256]{2,1,0:T(8,128)} %pad_maximum_fusion), calls=%async_computation | async-start | bytes 4718592 | tf_op jit(solution)/shard_map/all_to_all | solution.py:131
  36.7 0.0 all-gather.2.cloned.1.call-start
  36.7 0.0 copy-done.4
  36.7 0.0 copy-done.5
  36.7 0.6 pad_maximum_fusion.1
  37.4 0.0 all-gather.2.cloned.1.call-update
  37.4 27.8 %all-to-all-done = f32[32,72,256]{2,1,0:T(8,128)S(1)} async-done(((f32[32,72,256]{2,1,0:T(8,128)}), f32[32,72,256]{2,1,0:T(8,128)S(1)}, u32[]{:S(2)}, u32[]{:S(2)}) %all-to-all-start) | async-done | bytes 2359328 | tf_op jit(solution)/shard_map/all_to_all | solution.py:131
  65.3 0.2 slice_bitcast_fusion
  65.5 0.3 slice_reduce_fusion
  65.8 0.2 select_reduce_fusion
  66.0 3.2 %fusion.10 = f32[32,64,256]{2,0,1:T(8,128)S(1)} fusion(f32[32,64,256]{2,1,0:T(8,128)S(1)} %slice_bitcast_fusion, f32[32,32]{1,0:T(8,128)S(1)} %select_reduce_fusion), kind=kOutput, calls=%fused_computation.12 | convolution fusion | flops 201328640 | bytes 4198400 | tf_op jit(solution)/shard_map/kcd,dkpn->ckpn/dot_general | solution.py:145
  69.3 2.5 %copy.41 = f32[32,64,256]{2,1,0:T(8,128)} copy(f32[32,64,256]{2,0,1:T(8,128)S(1)} %fusion.10) | data formatting | bytes 4194304 | tf_op jit(solution)/shard_map/reshape | solution.py:147
  71.8 0.0 copy-start.3
  71.8 0.0 copy-start.6
  71.8 7.7 %all-to-all-start.1 = ((f32[32,64,256]{2,1,0:T(8,128)}), f32[32,64,256]{2,1,0:T(8,128)S(1)}, u32[]{:S(2)}, u32[]{:S(2)}) async-start(f32[32,64,256]{2,1,0:T(8,128)} %copy.41), calls=%async_computation.1 | async-start | bytes 4194304 | tf_op jit(solution)/shard_map/all_to_all | solution.py:146
  79.6 0.7 copy.43.low_ref
  80.4 0.6 pad_add_fusion.chunk_ref
  81.0 0.0 copy-start.8
  81.0 0.6 iota_add_fusion.high_ref
  81.6 0.1 fusion.35
  81.7 0.0 copy-done.3
  81.7 0.1 fusion.45
  81.9 0.0 copy-done.6
  81.9 3.5 %fusion.13 = f32[128,1,32,64]{0,3,2,1:T(8,128)} fusion(bf16[128,32,64]{0,2,1:T(8,128)(2,1)S(1)} %bitcast.148, f32[32,128]{1,0:T(8,128)S(1)} %copy-done.6, f32[32,128]{1,0:T(8,128)S(1)} %bitcast.154, f32[128,128]{1,0:T(8,128)S(1)} %fusion.45, pred[128,128]{1,0:T(8,128)(4,1)S(1)} %fusion.35), kind=kOutput, calls=%fused_computation.13 | convolution fusion | flops 404750336 | bytes 1687552 | tf_op jit(solution)/shard_map/gjts,sgjp->tgjp/dot_general | solution.py:156
  85.4 22.8 %all-to-all-done.1 = f32[32,64,256]{2,1,0:T(8,128)S(1)} async-done(((f32[32,64,256]{2,1,0:T(8,128)}), f32[32,64,256]{2,1,0:T(8,128)S(1)}, u32[]{:S(2)}, u32[]{:S(2)}) %all-to-all-start.1) | async-done | bytes 2097184 | tf_op jit(solution)/shard_map/all_to_all | solution.py:146
  108.2 0.0 copy-done.8
  108.2 3.3 %fusion.18 = f32[128,1,32,64]{0,3,2,1:T(8,128)} fusion(f32[128,1,32,64]{0,3,2,1:T(8,128)} %fusion.13, f32[32,64,256]{2,1,0:T(8,128)S(1)} %all-to-all-done.1, f32[32]{0:T(128)S(1)} %copy-done.8, f32[128,32]{0,1:T(8,128)S(1)} %get-tuple-element.4, bf16[128,256]{1,0:T(8,128)(2,1)S(1)} %copy-done.3, bf16[128,1,32,64]{0,3,2,1:T(8,128)(2,1)S(1)} %bitcast.149), kind=kOutput, calls=%fused_computation.17 | convolution fusion | flops 806617088 | bytes 4800640 | tf_op jit(solution)/shard_map/tgn,gjpn->tgjp/dot_general | solution.py:159
  111.5 0.0 copy-start.2
  111.5 0.0 copy-start.7
  111.5 1.6 copy.42
  113.1 0.0 copy-done.2
  113.1 0.4 multiply_reduce_fusion
  113.5 20.5 %psum.7 = f32[128]{0:T(128)S(1)} all-reduce(f32[128]{0:T(128)S(1)} %multiply_reduce_fusion), channel_id=1, replica_groups=mesh['ctx'=32,'head'=8] {'head'}, use_global_device_ids=true, to_apply=%region_5.6 | all-reduce | flops 128 | bytes 1024 | tf_op jit(solution)/shard_map/psum | solution.py:166
  134.1 0.0 copy-done.7
  134.1 0.4 multiply_convert_fusion
  134.5 0.0 copy-start.1
  134.5 3.8 %fusion.19.query_ref = bf16[128,1024]{1,0:T(8,128)(2,1)} fusion(bf16[128,2048]{1,0:T(8,128)(2,1)S(1)} %multiply_convert_fusion, bf16[1,2048,1024]{2,1,0:T(8,128)(2,1)} %param.20), kind=kOutput, calls=%fused_computation.20 | convolution fusion | flops 537001984 | bytes 4980736 | tf_op jit(solution)/shard_map/tgf,gfo->tgo/dot_general | solution.py:172
  138.3 0.0 copy-done.1
  138.3 0.0 all-gather.2.cloned.1.call-done
  138.3 35.1 %shard_map.131 = bf16[128,1024]{1,0:T(8,128)(2,1)} custom-call(s32[2]{0:T(128)} %pad_add_fusion.chunk_ref, bf16[128,1024]{1,0:T(8,128)(2,1)} %fusion.19.query_ref, bf16[4096,256]{1,0:T(8,128)(2,1)} %bitcast.152, s32[128,1]{1,0:T(8,128)} %copy.43.low_ref, s32[128,1]{1,0:T(8,128)} %iota_add_fusion.high_ref), custom_call_target="tpu_custom_call" | custom-call | tf_op jit(solution)/shard_map/pallas_call | solution.py:78
  (5 shorter events, 0.1 us)
Async XLA Ops:
  7.2 19.4 %copy-start = (bf16[128,256]{1,0:T(8,128)(2,1)S(1)}, bf16[128,256]{1,0:T(8,128)(2,1)}, u32[]{:S(2)}) copy-start(bf16[128,256]{1,0:T(8,128)(2,1)} %param.14) | copy-start | bytes 196612
  29.2 7.5 %copy-start.4 = (bf16[128,128]{1,0:T(8,128)(2,1)S(1)}, bf16[128,128]{1,0:T(8,128)(2,1)}, u32[]{:S(2)}) copy-start(bf16[128,128]{1,0:T(8,128)(2,1)} %param.22) | copy-start | bytes 98308
  29.2 7.5 %copy-start.5 = (bf16[128,128]{1,0:T(8,128)(2,1)S(1)}, bf16[128,128]{1,0:T(8,128)(2,1)}, u32[]{:S(2)}) copy-start(bf16[128,128]{1,0:T(8,128)(2,1)} %param.21) | copy-start | bytes 98308
  29.2 36.0 %all-to-all-start = ((f32[32,72,256]{2,1,0:T(8,128)}), f32[32,72,256]{2,1,0:T(8,128)S(1)}, u32[]{:S(2)}, u32[]{:S(2)}) async-start(f32[32,72,256]{2,1,0:T(8,128)} %pad_maximum_fusion), calls=%async_computation | async-start | bytes 4718592 | tf_op jit(solution)/shard_map/all_to_all | solution.py:131
  36.7 101.6 %all-gather.2.cloned.1.call-start = ((), (), s32[]{:S(2)}) async-start(), calls=%async_computation.2 | async-start | bytes 2162688 | tf_op jit(solution)/shard_map/all_gather | solution.py:187
  71.8 10.0 %copy-start.3 = (bf16[128,256]{1,0:T(8,128)(2,1)S(1)}, bf16[128,256]{1,0:T(8,128)(2,1)}, u32[]{:S(2)}) copy-start(bf16[128,256]{1,0:T(8,128)(2,1)} %param.15) | copy-start | bytes 196612
  71.8 10.1 %copy-start.6 = (f32[32,128]{1,0:T(8,128)S(1)}, f32[32,128]{1,0:T(8,128)}, u32[]{:S(2)}) copy-start(f32[32,128]{1,0:T(8,128)} %param.16) | copy-start | bytes 49156
  71.8 36.4 %all-to-all-start.1 = ((f32[32,64,256]{2,1,0:T(8,128)}), f32[32,64,256]{2,1,0:T(8,128)S(1)}, u32[]{:S(2)}, u32[]{:S(2)}) async-start(f32[32,64,256]{2,1,0:T(8,128)} %copy.41), calls=%async_computation.1 | async-start | bytes 4194304 | tf_op jit(solution)/shard_map/all_to_all | solution.py:146
  81.0 27.2 %copy-start.8 = (f32[32]{0:T(128)S(1)}, f32[32]{0:T(128)}, u32[]{:S(2)}) copy-start(f32[32]{0:T(128)} %param.18) | copy-start | bytes 388
  111.5 1.6 copy-start.2
  111.5 22.6 %copy-start.7 = (f32[2048]{0:T(1024)S(1)}, f32[2048]{0:T(1024)}, u32[]{:S(2)}) copy-start(f32[2048]{0:T(1024)} %param.19) | copy-start | bytes 24580
  134.5 3.8 %copy-start.1 = (bf16[128,2048]{1,0:T(8,128)(2,1)}, bf16[128,2048]{1,0:T(8,128)(2,1)S(1)}, u32[]{:S(2)}) copy-start(bf16[128,2048]{1,0:T(8,128)(2,1)S(1)} %multiply_convert_fusion) | copy-start | bytes 1572868
Sparse Core Ops, SparseCore 0:
  40.6 69.3 all-gather.1

commit v7 on v6

--- a/solution.py
+++ b/solution.py
@@ -61,24 +61,23 @@
 
 
 def flash_attention(query_flat, kv_rows, low, high, first_chunk, chunk_count):
-    rows, width = query_flat.shape
-    heads = width // ATT_DIM
+    rows = query_flat.shape[0]
     chunk_info = jnp.stack([first_chunk, chunk_count]).astype(jnp.int32)
     grid_spec = pltpu.PrefetchScalarGridSpec(
         num_scalar_prefetch=1,
-        grid=(heads,),
+        grid=(1,),
         in_specs=[
-            pl.BlockSpec((rows, ATT_DIM), lambda i, info: (0, i)),
+            pl.BlockSpec(query_flat.shape, lambda i, info: (0, 0)),
             pl.BlockSpec(kv_rows.shape, lambda i, info: (0, 0)),
             pl.BlockSpec((rows, 1), lambda i, info: (0, 0)),
             pl.BlockSpec((rows, 1), lambda i, info: (0, 0)),
         ],
-        out_specs=pl.BlockSpec((rows, ATT_DIM), lambda i, info: (0, i)),
+        out_specs=pl.BlockSpec(query_flat.shape, lambda i, info: (0, 0)),
     )
     return pl.pallas_call(
         attention_kernel,
         grid_spec=grid_spec,
-        out_shape=jax.ShapeDtypeStruct((rows, width), jnp.bfloat16),
+        out_shape=jax.ShapeDtypeStruct(query_flat.shape, jnp.bfloat16),
     )(chunk_info, query_flat, kv_rows, low, high)
 
 
@@ -186,22 +185,28 @@
     )
     kv_all = lax.all_gather(kv_local, "ctx", axis=0, tiled=True)
     doc_starts = jnp.cumsum(doc_lengths) - doc_lengths
-    row_low = doc_starts[own_docs]
+    row_low = jnp.max(
+        jnp.where(doc_starts[None, :] <= own_pos[:, None], doc_starts[None, :], 0), axis=1
+    )
     first_chunk = row_low[0] // KEY_CHUNK
     last_chunk = (first_pos + tok_rows - 1) // KEY_CHUNK
+    stacked_low = jnp.tile(row_low, query_group)[:, None]
+    stacked_high = jnp.tile(own_pos, query_group)[:, None]
     group_outs = []
     for group in range(groups_dev):
+        stacked_query = jnp.transpose(query[:, group], (1, 0, 2)).reshape(-1, ATT_DIM)
+        stacked_out = flash_attention(
+            stacked_query,
+            kv_all[:, group],
+            stacked_low,
+            stacked_high,
+            first_chunk,
+            last_chunk - first_chunk + 1,
+        )
         group_outs.append(
-            flash_attention(
-                query[:, group].reshape(tok_rows, query_group * ATT_DIM),
-                kv_all[:, group],
-                row_low[:, None],
-                own_pos[:, None],
-                first_chunk,
-                last_chunk - first_chunk + 1,
-            )
+            jnp.transpose(stacked_out.reshape(query_group, tok_rows, ATT_DIM), (1, 0, 2))
         )
-    attn_out = jnp.concatenate(group_outs, axis=1)
+    attn_out = jnp.stack(group_outs, axis=1).reshape(tok_rows, -1)
     return (mixer_out, attn_out)
 
 

time: 180 us -> 154 us (0.86)
  the two profiles are of different devices: /device:TPU:28 before, /device:TPU:6 now
where the time goes in v7:
time: 154 us
  waiting for transfers between devices  50.8 us (33%)
  blocking collectives  21.1 us (14%)
  Pallas kernels  16.6 us (11%)
  between operations  15.7 us (10%)
  starting transfers between devices  15.2 us (10%)
  matrix products  15.1 us (10%)
  local copies, waits for them, and re-layouts  12.9 us (8%)
  other arithmetic  6.96 us (5%)
    all_to_all x1, waiting for transfers between devices, shards(): lax.all_to_all(payload, 'ctx', 0, 0, tiled=True)  28.1 us
    all_to_all x1, waiting for transfers between devices, shards(): lax.all_to_all(incoming_mine.reshape(ctx_count * owned, HEAD_DIM, STATE),...  22.6 us
    psum x1, blocking collectives, shards(): square_sum = lax.psum(square_local, 'head')  21.1 us
    pallas_call x1, Pallas kernels, flash_attention(): pl.pallas_call(attention_kernel, grid_spec=grid_spec, out_shape=jax.Shape...  16.6 us
    all_to_all x1, starting transfers between devices, shards(): lax.all_to_all(payload, 'ctx', 0, 0, tiled=True)  7.74 us
    all_to_all x1, starting transfers between devices, shards(): lax.all_to_all(incoming_mine.reshape(ctx_count * owned, HEAD_DIM, STATE),...  7.46 us
    dot_general x1, matrix products, shards(): jnp.einsum('gjts,sgjp->tgjp', mixing, input_f32, precision=highest)  3.53 us
    dot_general x1, matrix products, shards(): jnp.einsum('tgn,gjpn->tgjp', state_out.astype(jnp.float32), incoming, pre...  3.31 us
  transfers between devices with their start and end apart: 3, of which 2 were waited for; matrix products, arithmetic and copies ran while one was open for 15% of the time, Pallas kernels for 0%

profile of v7, /device:TPU:6, one launch (start us, length us, event | category | flops | bytes accessed | tf_op | source)
XLA Modules:
  0.0 154.4 jit_solution(3648852558390957351)
XLA Ops:
  7.2 0.0 copy-start
  7.2 0.8 copy.44
  8.0 0.1 reduce.3
  8.1 1.3 fusion.45
  9.4 0.1 fusion.43
  9.5 0.6 slice.20
  10.7 0.8 fusion.39
  11.6 0.2 slice_reduce_fusion.1
  11.8 1.3 copy.45
  13.1 0.7 compare_convert_fusion.3
  13.8 0.6 slice.21
  15.0 0.8 multiply_bitcast_fusion
  15.8 0.1 bitcast_multiply_fusion
  15.9 0.0 copy-done
  15.9 1.0 fusion.36
  16.9 0.1 broadcast_in_dim.45
  17.0 1.6 %pad_maximum_fusion = f32[32,72,256]{2,1,0:T(8,128)} fusion(f32[32,8,256]{2,1,0:T(8,128)S(1)} %broadcast_in_dim.45, f32[32,64,256]{2,1,0:T(8,128)S(1)} %fusion.36), kind=kLoop, calls=%fused_computation.2 | loop fusion | flops 589824 | bytes 4718592 | tf_op jit(solution)/shard_map/concatenate | solution.py:129
  18.6 0.0 copy-start.4
  18.6 0.0 copy-start.5
  18.6 7.7 %all-to-all-start = ((f32[32,72,256]{2,1,0:T(8,128)}), f32[32,72,256]{2,1,0:T(8,128)S(1)}, u32[]{:S(2)}, u32[]{:S(2)}) async-start(f32[32,72,256]{2,1,0:T(8,128)} %pad_maximum_fusion), calls=%async_computation | async-start | bytes 4718592 | tf_op jit(solution)/shard_map/all_to_all | solution.py:130
  26.3 0.0 all-gather.2.cloned.1.call-start
  26.4 0.0 copy-done.4
  26.4 0.0 copy-done.5
  26.4 0.6 pad_maximum_fusion.1
  27.0 0.0 all-gather.2.cloned.1.call-update
  27.1 28.1 %all-to-all-done = f32[32,72,256]{2,1,0:T(8,128)S(1)} async-done(((f32[32,72,256]{2,1,0:T(8,128)}), f32[32,72,256]{2,1,0:T(8,128)S(1)}, u32[]{:S(2)}, u32[]{:S(2)}) %all-to-all-start) | async-done | bytes 2359328 | tf_op jit(solution)/shard_map/all_to_all | solution.py:130
  55.2 0.3 slice_reduce_fusion
  55.5 0.2 slice_bitcast_fusion
  55.8 0.2 select_reduce_fusion
  56.0 3.2 %fusion.10 = f32[32,64,256]{2,0,1:T(8,128)S(1)} fusion(f32[32,64,256]{2,1,0:T(8,128)S(1)} %slice_bitcast_fusion, f32[32,32]{1,0:T(8,128)S(1)} %select_reduce_fusion), kind=kOutput, calls=%fused_computation.12 | convolution fusion | flops 201328640 | bytes 4198400 | tf_op jit(solution)/shard_map/kcd,dkpn->ckpn/dot_general | solution.py:144
  59.2 2.6 %copy.48 = f32[32,64,256]{2,1,0:T(8,128)} copy(f32[32,64,256]{2,0,1:T(8,128)S(1)} %fusion.10) | data formatting | bytes 4194304 | tf_op jit(solution)/shard_map/reshape | solution.py:146
  61.8 0.0 copy-start.3
  61.8 0.0 copy-start.6
  61.8 7.5 %all-to-all-start.1 = ((f32[32,64,256]{2,1,0:T(8,128)}), f32[32,64,256]{2,1,0:T(8,128)S(1)}, u32[]{:S(2)}, u32[]{:S(2)}) async-start(f32[32,64,256]{2,1,0:T(8,128)} %copy.48), calls=%async_computation.1 | async-start | bytes 4194304 | tf_op jit(solution)/shard_map/all_to_all | solution.py:145
  69.4 1.0 copy.51.low_ref
  70.5 1.0 copy.52.high_ref
  71.5 0.0 copy-start.8
  71.5 0.6 pad_add_fusion.chunk_ref
  72.1 0.1 fusion.38
  72.1 0.0 copy-done.3
  72.2 0.1 fusion.48
  72.3 0.0 copy-done.6
  72.3 3.5 %fusion.13 = f32[128,1,32,64]{0,3,2,1:T(8,128)} fusion(bf16[128,32,64]{0,2,1:T(8,128)(2,1)S(1)} %bitcast.113, f32[32,128]{1,0:T(8,128)S(1)} %copy-done.6, f32[32,128]{1,0:T(8,128)S(1)} %bitcast.123, f32[128,128]{1,0:T(8,128)S(1)} %fusion.48, pred[128,128]{1,0:T(8,128)(4,1)S(1)} %fusion.38), kind=kOutput, calls=%fused_computation.13 | convolution fusion | flops 404750336 | bytes 1687552 | tf_op jit(solution)/shard_map/gjts,sgjp->tgjp/dot_general | solution.py:155
  75.9 22.6 %all-to-all-done.1 = f32[32,64,256]{2,1,0:T(8,128)S(1)} async-done(((f32[32,64,256]{2,1,0:T(8,128)}), f32[32,64,256]{2,1,0:T(8,128)S(1)}, u32[]{:S(2)}, u32[]{:S(2)}) %all-to-all-start.1) | async-done | bytes 2097184 | tf_op jit(solution)/shard_map/all_to_all | solution.py:145
  98.5 0.0 copy-done.8
  98.5 3.3 %fusion.18 = f32[128,1,32,64]{0,3,2,1:T(8,128)} fusion(f32[128,1,32,64]{0,3,2,1:T(8,128)} %fusion.13, f32[32,64,256]{2,1,0:T(8,128)S(1)} %all-to-all-done.1, f32[32]{0:T(128)S(1)} %copy-done.8, f32[128,32]{0,1:T(8,128)S(1)} %get-tuple-element.6, bf16[128,256]{1,0:T(8,128)(2,1)S(1)} %copy-done.3, bf16[128,1,32,64]{0,3,2,1:T(8,128)(2,1)S(1)} %bitcast.114), kind=kOutput, calls=%fused_computation.17 | convolution fusion | flops 806617088 | bytes 4800640 | tf_op jit(solution)/shard_map/tgn,gjpn->tgjp/dot_general | solution.py:158
  101.8 0.0 copy-start.2
  101.8 0.0 copy-start.7
  101.8 1.6 %copy.49 = f32[128,2048]{1,0:T(8,128)S(1)} copy(f32[128,2048]{0,1:T(8,128)} %bitcast.115) | data formatting | bytes 2097152 | tf_op jit(solution)/shard_map/reshape | solution.py:162
  103.4 0.0 copy-done.2
  103.4 0.4 multiply_reduce_fusion
  103.8 21.1 %psum.7 = f32[128]{0:T(128)S(1)} all-reduce(f32[128]{0:T(128)S(1)} %multiply_reduce_fusion), channel_id=1, replica_groups=mesh['ctx'=32,'head'=8] {'head'}, use_global_device_ids=true, to_apply=%region_5.6 | all-reduce | flops 128 | bytes 1024 | tf_op jit(solution)/shard_map/psum | solution.py:165
  124.9 0.0 copy-done.7
  124.9 0.4 multiply_convert_fusion
  125.3 0.0 copy-start.1
  125.3 3.1 %fusion.22 = bf16[16,8,8,128]{3,1,2,0:T(8,128)(2,1)S(1)} fusion(bf16[128,2048]{1,0:T(8,128)(2,1)S(1)} %multiply_convert_fusion, bf16[1,2048,1024]{2,1,0:T(8,128)(2,1)} %param.20), kind=kOutput, calls=%fused_computation.21 | convolution fusion | flops 537001984 | bytes 4980736 | tf_op jit(solution)/shard_map/tgf,gfo->tgo/dot_general | solution.py:171
  128.5 0.0 copy-done.1
  128.5 0.7 copy.50
  129.3 0.0 all-gather.2.cloned.1.call-done
  129.3 16.6 %shard_map.131 = bf16[1024,128]{1,0:T(8,128)(2,1)} custom-call(s32[2]{0:T(128)} %pad_add_fusion.chunk_ref, bf16[1024,128]{1,0:T(8,128)(2,1)} %bitcast.119, bf16[4096,256]{1,0:T(8,128)(2,1)} %bitcast.117, s32[1024,1]{1,0:T(8,128)} %copy.51.low_ref, s32[1024,1]{1,0:T(8,128)} %copy.52.high_ref), custom_call_target="tpu_custom_call" | custom-call | tf_op jit(solution)/shard_map/pallas_call | solution.py:77
  145.9 1.7 %copy.61 = bf16[8,16,8,128]{3,2,0,1:T(8,128)(2,1)} copy(bf16[8,16,8,128]{3,2,1,0:T(8,128)(2,1)} %bitcast.120) | data formatting | bytes 524288 | tf_op jit(solution)/shard_map/reshape;stack | solution.py:209
  (9 shorter events, 0.1 us)
Async XLA Ops:
  7.2 8.8 %copy-start = (bf16[128,256]{1,0:T(8,128)(2,1)S(1)}, bf16[128,256]{1,0:T(8,128)(2,1)}, u32[]{:S(2)}) copy-start(bf16[128,256]{1,0:T(8,128)(2,1)} %param.14) | copy-start | bytes 196612
  18.6 7.8 %copy-start.4 = (bf16[128,128]{1,0:T(8,128)(2,1)S(1)}, bf16[128,128]{1,0:T(8,128)(2,1)}, u32[]{:S(2)}) copy-start(bf16[128,128]{1,0:T(8,128)(2,1)} %param.22) | copy-start | bytes 98308
  18.6 7.8 %copy-start.5 = (bf16[128,128]{1,0:T(8,128)(2,1)S(1)}, bf16[128,128]{1,0:T(8,128)(2,1)}, u32[]{:S(2)}) copy-start(bf16[128,128]{1,0:T(8,128)(2,1)} %param.21) | copy-start | bytes 98308
  18.6 36.6 %all-to-all-start = ((f32[32,72,256]{2,1,0:T(8,128)}), f32[32,72,256]{2,1,0:T(8,128)S(1)}, u32[]{:S(2)}, u32[]{:S(2)}) async-start(f32[32,72,256]{2,1,0:T(8,128)} %pad_maximum_fusion), calls=%async_computation | async-start | bytes 4718592 | tf_op jit(solution)/shard_map/all_to_all | solution.py:130
  26.3 102.9 %all-gather.2.cloned.1.call-start = ((), (), s32[]{:S(2)}) async-start(), calls=%async_computation.2 | async-start | bytes 2162688 | tf_op jit(solution)/shard_map/all_gather | solution.py:186
  61.8 10.4 %copy-start.3 = (bf16[128,256]{1,0:T(8,128)(2,1)S(1)}, bf16[128,256]{1,0:T(8,128)(2,1)}, u32[]{:S(2)}) copy-start(bf16[128,256]{1,0:T(8,128)(2,1)} %param.15) | copy-start | bytes 196612
  61.8 10.5 %copy-start.6 = (f32[32,128]{1,0:T(8,128)S(1)}, f32[32,128]{1,0:T(8,128)}, u32[]{:S(2)}) copy-start(f32[32,128]{1,0:T(8,128)} %param.16) | copy-start | bytes 49156
  61.8 36.7 %all-to-all-start.1 = ((f32[32,64,256]{2,1,0:T(8,128)}), f32[32,64,256]{2,1,0:T(8,128)S(1)}, u32[]{:S(2)}, u32[]{:S(2)}) async-start(f32[32,64,256]{2,1,0:T(8,128)} %copy.48), calls=%async_computation.1 | async-start | bytes 4194304 | tf_op jit(solution)/shard_map/all_to_all | solution.py:145
  71.5 27.0 %copy-start.8 = (f32[32]{0:T(128)S(1)}, f32[32]{0:T(128)}, u32[]{:S(2)}) copy-start(f32[32]{0:T(128)} %param.18) | copy-start | bytes 388
  101.8 1.6 %copy-start.2 = (bf16[128,2048]{1,0:T(8,128)(2,1)S(1)}, bf16[128,2048]{1,0:T(8,128)(2,1)}, u32[]{:S(2)}) copy-start(bf16[128,2048]{1,0:T(8,128)(2,1)} %param.13) | copy-start | bytes 1572868
  101.8 23.1 %copy-start.7 = (f32[2048]{0:T(1024)S(1)}, f32[2048]{0:T(1024)}, u32[]{:S(2)}) copy-start(f32[2048]{0:T(1024)} %param.19) | copy-start | bytes 24580
  125.3 3.2 %copy-start.1 = (bf16[128,2048]{1,0:T(8,128)(2,1)}, bf16[128,2048]{1,0:T(8,128)(2,1)S(1)}, u32[]{:S(2)}) copy-start(bf16[128,2048]{1,0:T(8,128)(2,1)S(1)} %multiply_convert_fusion) | copy-start | bytes 1572868
Sparse Core Ops, SparseCore 0:
  29.7 71.6 all-gather.1

commit v8 on v6

--- a/solution.py
+++ b/solution.py
@@ -25,10 +25,14 @@
 
 
 def attention_kernel(chunk_ref, query_ref, kv_ref, low_ref, high_ref, out_ref):
-    rows = query_ref.shape[0]
-    query_rows = query_ref[...]
-    low = low_ref[...]
-    high = high_ref[...]
+    tokens = query_ref.shape[0]
+    heads = query_ref.shape[1] // ATT_DIM
+    rows = tokens * heads
+    query_rows = jnp.concatenate(
+        [query_ref[:, head * ATT_DIM : (head + 1) * ATT_DIM] for head in range(heads)], axis=0
+    )
+    low = jnp.concatenate([low_ref[...]] * heads, axis=0)
+    high = jnp.concatenate([high_ref[...]] * heads, axis=0)
 
     def chunk_turn(turn, carried):
         best_old, total_old, accum_old = carried
@@ -41,9 +45,9 @@
         ) * ATT_DIM ** (-0.5)
         key_pos = start + lax.broadcasted_iota(jnp.int32, (rows, KEY_CHUNK), 1)
         visible = (key_pos >= low) & (key_pos <= high)
-        scores = jnp.where(visible, scores, NEG_FILL)
+        scores = jnp.where(visible, scores, -jnp.inf)
         best_new = jnp.maximum(best_old, jnp.max(scores, axis=1, keepdims=True))
-        weights = jnp.where(visible, jnp.exp(scores - best_new), 0.0)
+        weights = jnp.exp(scores - best_new)
         rescale = jnp.exp(best_old - best_new)
         total_new = total_old * rescale + jnp.sum(weights, axis=1, keepdims=True)
         accum_new = accum_old * rescale + jnp.dot(
@@ -57,30 +61,32 @@
         jnp.zeros((rows, ATT_DIM), jnp.float32),
     )
     _, total, accum = lax.fori_loop(0, chunk_ref[1], chunk_turn, initial)
-    out_ref[...] = (accum / total).astype(out_ref.dtype)
-
-
-def flash_attention(query_flat, kv_rows, low, high, first_chunk, chunk_count):
-    rows, width = query_flat.shape
-    heads = width // ATT_DIM
+    result = (accum / total).astype(out_ref.dtype)
+    for head in range(heads):
+        out_ref[:, head * ATT_DIM : (head + 1) * ATT_DIM] = result[
+            head * tokens : (head + 1) * tokens
+        ]
+
+
+def flash_attention(query_rows, kv_rows, low, high, first_chunk, chunk_count):
+    tokens = query_rows.shape[0]
     chunk_info = jnp.stack([first_chunk, chunk_count]).astype(jnp.int32)
     grid_spec = pltpu.PrefetchScalarGridSpec(
         num_scalar_prefetch=1,
-        grid=(heads,),
+        grid=(1,),
         in_specs=[
-            pl.BlockSpec((rows, ATT_DIM), lambda i, info: (0, i)),
+            pl.BlockSpec(query_rows.shape, lambda i, info: (0, 0)),
             pl.BlockSpec(kv_rows.shape, lambda i, info: (0, 0)),
-            pl.BlockSpec((rows, 1), lambda i, info: (0, 0)),
-            pl.BlockSpec((rows, 1), lambda i, info: (0, 0)),
+            pl.BlockSpec((tokens, 1), lambda i, info: (0, 0)),
+            pl.BlockSpec((tokens, 1), lambda i, info: (0, 0)),
         ],
-        out_specs=pl.BlockSpec((rows, ATT_DIM), lambda i, info: (0, i)),
+        out_specs=pl.BlockSpec(query_rows.shape, lambda i, info: (0, 0)),
     )
     return pl.pallas_call(
         attention_kernel,
         grid_spec=grid_spec,
-        out_shape=jax.ShapeDtypeStruct((rows, width), jnp.bfloat16),
-    )(chunk_info, query_flat, kv_rows, low, high)
-
+        out_shape=jax.ShapeDtypeStruct(query_rows.shape, jnp.bfloat16),
+    )(chunk_info, query_rows, kv_rows, low, high)
 
 def shards(
     mixer_input,
@@ -186,7 +192,9 @@
     )
     kv_all = lax.all_gather(kv_local, "ctx", axis=0, tiled=True)
     doc_starts = jnp.cumsum(doc_lengths) - doc_lengths
-    row_low = doc_starts[own_docs]
+    row_low = jnp.max(
+        jnp.where(doc_starts[None, :] <= own_pos[:, None], doc_starts[None, :], 0), axis=1
+    )
     first_chunk = row_low[0] // KEY_CHUNK
     last_chunk = (first_pos + tok_rows - 1) // KEY_CHUNK
     group_outs = []

time: 180 us -> 147 us (0.82)
  the two profiles are of different devices: /device:TPU:28 before, /device:TPU:4 now
where the time goes in v8:
time: 147 us; the launch traced here: 146 us
  waiting for transfers between devices  51.4 us (35%)
  blocking collectives  21.1 us (14%)
  matrix products  15.8 us (11%)
  between operations  15.7 us (11%)
  starting transfers between devices  14.9 us (10%)
  Pallas kernels  10.3 us (7%)
  local copies, waits for them, and re-layouts  9.03 us (6%)
  other arithmetic  7.69 us (5%)
    all_to_all x1, waiting for transfers between devices, shards(): lax.all_to_all(payload, 'ctx', 0, 0, tiled=True)  28.4 us
    all_to_all x1, waiting for transfers between devices, shards(): lax.all_to_all(incoming_mine.reshape(ctx_count * owned, HEAD_DIM, STATE),...  23 us
    psum x1, blocking collectives, shards(): square_sum = lax.psum(square_local, 'head')  21.1 us
    pallas_call x1, Pallas kernels, flash_attention(): pl.pallas_call(attention_kernel, grid_spec=grid_spec, out_shape=jax.Shape...  10.3 us
    all_to_all x1, starting transfers between devices, shards(): lax.all_to_all(payload, 'ctx', 0, 0, tiled=True)  7.73 us
    all_to_all x1, starting transfers between devices, shards(): lax.all_to_all(incoming_mine.reshape(ctx_count * owned, HEAD_DIM, STATE),...  7.15 us
    dot_general x1, matrix products, shards(): jnp.einsum('tgf,gfo->tgo', mixer_out.reshape(tok_rows, groups_dev, -1), q...  3.8 us
    dot_general x1, matrix products, shards(): jnp.einsum('gjts,sgjp->tgjp', mixing, input_f32, precision=highest)  3.53 us
  transfers between devices with their start and end apart: 3, of which 2 were waited for; matrix products, arithmetic and copies ran while one was open for 15% of the time, Pallas kernels for 0%

profile of v8, /device:TPU:4, one launch (start us, length us, event | category | flops | bytes accessed | tf_op | source)
XLA Modules:
  0.0 145.9 jit_solution(9642773139083416796)
XLA Ops:
  7.2 0.0 copy-start
  7.2 0.8 copy.37
  8.0 0.1 reduce.3
  8.1 1.3 fusion.42
  9.4 0.1 fusion.40
  9.5 0.6 slice.20
  10.7 0.8 fusion.36
  11.6 0.2 slice_reduce_fusion.1
  11.8 1.3 copy.38
  13.1 0.7 compare_convert_fusion.3
  13.8 0.6 slice.21
  15.0 0.8 multiply_bitcast_fusion
  15.8 0.1 bitcast_multiply_fusion
  15.9 0.0 copy-done
  15.9 1.0 fusion.33
  16.9 0.1 broadcast_in_dim.47
  17.0 1.6 %pad_maximum_fusion = f32[32,72,256]{2,1,0:T(8,128)} fusion(f32[32,8,256]{2,1,0:T(8,128)S(1)} %broadcast_in_dim.47, f32[32,64,256]{2,1,0:T(8,128)S(1)} %fusion.33), kind=kLoop, calls=%fused_computation.2 | loop fusion | flops 589824 | bytes 4718592 | tf_op jit(solution)/shard_map/concatenate | solution.py:136
  18.6 0.0 copy-start.4
  18.6 0.0 copy-start.5
  18.6 7.7 %all-to-all-start = ((f32[32,72,256]{2,1,0:T(8,128)}), f32[32,72,256]{2,1,0:T(8,128)S(1)}, u32[]{:S(2)}, u32[]{:S(2)}) async-start(f32[32,72,256]{2,1,0:T(8,128)} %pad_maximum_fusion), calls=%async_computation | async-start | bytes 4718592 | tf_op jit(solution)/shard_map/all_to_all | solution.py:137
  26.3 0.0 all-gather.2.cloned.1.call-start
  26.4 0.0 copy-done.4
  26.4 0.0 copy-done.5
  26.4 0.6 pad_maximum_fusion.1
  27.0 0.0 all-gather.2.cloned.1.call-update
  27.1 28.4 %all-to-all-done = f32[32,72,256]{2,1,0:T(8,128)S(1)} async-done(((f32[32,72,256]{2,1,0:T(8,128)}), f32[32,72,256]{2,1,0:T(8,128)S(1)}, u32[]{:S(2)}, u32[]{:S(2)}) %all-to-all-start) | async-done | bytes 2359328 | tf_op jit(solution)/shard_map/all_to_all | solution.py:137
  55.4 0.3 slice_reduce_fusion
  55.8 0.2 slice_bitcast_fusion
  56.0 0.2 select_reduce_fusion
  56.2 3.2 %fusion.10 = f32[32,64,256]{2,0,1:T(8,128)S(1)} fusion(f32[32,64,256]{2,1,0:T(8,128)S(1)} %slice_bitcast_fusion, f32[32,32]{1,0:T(8,128)S(1)} %select_reduce_fusion), kind=kOutput, calls=%fused_computation.12 | convolution fusion | flops 201328640 | bytes 4198400 | tf_op jit(solution)/shard_map/kcd,dkpn->ckpn/dot_general | solution.py:151
  59.4 2.5 %copy.41 = f32[32,64,256]{2,1,0:T(8,128)} copy(f32[32,64,256]{2,0,1:T(8,128)S(1)} %fusion.10) | data formatting | bytes 4194304 | tf_op jit(solution)/shard_map/reshape | solution.py:153
  62.0 0.0 copy-start.3
  62.0 0.0 copy-start.6
  62.0 7.2 %all-to-all-start.1 = ((f32[32,64,256]{2,1,0:T(8,128)}), f32[32,64,256]{2,1,0:T(8,128)S(1)}, u32[]{:S(2)}, u32[]{:S(2)}) async-start(f32[32,64,256]{2,1,0:T(8,128)} %copy.41), calls=%async_computation.1 | async-start | bytes 4194304 | tf_op jit(solution)/shard_map/all_to_all | solution.py:152
  69.3 0.7 copy.43.low_ref
  70.0 0.6 pad_add_fusion.chunk_ref
  70.7 0.0 copy-start.8
  70.7 0.6 iota_add_fusion.high_ref
  71.3 0.1 fusion.35
  71.4 0.0 copy-done.3
  71.4 0.1 fusion.45
  71.5 0.0 copy-done.6
  71.6 3.5 %fusion.13 = f32[128,1,32,64]{0,3,2,1:T(8,128)} fusion(bf16[128,32,64]{0,2,1:T(8,128)(2,1)S(1)} %bitcast.90, f32[32,128]{1,0:T(8,128)S(1)} %copy-done.6, f32[32,128]{1,0:T(8,128)S(1)} %bitcast.96, f32[128,128]{1,0:T(8,128)S(1)} %fusion.45, pred[128,128]{1,0:T(8,128)(4,1)S(1)} %fusion.35), kind=kOutput, calls=%fused_computation.13 | convolution fusion | flops 404750336 | bytes 1687552 | tf_op jit(solution)/shard_map/gjts,sgjp->tgjp/dot_general | solution.py:162
  75.1 23.0 %all-to-all-done.1 = f32[32,64,256]{2,1,0:T(8,128)S(1)} async-done(((f32[32,64,256]{2,1,0:T(8,128)}), f32[32,64,256]{2,1,0:T(8,128)S(1)}, u32[]{:S(2)}, u32[]{:S(2)}) %all-to-all-start.1) | async-done | bytes 2097184 | tf_op jit(solution)/shard_map/all_to_all | solution.py:152
  98.1 0.0 copy-done.8
  98.1 3.3 %fusion.18 = f32[128,1,32,64]{0,3,2,1:T(8,128)} fusion(f32[128,1,32,64]{0,3,2,1:T(8,128)} %fusion.13, f32[32,64,256]{2,1,0:T(8,128)S(1)} %all-to-all-done.1, f32[32]{0:T(128)S(1)} %copy-done.8, f32[128,32]{0,1:T(8,128)S(1)} %get-tuple-element.6, bf16[128,256]{1,0:T(8,128)(2,1)S(1)} %copy-done.3, bf16[128,1,32,64]{0,3,2,1:T(8,128)(2,1)S(1)} %bitcast.91), kind=kOutput, calls=%fused_computation.17 | convolution fusion | flops 806617088 | bytes 4800640 | tf_op jit(solution)/shard_map/tgn,gjpn->tgjp/dot_general | solution.py:165
  101.4 0.0 copy-start.2
  101.4 0.0 copy-start.7
  101.4 1.6 %copy.42 = f32[128,2048]{1,0:T(8,128)S(1)} copy(f32[128,2048]{0,1:T(8,128)} %bitcast.92) | data formatting | bytes 2097152 | tf_op jit(solution)/shard_map/reshape | solution.py:169
  103.0 0.0 copy-done.2
  103.0 0.4 multiply_reduce_fusion
  103.4 21.1 %psum.7 = f32[128]{0:T(128)S(1)} all-reduce(f32[128]{0:T(128)S(1)} %multiply_reduce_fusion), channel_id=1, replica_groups=mesh['ctx'=32,'head'=8] {'head'}, use_global_device_ids=true, to_apply=%region_5.6 | all-reduce | flops 128 | bytes 1024 | tf_op jit(solution)/shard_map/psum | solution.py:172
  124.5 0.0 copy-done.7
  124.5 0.4 multiply_convert_fusion
  124.9 0.0 copy-start.1
  124.9 3.8 %fusion.19.query_ref = bf16[128,1024]{1,0:T(8,128)(2,1)} fusion(bf16[128,2048]{1,0:T(8,128)(2,1)S(1)} %multiply_convert_fusion, bf16[1,2048,1024]{2,1,0:T(8,128)(2,1)} %param.20), kind=kOutput, calls=%fused_computation.20 | convolution fusion | flops 537001984 | bytes 4980736 | tf_op jit(solution)/shard_map/tgf,gfo->tgo/dot_general | solution.py:178
  128.7 0.0 copy-done.1
  128.7 0.0 all-gather.2.cloned.1.call-done
  128.8 10.3 %shard_map.131 = bf16[128,1024]{1,0:T(8,128)(2,1)} custom-call(s32[2]{0:T(128)} %pad_add_fusion.chunk_ref, bf16[128,1024]{1,0:T(8,128)(2,1)} %fusion.19.query_ref, bf16[4096,256]{1,0:T(8,128)(2,1)} %bitcast.94, s32[128,1]{1,0:T(8,128)} %copy.43.low_ref, s32[128,1]{1,0:T(8,128)} %iota_add_fusion.high_ref), custom_call_target="tpu_custom_call" | custom-call | tf_op jit(solution)/shard_map/pallas_call | solution.py:85
  (6 shorter events, 0.1 us)
Async XLA Ops:
  7.2 8.8 %copy-start = (bf16[128,256]{1,0:T(8,128)(2,1)S(1)}, bf16[128,256]{1,0:T(8,128)(2,1)}, u32[]{:S(2)}) copy-start(bf16[128,256]{1,0:T(8,128)(2,1)} %param.14) | copy-start | bytes 196612
  18.6 7.8 %copy-start.4 = (bf16[128,128]{1,0:T(8,128)(2,1)S(1)}, bf16[128,128]{1,0:T(8,128)(2,1)}, u32[]{:S(2)}) copy-start(bf16[128,128]{1,0:T(8,128)(2,1)} %param.22) | copy-start | bytes 98308
  18.6 7.8 %copy-start.5 = (bf16[128,128]{1,0:T(8,128)(2,1)S(1)}, bf16[128,128]{1,0:T(8,128)(2,1)}, u32[]{:S(2)}) copy-start(bf16[128,128]{1,0:T(8,128)(2,1)} %param.21) | copy-start | bytes 98308
  18.6 36.9 %all-to-all-start = ((f32[32,72,256]{2,1,0:T(8,128)}), f32[32,72,256]{2,1,0:T(8,128)S(1)}, u32[]{:S(2)}, u32[]{:S(2)}) async-start(f32[32,72,256]{2,1,0:T(8,128)} %pad_maximum_fusion), calls=%async_computation | async-start | bytes 4718592 | tf_op jit(solution)/shard_map/all_to_all | solution.py:137
  26.3 102.4 %all-gather.2.cloned.1.call-start = ((), (), s32[]{:S(2)}) async-start(), calls=%async_computation.2 | async-start | bytes 2162688 | tf_op jit(solution)/shard_map/all_gather | solution.py:193
  62.0 9.4 %copy-start.3 = (bf16[128,256]{1,0:T(8,128)(2,1)S(1)}, bf16[128,256]{1,0:T(8,128)(2,1)}, u32[]{:S(2)}) copy-start(bf16[128,256]{1,0:T(8,128)(2,1)} %param.15) | copy-start | bytes 196612
  62.0 9.6 %copy-start.6 = (f32[32,128]{1,0:T(8,128)S(1)}, f32[32,128]{1,0:T(8,128)}, u32[]{:S(2)}) copy-start(f32[32,128]{1,0:T(8,128)} %param.16) | copy-start | bytes 49156
  62.0 36.1 %all-to-all-start.1 = ((f32[32,64,256]{2,1,0:T(8,128)}), f32[32,64,256]{2,1,0:T(8,128)S(1)}, u32[]{:S(2)}, u32[]{:S(2)}) async-start(f32[32,64,256]{2,1,0:T(8,128)} %copy.41), calls=%async_computation.1 | async-start | bytes 4194304 | tf_op jit(solution)/shard_map/all_to_all | solution.py:152
  70.7 27.5 %copy-start.8 = (f32[32]{0:T(128)S(1)}, f32[32]{0:T(128)}, u32[]{:S(2)}) copy-start(f32[32]{0:T(128)} %param.18) | copy-start | bytes 388
  101.4 1.6 %copy-start.2 = (bf16[128,2048]{1,0:T(8,128)(2,1)S(1)}, bf16[128,2048]{1,0:T(8,128)(2,1)}, u32[]{:S(2)}) copy-start(bf16[128,2048]{1,0:T(8,128)(2,1)} %param.13) | copy-start | bytes 1572868
  101.4 23.2 %copy-start.7 = (f32[2048]{0:T(1024)S(1)}, f32[2048]{0:T(1024)}, u32[]{:S(2)}) copy-start(f32[2048]{0:T(1024)} %param.19) | copy-start | bytes 24580
  124.9 3.8 %copy-start.1 = (bf16[128,2048]{1,0:T(8,128)(2,1)}, bf16[128,2048]{1,0:T(8,128)(2,1)S(1)}, u32[]{:S(2)}) copy-start(bf16[128,2048]{1,0:T(8,128)(2,1)S(1)} %multiply_convert_fusion) | copy-start | bytes 1572868
Sparse Core Ops, SparseCore 0:
  30.3 70.9 all-gather.1

commit v9 on v8

--- a/solution.py
+++ b/solution.py
@@ -132,14 +132,41 @@
     ctx_count = lax.axis_size("ctx")
     owned = heads_dev // ctx_count
     block_log = jnp.where(carry_mask[-1] > 0, cum_decay[:, :, -1], -jnp.inf).reshape(heads_dev)
+    core = shard_index % 2
+    half_heads = heads_dev // 2
+    pair_swap = [(source, source ^ 1) for source in range(ctx_count)]
     log_rows = jnp.broadcast_to(block_log[:, None, None], (heads_dev, 8, STATE))
-    payload = jnp.concatenate([local_state.reshape(heads_dev, HEAD_DIM, STATE), log_rows], axis=1)
+    augmented = jnp.concatenate(
+        [local_state.reshape(heads_dev, HEAD_DIM, STATE), log_rows], axis=1
+    )
+    partner = lax.ppermute(
+        lax.dynamic_slice_in_dim(augmented, (1 - core) * half_heads, half_heads, 0),
+        "ctx",
+        pair_swap,
+    )
+    mine = lax.dynamic_slice_in_dim(augmented, core * half_heads, half_heads, 0)
+    first_core = core == 0
+    early_state = jnp.where(first_core, mine[:, :HEAD_DIM], partner[:, :HEAD_DIM])
+    late_state = jnp.where(first_core, partner[:, :HEAD_DIM], mine[:, :HEAD_DIM])
+    early_log = jnp.where(first_core, mine[:, HEAD_DIM, 0], partner[:, HEAD_DIM, 0])
+    late_log = jnp.where(first_core, partner[:, HEAD_DIM, 0], mine[:, HEAD_DIM, 0])
+    pair_state = jnp.exp(late_log)[:, None, None] * early_state + late_state
+    pair_log = early_log + late_log
+    splits = ctx_count // half_heads
+    part_rows = HEAD_DIM // splits
+    pair_rows = jnp.broadcast_to(
+        jnp.repeat(pair_log, splits)[:, None, None], (ctx_count, 8, STATE)
+    )
+    payload = jnp.concatenate(
+        [pair_state.reshape(ctx_count, part_rows, STATE), pair_rows], axis=1
+    )
+    pair_count = ctx_count // 2
     gathered = lax.all_to_all(payload, "ctx", 0, 0, tiled=True).reshape(
-        ctx_count, owned, HEAD_DIM + 8, STATE
-    )
-    states_mine = gathered[:, :, :HEAD_DIM, :]
-    mine_log = gathered[:, :, HEAD_DIM, 0]
-    block_row = jnp.arange(ctx_count, dtype=jnp.int32)
+        pair_count, 2, part_rows + 8, STATE
+    )
+    states_mine = gathered[:, :, :part_rows, :]
+    mine_log = gathered[:, :, part_rows, 0]
+    block_row = jnp.arange(pair_count, dtype=jnp.int32)
     between = (block_row[None, :, None] < block_row[None, None, :]) & (
         block_row[None, None, :] < block_row[:, None, None]
     )
@@ -148,9 +175,19 @@
     )
     earlier = block_row[:, None] > block_row[None, :]
     transfer = jnp.where(earlier[None], jnp.exp(log_span), 0.0)
-    incoming_mine = jnp.einsum("kcd,dkpn->ckpn", transfer, states_mine, precision=highest)
-    incoming = lax.all_to_all(
-        incoming_mine.reshape(ctx_count * owned, HEAD_DIM, STATE), "ctx", 0, 0, tiled=True
+    incoming_mine = jnp.einsum("ukd,dupn->kupn", transfer, states_mine, precision=highest)
+    pair_incoming = lax.all_to_all(
+        incoming_mine.reshape(ctx_count, part_rows, STATE), "ctx", 0, 0, tiled=True
+    ).reshape(half_heads, HEAD_DIM, STATE)
+    after_early = jnp.exp(early_log)[:, None, None] * pair_incoming + early_state
+    swapped = lax.ppermute(
+        jnp.where(first_core, after_early, pair_incoming), "ctx", pair_swap
+    )
+    kept = jnp.where(first_core, pair_incoming, after_early)
+    incoming = jnp.where(
+        first_core,
+        jnp.concatenate([kept, swapped], axis=0),
+        jnp.concatenate([swapped, kept], axis=0),
     ).reshape(groups_dev, head_group, HEAD_DIM, STATE)
     same_doc = (own_docs[:, None] == own_docs[None, :]) & (row_index[:, None] >= row_index[None, :])
     log_gap = cum_decay[:, :, :, None] - cum_decay[:, :, None, :]

time: 147 us -> 136 us (0.925)
  waiting for transfers between devices: 51.4 us -> 35.4 us
  other arithmetic: 7.69 us -> 13.7 us
  matrix products: 15.8 us -> 13.5 us
  between operations: 15.7 us -> 17.9 us
    all_to_all x1, waiting for transfers between devices: 28.4 us -> 17.6 us  [shards(): lax.all_to_all(payload, 'ctx', 0, 0, tiled=True)]
    all_to_all x1, waiting for transfers between devices: 23 us -> 14 us  [shards(): lax.all_to_all(incoming_mine.reshape(ctx_count, part_rows, STATE), 'ctx',...]
    ppermute x0 -> x2, waiting for transfers between devices: none -> 3.06 us  [the longest x1 3.06 us: shards(): lax.ppermute(lax.dynamic_slice_in_dim(augmented, (1 - core) * half_heads,...]
    reshape x1 -> x0, local copies, waits for them, and re-layouts: 2.52 us -> none  [shards(): incoming_mine.reshape(ctx_count * owned, HEAD_DIM, STATE)]
    select_n x0 -> x2, other arithmetic: none -> 2.34 us  [the longest x1 2.33 us: shards(): kept = jnp.where(first_core, pair_incoming, after_early)]
    dot_general x1, matrix products: 3.26 us -> 1.2 us  [shards(): jnp.einsum('tgn,gjpn->tgjp', state_out.astype(jnp.float32), incoming, pre...]
    transpose x0 -> x1, local copies, waits for them, and re-layouts: none -> 1.6 us  [shards(): jnp.einsum('ukd,dupn->kupn', transfer, states_mine, precision=highest)]
  transfers between devices with their start and end apart: 3 -> 5, of which waited for: 2 -> 4; matrix products, arithmetic and copies ran while one was open for 15% -> 12% of each run, Pallas kernels for 0% -> 0%
where the time goes in v9:
time: 136 us; the launch traced here: 135 us
  waiting for transfers between devices  35.4 us (26%)
  blocking collectives  20 us (15%)
  between operations  17.9 us (13%)
  starting transfers between devices  14.6 us (11%)
  other arithmetic  13.7 us (10%)
  matrix products  13.5 us (10%)
  Pallas kernels  11.1 us (8%)
  local copies, waits for them, and re-layouts  9.08 us (7%)
    psum x1, blocking collectives, shards(): square_sum = lax.psum(square_local, 'head')  20 us
    all_to_all x1, waiting for transfers between devices, shards(): lax.all_to_all(payload, 'ctx', 0, 0, tiled=True)  17.6 us
    all_to_all x1, waiting for transfers between devices, shards(): lax.all_to_all(incoming_mine.reshape(ctx_count, part_rows, STATE), 'ctx',...  14 us
    pallas_call x1, Pallas kernels, flash_attention(): pl.pallas_call(attention_kernel, grid_spec=grid_spec, out_shape=jax.Shape...  11.1 us
    all_to_all x1, starting transfers between devices, shards(): lax.all_to_all(payload, 'ctx', 0, 0, tiled=True)  7.6 us
    all_to_all x1, starting transfers between devices, shards(): lax.all_to_all(incoming_mine.reshape(ctx_count, part_rows, STATE), 'ctx',...  6.21 us
    dot_general x1, matrix products, shards(): jnp.einsum('tgf,gfo->tgo', mixer_out.reshape(tok_rows, groups_dev, -1), q...  3.83 us
    dot_general x1, matrix products, shards(): jnp.einsum('gjts,sgjp->tgjp', mixing, input_f32, precision=highest)  3.77 us
  transfers between devices with their start and end apart: 5, of which 4 were waited for; matrix products, arithmetic and copies ran while one was open for 12% of the time, Pallas kernels for 0%

profile of v9, /device:TPU:4, one launch (start us, length us, event | category | flops | bytes accessed | tf_op | source)
XLA Modules:
  0.0 135.4 jit_solution(3094571330616267291)
XLA Ops:
  7.2 0.0 copy-start
  7.2 0.7 copy.29
  8.0 0.1 reduce.2
  8.1 1.3 fusion.51
  9.4 0.6 fusion.48
  10.0 0.7 slice.36
  10.7 0.0 copy-done.13
  11.3 0.8 fusion.43
  12.2 0.2 slice_reduce_fusion
  12.4 1.3 copy.30
  13.7 0.0 copy-start.5
  13.7 0.7 compare_convert_fusion.1
  14.4 0.6 slice.37
  15.6 1.3 multiply_bitcast_fusion
  17.0 0.1 bitcast_multiply_fusion.1
  17.1 1.0 fusion.40
  18.1 0.1 broadcast_in_dim.67
  18.2 1.2 fusion.25
  19.4 0.0 collective-permute-start
  19.4 3.1 %collective-permute-done = f32[16,72,256]{2,1,0:T(8,128)S(1)} collective-permute-done((f32[16,72,256]{2,1,0:T(8,128)}, f32[16,72,256]{2,1,0:T(8,128)S(1)}, u32[]{:S(2)}, u32[]{:S(2)}) %collective-permute-start) | collective-permute-done | bytes 1179680 | tf_op jit(solution)/shard_map/ppermute | solution.py:142
  22.5 0.9 exponential_reduce_fusion
  23.4 0.1 broadcast_in_dim.68
  23.4 0.1 broadcast_in_dim.69
  23.5 0.3 select_add_fusion
  23.8 0.1 broadcast_in_dim.70
  23.9 1.2 pad_maximum_fusion
  25.1 0.0 copy-done.1
  25.1 7.6 %all-to-all-start = ((f32[32,40,256]{2,1,0:T(8,128)}), f32[32,40,256]{2,1,0:T(8,128)S(1)}, u32[]{:S(2)}, u32[]{:S(2)}) async-start(f32[32,40,256]{2,1,0:T(8,128)} %pad_maximum_fusion), calls=%async_computation | async-start | bytes 2621440 | tf_op jit(solution)/shard_map/all_to_all | solution.py:164
  32.8 17.6 %all-to-all-done = f32[32,40,256]{2,1,0:T(8,128)S(1)} async-done(((f32[32,40,256]{2,1,0:T(8,128)}), f32[32,40,256]{2,1,0:T(8,128)S(1)}, u32[]{:S(2)}, u32[]{:S(2)}) %all-to-all-start) | async-done | bytes 1310752 | tf_op jit(solution)/shard_map/all_to_all | solution.py:164
  50.3 1.1 slice.50
  51.5 0.1 copy.33
  51.6 0.2 select_reduce_fusion
  51.7 2.8 %convolution_bitcast_fusion = f32[16,2,32,256]{3,0,2,1:T(8,128)S(1)} fusion(f32[16,2,32,256]{3,2,1,0:T(8,128)} %slice.50, f32[2,16,16]{2,1,0:T(8,128)S(1)} %select_reduce_fusion, pred[16,16]{1,0:T(8,128)(4,1)S(1)} %iota_compare_fusion.5), kind=kOutput, calls=%fused_computation.21 | convolution fusion | flops 50332160 | bytes 2099456 | tf_op jit(solution)/shard_map/ukd,dupn->kupn/dot_general | solution.py:178
  54.5 0.0 copy-start.9
  54.5 0.0 copy-start.10
  54.5 0.0 copy-start.2
  54.5 1.6 %copy.34 = f32[16,2,32,256]{3,2,1,0:T(8,128)} copy(f32[16,2,32,256]{3,0,2,1:T(8,128)S(1)} %convolution_bitcast_fusion) | data formatting | bytes 2097152 | tf_op jit(solution)/shard_map/ukd,dupn->kupn/transpose | solution.py:178
  56.1 6.2 %all-to-all-start.1 = ((f32[32,32,256]{2,1,0:T(8,128)}), f32[32,32,256]{2,1,0:T(8,128)S(1)}, u32[]{:S(2)}, u32[]{:S(2)}) async-start(f32[32,32,256]{2,1,0:T(8,128)} %bitcast.22), calls=%async_computation.1 | async-start | bytes 2097152 | tf_op jit(solution)/shard_map/all_to_all | solution.py:179
  62.4 0.0 all-gather.2.cloned.1.call-start
  62.4 0.6 pad_maximum_fusion.1
  63.1 0.0 all-gather.2.cloned.1.call-update
  63.1 14.0 %all-to-all-done.1 = f32[32,32,256]{2,1,0:T(8,128)S(1)} async-done(((f32[32,32,256]{2,1,0:T(8,128)}), f32[32,32,256]{2,1,0:T(8,128)S(1)}, u32[]{:S(2)}, u32[]{:S(2)}) %all-to-all-start.1) | async-done | bytes 1048608 | tf_op jit(solution)/shard_map/all_to_all | solution.py:179
  77.1 2.3 %bitcast_select_fusion.1 = (f32[16,64,256]{2,1,0:T(8,128)}, f32[16,64,256]{2,1,0:T(8,128)}) fusion(f32[16]{0:T(128)} %get-tuple-element.2, pred[]{:T(512)S(6)} %eq.45, f32[16,72,256]{2,1,0:T(8,128)S(1)} %copy-done.2, f32[16,72,256]{2,1,0:T(8,128)S(1)} %get-tuple-element.14, f32[16,64,256]{2,1,0:T(8,128)S(1)} %bitcast.96), kind=kLoop, calls=%fused_computation.37 | loop fusion | flops 1310720 | bytes 5242945 | tf_op jit(solution)/shard_map/jit(_where)/select_n | solution.py:186
  79.4 0.7 collective-permute-start.1
  82.4 1.3 copy.36.low_ref
  83.7 0.6 pad_add_fusion.chunk_ref
  84.3 0.6 iota_add_fusion.high_ref
  85.0 0.8 fusion.42
  85.7 0.0 copy-done.8
  85.7 0.1 fusion.55
  85.9 3.8 %fusion.15 = f32[128,1,32,64]{0,3,2,1:T(8,128)S(1)} fusion(bf16[128,32,64]{0,2,1:T(8,128)(2,1)} %bitcast.97, f32[32,128]{1,0:T(8,128)} %param.16, f32[32,128]{1,0:T(8,128)S(1)} %bitcast.102, f32[128,128]{1,0:T(8,128)S(1)} %fusion.55, pred[128,128]{1,0:T(8,128)(4,1)S(1)} %fusion.42), kind=kOutput, calls=%fused_computation.20 | convolution fusion | flops 404750336 | bytes 1687552 | tf_op jit(solution)/shard_map/gjts,sgjp->tgjp/dot_general | solution.py:199
  89.6 0.0 collective-permute-done.1
  89.7 1.2 fusion.20
  90.9 0.0 copy-start.4
  90.9 0.0 copy-start.12
  90.9 0.3 copy.35
  91.3 0.7 copy-done.4
  91.9 0.4 multiply_reduce_fusion
  92.4 20.0 %psum.7 = f32[128]{0:T(128)S(1)} all-reduce(f32[128]{0:T(128)S(1)} %multiply_reduce_fusion), channel_id=1, replica_groups=mesh['ctx'=32,'head'=8] {'head'}, use_global_device_ids=true, to_apply=%region_5.6 | all-reduce | flops 128 | bytes 1024 | tf_op jit(solution)/shard_map/psum | solution.py:209
  112.4 0.4 multiply_convert_fusion
  112.8 0.0 copy-start.3
  112.8 3.8 %fusion.21.query_ref = bf16[128,1024]{1,0:T(8,128)(2,1)} fusion(bf16[128,2048]{1,0:T(8,128)(2,1)S(1)} %multiply_convert_fusion, bf16[1,2048,1024]{2,1,0:T(8,128)(2,1)} %param.20), kind=kOutput, calls=%fused_computation.28 | convolution fusion | flops 537001984 | bytes 4980736 | tf_op jit(solution)/shard_map/tgf,gfo->tgo/dot_general | solution.py:215
  116.7 0.7 all-gather.2.cloned.1.call-done
  117.4 11.1 %shard_map.131 = bf16[128,1024]{1,0:T(8,128)(2,1)} custom-call(s32[2]{0:T(128)} %pad_add_fusion.chunk_ref, bf16[128,1024]{1,0:T(8,128)(2,1)} %fusion.21.query_ref, bf16[4096,256]{1,0:T(8,128)(2,1)} %bitcast.99, s32[128,1]{1,0:T(8,128)} %copy.36.low_ref, s32[128,1]{1,0:T(8,128)} %iota_add_fusion.high_ref), custom_call_target="tpu_custom_call" | custom-call | tf_op jit(solution)/shard_map/pallas_call | solution.py:85
  (28 shorter events, 0.1 us)
Async XLA Ops:
  7.2 9.9 %copy-start = (bf16[128,256]{1,0:T(8,128)(2,1)S(1)}, bf16[128,256]{1,0:T(8,128)(2,1)}, u32[]{:S(2)}) copy-start(bf16[128,256]{1,0:T(8,128)(2,1)} %param.14) | copy-start | bytes 196612
  10.0 0.7 copy-start.13
  13.7 4.4 %copy-start.5 = (bf16[128,2048]{0,1:T(8,128)(2,1)}, bf16[128,2048]{0,1:T(8,128)(2,1)S(1)}, u32[]{:S(2)}) copy-start(bf16[128,2048]{0,1:T(8,128)(2,1)S(1)} %copy.30) | copy-start | bytes 1572868
  19.4 3.1 %collective-permute-start = (f32[16,72,256]{2,1,0:T(8,128)}, f32[16,72,256]{2,1,0:T(8,128)S(1)}, u32[]{:S(2)}, u32[]{:S(2)}) collective-permute-start(f32[16,72,256]{2,1,0:T(8,128)} %get-tuple-element.13), channel_id=1, source_target_pairs={{0,8},{8,0},{16,24},{24,16},{32,40},{40,32},{48,56},{56,48},{64,72... | collective-permute-start | bytes 3538952 | tf_op jit(solution)/shard_map/ppermute | solution.py:142
  22.4 2.7 %copy-start.1 = (f32[16,72,256]{2,1,0:T(8,128)}, f32[16,72,256]{2,1,0:T(8,128)S(1)}, u32[]{:S(2)}) copy-start(f32[16,72,256]{2,1,0:T(8,128)S(1)} %collective-permute-done) | copy-start | bytes 3538948
  25.1 25.3 %all-to-all-start = ((f32[32,40,256]{2,1,0:T(8,128)}), f32[32,40,256]{2,1,0:T(8,128)S(1)}, u32[]{:S(2)}, u32[]{:S(2)}) async-start(f32[32,40,256]{2,1,0:T(8,128)} %pad_maximum_fusion), calls=%async_computation | async-start | bytes 2621440 | tf_op jit(solution)/shard_map/all_to_all | solution.py:164
  54.5 7.9 %copy-start.9 = (bf16[128,128]{1,0:T(8,128)(2,1)S(1)}, bf16[128,128]{1,0:T(8,128)(2,1)}, u32[]{:S(2)}) copy-start(bf16[128,128]{1,0:T(8,128)(2,1)} %param.22) | copy-start | bytes 98308
  54.5 7.9 %copy-start.10 = (bf16[128,128]{1,0:T(8,128)(2,1)S(1)}, bf16[128,128]{1,0:T(8,128)(2,1)}, u32[]{:S(2)}) copy-start(bf16[128,128]{1,0:T(8,128)(2,1)} %param.21) | copy-start | bytes 98308
  54.5 22.6 %copy-start.2 = (f32[16,72,256]{2,1,0:T(8,128)S(1)}, f32[16,72,256]{2,1,0:T(8,128)}, u32[]{:S(2)}) copy-start(f32[16,72,256]{2,1,0:T(8,128)} %copy-done.1) | copy-start | bytes 3538948
  56.1 21.0 %all-to-all-start.1 = ((f32[32,32,256]{2,1,0:T(8,128)}), f32[32,32,256]{2,1,0:T(8,128)S(1)}, u32[]{:S(2)}, u32[]{:S(2)}) async-start(f32[32,32,256]{2,1,0:T(8,128)} %bitcast.22), calls=%async_computation.1 | async-start | bytes 2097152 | tf_op jit(solution)/shard_map/all_to_all | solution.py:179
  62.4 55.0 %all-gather.2.cloned.1.call-start = ((), (), s32[]{:S(2)}) async-start(), calls=%async_computation.2 | async-start | bytes 2162688 | tf_op jit(solution)/shard_map/all_gather | solution.py:230
  77.1 8.6 %copy-start.8 = (bf16[128,256]{1,0:T(8,128)(2,1)S(1)}, bf16[128,256]{1,0:T(8,128)(2,1)}, u32[]{:S(2)}) copy-start(bf16[128,256]{1,0:T(8,128)(2,1)} %param.15) | copy-start | bytes 196612
  79.4 10.2 %collective-permute-start.1 = (f32[16,64,256]{2,1,0:T(8,128)}, f32[16,64,256]{2,1,0:T(8,128)S(1)}, u32[]{:S(2)}, u32[]{:S(2)}) collective-permute-start(f32[16,64,256]{2,1,0:T(8,128)} %get-tuple-element.10), channel_id=1, source_target_pairs={{0,8},{8,0},{16,24},{24,16},{32,40},{40,32},{48,56},{56,48},{64,72... | collective-permute-start | bytes 3145736 | tf_op jit(solution)/shard_map/ppermute | solution.py:183
  84.3 5.3 %copy-start.6 = (bf16[128,2048]{0,1:T(8,128)(2,1)S(1)}, bf16[128,2048]{0,1:T(8,128)(2,1)}, u32[]{:S(2)}) copy-start(bf16[128,2048]{0,1:T(8,128)(2,1)} %copy-done.5) | copy-start | bytes 1572868
  84.3 5.3 %copy-start.7 = (f32[16,64,256]{2,1,0:T(8,128)S(1)}, f32[16,64,256]{2,1,0:T(8,128)}, u32[]{:S(2)}) copy-start(f32[16,64,256]{2,1,0:T(8,128)} %get-tuple-element.9) | copy-start | bytes 3145732
  84.3 5.3 %copy-start.11 = (f32[128,32]{0,1:T(8,128)S(1)}, f32[128,32]{0,1:T(8,128)}, u32[]{:S(2)}) copy-start(f32[128,32]{0,1:T(8,128)} %get-tuple-element.15) | copy-start | bytes 49156
  84.3 5.4 %copy-start.14 = (f32[32]{0:T(128)S(1)}, f32[32]{0:T(128)}, u32[]{:S(2)}) copy-start(f32[32]{0:T(128)} %param.18) | copy-start | bytes 388
  90.9 1.0 copy-start.4
  90.9 21.5 %copy-start.12 = (f32[2048]{0:T(1024)S(1)}, f32[2048]{0:T(1024)}, u32[]{:S(2)}) copy-start(f32[2048]{0:T(1024)} %param.19) | copy-start | bytes 24580
  112.8 3.8 %copy-start.3 = (bf16[128,2048]{1,0:T(8,128)(2,1)}, bf16[128,2048]{1,0:T(8,128)(2,1)S(1)}, u32[]{:S(2)}) copy-start(bf16[128,2048]{1,0:T(8,128)(2,1)S(1)} %multiply_convert_fusion) | copy-start | bytes 1572868
Sparse Core Ops, SparseCore 0:
  66.3 51.0 all-gather.1

commit v10 on v9

--- a/solution.py
+++ b/solution.py
@@ -131,6 +131,14 @@
     carry_mask = (own_docs == prev_doc).astype(jnp.float32)
     ctx_count = lax.axis_size("ctx")
     owned = heads_dev // ctx_count
+    kv_local = jnp.concatenate(
+        [
+            keys.reshape(tok_rows, groups_dev, ATT_DIM),
+            values.reshape(tok_rows, groups_dev, ATT_DIM),
+        ],
+        axis=2,
+    )
+    kv_all = lax.all_gather(kv_local, "ctx", axis=0, tiled=True)
     block_log = jnp.where(carry_mask[-1] > 0, cum_decay[:, :, -1], -jnp.inf).reshape(heads_dev)
     core = shard_index % 2
     half_heads = heads_dev // 2
@@ -179,6 +187,7 @@
     pair_incoming = lax.all_to_all(
         incoming_mine.reshape(ctx_count, part_rows, STATE), "ctx", 0, 0, tiled=True
     ).reshape(half_heads, HEAD_DIM, STATE)
+    kv_all, pair_incoming = lax.optimization_barrier((kv_all, pair_incoming))
     after_early = jnp.exp(early_log)[:, None, None] * pair_incoming + early_state
     swapped = lax.ppermute(
         jnp.where(first_core, after_early, pair_incoming), "ctx", pair_swap
@@ -220,14 +229,6 @@
     )
     query = query.astype(jnp.bfloat16).reshape(tok_rows, groups_dev, query_group, ATT_DIM)
 
-    kv_local = jnp.concatenate(
-        [
-            keys.reshape(tok_rows, groups_dev, ATT_DIM),
-            values.reshape(tok_rows, groups_dev, ATT_DIM),
-        ],
-        axis=2,
-    )
-    kv_all = lax.all_gather(kv_local, "ctx", axis=0, tiled=True)
     doc_starts = jnp.cumsum(doc_lengths) - doc_lengths
     row_low = jnp.max(
         jnp.where(doc_starts[None, :] <= own_pos[:, None], doc_starts[None, :], 0), axis=1

time: 136 us -> 140 us (1.029)
  blocking collectives: 20 us -> 41 us
  waiting for transfers between devices: 35.4 us -> 25.8 us
  starting transfers between devices: 14.6 us -> 7.91 us
    all_to_all x0 -> x1, blocking collectives: none -> 23.2 us  [shards(): lax.all_to_all(incoming_mine.reshape(ctx_count, part_rows, STATE), 'ctx',...]
    all_to_all x1 -> x0, waiting for transfers between devices: 14 us -> none  [shards(): lax.all_to_all(incoming_mine.reshape(ctx_count, part_rows, STATE), 'ctx',...]
    all_to_all x1 -> x0, starting transfers between devices: 6.21 us -> none  [shards(): lax.all_to_all(incoming_mine.reshape(ctx_count, part_rows, STATE), 'ctx',...]
    all_gather x1, waiting for transfers between devices: 0.74 us -> 4.91 us  [shards(): kv_all = lax.all_gather(kv_local, 'ctx', axis=0, tiled=True)]
    psum x1, blocking collectives: 20 us -> 17.8 us  [shards(): square_sum = lax.psum(square_local, 'head')]
  transfers between devices with their start and end apart: 5 -> 4, of which waited for: 4 -> 3; matrix products, arithmetic and copies ran while one was open for 12% -> 11% of each run, Pallas kernels for 0% -> 0%
where the time goes in v10:
time: 140 us
  blocking collectives  41 us (29%)
  waiting for transfers between devices  25.8 us (18%)
  between operations  18.2 us (13%)
  other arithmetic  13.8 us (10%)
  matrix products  13.6 us (10%)
  Pallas kernels  11.1 us (8%)
  local copies, waits for them, and re-layouts  8.69 us (6%)
  starting transfers between devices  7.91 us (6%)
    all_to_all x1, blocking collectives, shards(): lax.all_to_all(incoming_mine.reshape(ctx_count, part_rows, STATE), 'ctx',...  23.2 us
    all_to_all x1, waiting for transfers between devices, shards(): lax.all_to_all(payload, 'ctx', 0, 0, tiled=True)  18.5 us
    psum x1, blocking collectives, shards(): square_sum = lax.psum(square_local, 'head')  17.8 us
    pallas_call x1, Pallas kernels, flash_attention(): pl.pallas_call(attention_kernel, grid_spec=grid_spec, out_shape=jax.Shape...  11.1 us
    all_to_all x1, starting transfers between devices, shards(): lax.all_to_all(payload, 'ctx', 0, 0, tiled=True)  7.6 us
    all_gather x1, waiting for transfers between devices, shards(): kv_all = lax.all_gather(kv_local, 'ctx', axis=0, tiled=True)  4.91 us
    dot_general x1, matrix products, shards(): jnp.einsum('tgf,gfo->tgo', mixer_out.reshape(tok_rows, groups_dev, -1), q...  3.87 us
    dot_general x1, matrix products, shards(): jnp.einsum('gjts,sgjp->tgjp', mixing, input_f32, precision=highest)  3.77 us
  transfers between devices with their start and end apart: 4, of which 3 were waited for; matrix products, arithmetic and copies ran while one was open for 11% of the time, Pallas kernels for 0%

profile of v10, /device:TPU:4, one launch (start us, length us, event | category | flops | bytes accessed | tf_op | source)
XLA Modules:
  0.0 140.1 jit_solution(3593456562389838293)
XLA Ops:
  7.2 0.0 copy-start
  7.2 0.0 all-gather.2.cloned.1.call-start
  7.3 0.7 copy.29
  8.0 0.1 reduce.2
  8.1 1.3 fusion.52
  9.4 0.6 fusion.49
  10.1 0.6 copy-done.13
  10.6 0.7 slice.36
  11.9 0.8 fusion.44
  12.8 0.2 slice_reduce_fusion
  13.0 1.3 copy.30
  14.3 0.0 copy-start.5
  14.3 0.7 compare_convert_fusion.1
  15.0 0.6 slice.37
  16.3 1.3 multiply_bitcast_fusion
  17.6 0.1 bitcast_multiply_fusion
  17.7 0.0 copy-done
  17.7 1.0 fusion.41
  18.7 0.1 broadcast_in_dim.67
  18.8 0.0 copy-start.9
  18.8 0.0 copy-start.10
  18.8 1.3 fusion.25
  20.1 0.0 collective-permute-start
  20.1 0.0 copy-done.10
  20.1 0.6 pad_maximum_fusion.1
  20.7 0.0 all-gather.2.cloned.1.call-update
  20.7 2.4 %collective-permute-done = f32[16,72,256]{2,1,0:T(8,128)S(1)} collective-permute-done((f32[16,72,256]{2,1,0:T(8,128)}, f32[16,72,256]{2,1,0:T(8,128)S(1)}, u32[]{:S(2)}, u32[]{:S(2)}) %collective-permute-start) | collective-permute-done | bytes 1179680 | tf_op jit(solution)/shard_map/ppermute | solution.py:150
  23.1 0.9 exponential_reduce_fusion
  24.1 0.1 broadcast_in_dim.68
  24.1 0.1 broadcast_in_dim.69
  24.2 0.3 select_add_fusion
  24.5 0.1 broadcast_in_dim.70
  24.6 1.2 pad_maximum_fusion
  25.8 0.0 copy-done.1
  25.8 7.6 %all-to-all-start = ((f32[32,40,256]{2,1,0:T(8,128)}), f32[32,40,256]{2,1,0:T(8,128)S(1)}, u32[]{:S(2)}, u32[]{:S(2)}) async-start(f32[32,40,256]{2,1,0:T(8,128)} %pad_maximum_fusion), calls=%async_computation | async-start | bytes 2621440 | tf_op jit(solution)/shard_map/all_to_all | solution.py:172
  33.4 18.5 %all-to-all-done = f32[32,40,256]{2,1,0:T(8,128)S(1)} async-done(((f32[32,40,256]{2,1,0:T(8,128)}), f32[32,40,256]{2,1,0:T(8,128)S(1)}, u32[]{:S(2)}, u32[]{:S(2)}) %all-to-all-start) | async-done | bytes 1310752 | tf_op jit(solution)/shard_map/all_to_all | solution.py:172
  51.9 1.1 slice.50
  53.0 0.1 copy.33
  53.1 0.2 select_reduce_fusion
  53.3 2.8 %convolution_bitcast_fusion = f32[16,2,32,256]{3,0,2,1:T(8,128)S(1)} fusion(f32[16,2,32,256]{3,2,1,0:T(8,128)} %slice.50, f32[2,16,16]{2,1,0:T(8,128)S(1)} %select_reduce_fusion, pred[16,16]{1,0:T(8,128)(4,1)S(1)} %iota_compare_fusion.5), kind=kOutput, calls=%fused_computation.21 | convolution fusion | flops 50332160 | bytes 2099456 | tf_op jit(solution)/shard_map/ukd,dupn->kupn/dot_general | solution.py:186
  56.1 0.6 copy.34
  56.7 23.2 %all_to_all.10 = f32[32,32,256]{2,1,0:T(8,128)S(1)} all-to-all(f32[32,32,256]{2,1,0:T(8,128)S(1)} %bitcast.86), channel_id=1, replica_groups=mesh['ctx'=32,'head'=8] {'ctx'}, dimensions={0} | all-to-all | bytes 2097152 | tf_op jit(solution)/shard_map/all_to_all | solution.py:187
  79.9 4.9 %all-gather.2.cloned.1.call-done = bf16[4096,1,256]{2,0,1:T(8,128)(2,1)} async-done(((bf16[128,1,256]{2,0,1:T(8,128)(2,1)}), bf16[4096,1,256]{2,0,1:T(8,128)(2,1)}) %all-gather.2.cloned.1.call-update) | async-done | bytes 2097168 | tf_op jit(solution)/shard_map/all_gather | solution.py:141
  84.8 2.3 %fusion.32 = (f32[16,64,256]{2,1,0:T(8,128)}, f32[16,64,256]{2,1,0:T(8,128)}) fusion(f32[16,64,256]{2,1,0:T(8,128)S(1)} %bitcast.87, f32[16]{0:T(128)} %get-tuple-element.6, pred[]{:T(512)S(6)} %eq.45, f32[16,72,256]{2,1,0:T(8,128)S(1)} %copy-done.2, f32[16,72,256]{2,1,0:T(8,128)S(1)} %get-tuple-element.18), kind=kLoop, calls=%fused_computation.41 | loop fusion | flops 1310720 | bytes 5242945 | tf_op jit(solution)/shard_map/jit(_where)/select_n | solution.py:195
  87.1 0.3 collective-permute-start.1
  89.9 1.3 copy.36.low_ref
  91.2 0.6 pad_add_fusion.chunk_ref
  91.9 0.6 iota_add_fusion.high_ref
  92.5 0.8 fusion.43
  93.3 0.1 fusion.56
  93.5 3.8 %fusion.15 = f32[128,1,32,64]{0,3,2,1:T(8,128)S(1)} fusion(bf16[128,32,64]{0,2,1:T(8,128)(2,1)} %bitcast.88, f32[32,128]{1,0:T(8,128)} %param.16, f32[32,128]{1,0:T(8,128)S(1)} %bitcast.93, f32[128,128]{1,0:T(8,128)S(1)} %fusion.56, pred[128,128]{1,0:T(8,128)(4,1)S(1)} %fusion.43), kind=kOutput, calls=%fused_computation.20 | convolution fusion | flops 404750336 | bytes 1687552 | tf_op jit(solution)/shard_map/gjts,sgjp->tgjp/dot_general | solution.py:208
  97.2 0.0 collective-permute-done.1
  97.3 1.2 fusion.20
  98.5 0.0 copy-start.4
  98.5 0.0 copy-start.12
  98.5 0.3 copy.35
  98.9 0.7 copy-done.4
  99.5 0.4 multiply_reduce_fusion
  100.0 17.8 %psum.7 = f32[128]{0:T(128)S(1)} all-reduce(f32[128]{0:T(128)S(1)} %multiply_reduce_fusion), channel_id=1, replica_groups=mesh['ctx'=32,'head'=8] {'head'}, use_global_device_ids=true, to_apply=%region_5.6 | all-reduce | flops 128 | bytes 1024 | tf_op jit(solution)/shard_map/psum | solution.py:218
  117.8 0.4 multiply_convert_fusion
  118.2 0.0 copy-start.3
  118.2 3.9 %fusion.21.query_ref = bf16[128,1024]{1,0:T(8,128)(2,1)} fusion(bf16[128,2048]{1,0:T(8,128)(2,1)S(1)} %multiply_convert_fusion, bf16[1,2048,1024]{2,1,0:T(8,128)(2,1)} %param.20), kind=kOutput, calls=%fused_computation.28 | convolution fusion | flops 537001984 | bytes 4980736 | tf_op jit(solution)/shard_map/tgf,gfo->tgo/dot_general | solution.py:224
  122.1 0.0 copy-done.3
  122.1 11.1 %shard_map.131 = bf16[128,1024]{1,0:T(8,128)(2,1)} custom-call(s32[2]{0:T(128)} %pad_add_fusion.chunk_ref, bf16[128,1024]{1,0:T(8,128)(2,1)} %fusion.21.query_ref, bf16[4096,256]{1,0:T(8,128)(2,1)} %bitcast.90, s32[128,1]{1,0:T(8,128)} %copy.36.low_ref, s32[128,1]{1,0:T(8,128)} %iota_add_fusion.high_ref), custom_call_target="tpu_custom_call" | custom-call | tf_op jit(solution)/shard_map/pallas_call | solution.py:85
  (27 shorter events, 0.1 us)
Async XLA Ops:
  7.2 10.5 %copy-start = (bf16[128,256]{1,0:T(8,128)(2,1)S(1)}, bf16[128,256]{1,0:T(8,128)(2,1)}, u32[]{:S(2)}) copy-start(bf16[128,256]{1,0:T(8,128)(2,1)} %param.14) | copy-start | bytes 196612
  7.2 77.6 %all-gather.2.cloned.1.call-start = ((), (), s32[]{:S(2)}) async-start(), calls=%async_computation.2 | async-start | bytes 2162688 | tf_op jit(solution)/shard_map/all_gather | solution.py:141
  10.1 0.6 copy-start.13
  14.3 4.4 %copy-start.5 = (bf16[128,2048]{0,1:T(8,128)(2,1)}, bf16[128,2048]{0,1:T(8,128)(2,1)S(1)}, u32[]{:S(2)}) copy-start(bf16[128,2048]{0,1:T(8,128)(2,1)S(1)} %copy.30) | copy-start | bytes 1572868
  18.8 1.3 copy-start.9
  18.8 1.3 copy-start.10
  20.1 3.1 %collective-permute-start = (f32[16,72,256]{2,1,0:T(8,128)}, f32[16,72,256]{2,1,0:T(8,128)S(1)}, u32[]{:S(2)}, u32[]{:S(2)}) collective-permute-start(f32[16,72,256]{2,1,0:T(8,128)} %get-tuple-element.17), channel_id=1, source_target_pairs={{0,8},{8,0},{16,24},{24,16},{32,40},{40,32},{48,56},{56,48},{64,72... | collective-permute-start | bytes 3538952 | tf_op jit(solution)/shard_map/ppermute | solution.py:150
  23.1 2.7 %copy-start.1 = (f32[16,72,256]{2,1,0:T(8,128)}, f32[16,72,256]{2,1,0:T(8,128)S(1)}, u32[]{:S(2)}) copy-start(f32[16,72,256]{2,1,0:T(8,128)S(1)} %collective-permute-done) | copy-start | bytes 3538948
  25.8 26.1 %all-to-all-start = ((f32[32,40,256]{2,1,0:T(8,128)}), f32[32,40,256]{2,1,0:T(8,128)S(1)}, u32[]{:S(2)}, u32[]{:S(2)}) async-start(f32[32,40,256]{2,1,0:T(8,128)} %pad_maximum_fusion), calls=%async_computation | async-start | bytes 2621440 | tf_op jit(solution)/shard_map/all_to_all | solution.py:172
  56.1 28.7 %copy-start.2 = (f32[16,72,256]{2,1,0:T(8,128)S(1)}, f32[16,72,256]{2,1,0:T(8,128)}, u32[]{:S(2)}) copy-start(f32[16,72,256]{2,1,0:T(8,128)} %copy-done.1) | copy-start | bytes 3538948
  84.8 8.6 %copy-start.8 = (bf16[128,256]{1,0:T(8,128)(2,1)S(1)}, bf16[128,256]{1,0:T(8,128)(2,1)}, u32[]{:S(2)}) copy-start(bf16[128,256]{1,0:T(8,128)(2,1)} %param.15) | copy-start | bytes 196612
  87.1 10.1 %collective-permute-start.1 = (f32[16,64,256]{2,1,0:T(8,128)}, f32[16,64,256]{2,1,0:T(8,128)S(1)}, u32[]{:S(2)}, u32[]{:S(2)}) collective-permute-start(f32[16,64,256]{2,1,0:T(8,128)} %get-tuple-element.14), channel_id=1, source_target_pairs={{0,8},{8,0},{16,24},{24,16},{32,40},{40,32},{48,56},{56,48},{64,72... | collective-permute-start | bytes 3145736 | tf_op jit(solution)/shard_map/ppermute | solution.py:192
  91.9 5.4 %copy-start.6 = (bf16[128,2048]{0,1:T(8,128)(2,1)S(1)}, bf16[128,2048]{0,1:T(8,128)(2,1)}, u32[]{:S(2)}) copy-start(bf16[128,2048]{0,1:T(8,128)(2,1)} %copy-done.5) | copy-start | bytes 1572868
  91.9 5.4 %copy-start.7 = (f32[16,64,256]{2,1,0:T(8,128)S(1)}, f32[16,64,256]{2,1,0:T(8,128)}, u32[]{:S(2)}) copy-start(f32[16,64,256]{2,1,0:T(8,128)} %get-tuple-element.13) | copy-start | bytes 3145732
  91.9 5.4 %copy-start.11 = (f32[128,32]{0,1:T(8,128)S(1)}, f32[128,32]{0,1:T(8,128)}, u32[]{:S(2)}) copy-start(f32[128,32]{0,1:T(8,128)} %get-tuple-element.19) | copy-start | bytes 49156
  91.9 5.4 %copy-start.14 = (f32[32]{0:T(128)S(1)}, f32[32]{0:T(128)}, u32[]{:S(2)}) copy-start(f32[32]{0:T(128)} %param.18) | copy-start | bytes 388
  98.5 1.0 copy-start.4
  98.5 19.3 %copy-start.12 = (f32[2048]{0:T(1024)S(1)}, f32[2048]{0:T(1024)}, u32[]{:S(2)}) copy-start(f32[2048]{0:T(1024)} %param.19) | copy-start | bytes 24580
  118.2 3.9 %copy-start.3 = (bf16[128,2048]{1,0:T(8,128)(2,1)}, bf16[128,2048]{1,0:T(8,128)(2,1)S(1)}, u32[]{:S(2)}) copy-start(bf16[128,2048]{1,0:T(8,128)(2,1)S(1)} %multiply_convert_fusion) | copy-start | bytes 1572868
Sparse Core Ops, SparseCore 0:
  20.9 63.8 all-gather.1

commit v11 on v9

--- a/solution.py
+++ b/solution.py
@@ -189,6 +189,14 @@
         jnp.concatenate([kept, swapped], axis=0),
         jnp.concatenate([swapped, kept], axis=0),
     ).reshape(groups_dev, head_group, HEAD_DIM, STATE)
+    kv_local = jnp.concatenate(
+        [
+            keys.reshape(tok_rows, groups_dev, ATT_DIM),
+            values.reshape(tok_rows, groups_dev, ATT_DIM),
+        ],
+        axis=2,
+    )
+    kv_local, incoming = lax.optimization_barrier((kv_local, incoming))
     same_doc = (own_docs[:, None] == own_docs[None, :]) & (row_index[:, None] >= row_index[None, :])
     log_gap = cum_decay[:, :, :, None] - cum_decay[:, :, None, :]
     decay_matrix = jnp.exp(jnp.where(same_doc[None, None], log_gap, -jnp.inf))
@@ -220,13 +228,6 @@
     )
     query = query.astype(jnp.bfloat16).reshape(tok_rows, groups_dev, query_group, ATT_DIM)
 
-    kv_local = jnp.concatenate(
-        [
-            keys.reshape(tok_rows, groups_dev, ATT_DIM),
-            values.reshape(tok_rows, groups_dev, ATT_DIM),
-        ],
-        axis=2,
-    )
     kv_all = lax.all_gather(kv_local, "ctx", axis=0, tiled=True)
     doc_starts = jnp.cumsum(doc_lengths) - doc_lengths
     row_low = jnp.max(

time: 136 us -> 148 us (1.088); the launches traced: 135 us -> 146 us
  blocking collectives: 20 us -> 40.7 us
  starting transfers between devices: 14.6 us -> 8.23 us
  waiting for transfers between devices: 35.4 us -> 38.8 us
  Pallas kernels: 11.1 us -> 8.53 us
  between operations: 17.9 us -> 15.8 us
  other arithmetic: 13.7 us -> 12.2 us
    all_to_all x0 -> x1, blocking collectives: none -> 20.7 us  [shards(): lax.all_to_all(incoming_mine.reshape(ctx_count, part_rows, STATE), 'ctx',...]
    all_gather x1, waiting for transfers between devices: 0.74 us -> 16.2 us  [shards(): kv_all = lax.all_gather(kv_local, 'ctx', axis=0, tiled=True)]
    all_to_all x1 -> x0, waiting for transfers between devices: 14 us -> none  [shards(): lax.all_to_all(incoming_mine.reshape(ctx_count, part_rows, STATE), 'ctx',...]
    all_to_all x1 -> x0, starting transfers between devices: 6.21 us -> none  [shards(): lax.all_to_all(incoming_mine.reshape(ctx_count, part_rows, STATE), 'ctx',...]
    pallas_call x1, Pallas kernels: 11.1 us -> 8.53 us  [flash_attention(): pl.pallas_call(attention_kernel, grid_spec=grid_spec, out_shape=jax.Shape...]
    ppermute x1, waiting for transfers between devices: 0.01 us -> 1.98 us  [shards(): lax.ppermute(jnp.where(first_core, after_early, pair_incoming), 'ctx', pa...]
  transfers between devices with their start and end apart: 5 -> 4, of which waited for: 4 -> 4; matrix products, arithmetic and copies ran while one was open for 12% -> 9% of each run, Pallas kernels for 0% -> 0%
where the time goes in v11:
time: 148 us; the launch traced here: 146 us
  blocking collectives  40.7 us (28%)
  waiting for transfers between devices  38.8 us (26%)
  between operations  15.8 us (11%)
  matrix products  13.2 us (9%)
  other arithmetic  12.2 us (8%)
  Pallas kernels  8.53 us (6%)
  starting transfers between devices  8.23 us (6%)
  local copies, waits for them, and re-layouts  8.11 us (5%)
    all_to_all x1, blocking collectives, shards(): lax.all_to_all(incoming_mine.reshape(ctx_count, part_rows, STATE), 'ctx',...  20.7 us
    psum x1, blocking collectives, shards(): square_sum = lax.psum(square_local, 'head')  20 us
    all_to_all x1, waiting for transfers between devices, shards(): lax.all_to_all(payload, 'ctx', 0, 0, tiled=True)  17.5 us
    all_gather x1, waiting for transfers between devices, shards(): kv_all = lax.all_gather(kv_local, 'ctx', axis=0, tiled=True)  16.2 us
    pallas_call x1, Pallas kernels, flash_attention(): pl.pallas_call(attention_kernel, grid_spec=grid_spec, out_shape=jax.Shape...  8.53 us
    all_to_all x1, starting transfers between devices, shards(): lax.all_to_all(payload, 'ctx', 0, 0, tiled=True)  7.6 us
    dot_general x1, matrix products, shards(): jnp.einsum('tgf,gfo->tgo', mixer_out.reshape(tok_rows, groups_dev, -1), q...  3.82 us
    dot_general x1, matrix products, shards(): jnp.einsum('gjts,sgjp->tgjp', mixing, input_f32, precision=highest)  3.56 us
  transfers between devices with their start and end apart: 4, of which 4 were waited for; matrix products, arithmetic and copies ran while one was open for 9% of the time, Pallas kernels for 0%

profile of v11, /device:TPU:4, one launch (start us, length us, event | category | flops | bytes accessed | tf_op | source)
XLA Modules:
  0.0 145.6 jit_solution(5988761325225454866)
XLA Ops:
  7.2 0.0 copy-start
  7.2 0.7 copy.29
  8.0 0.1 reduce.2
  8.1 1.3 fusion.55
  9.4 0.1 fusion.52
  9.5 0.7 slice.36
  10.8 0.8 fusion.47
  11.7 0.2 slice_reduce_fusion
  11.9 1.3 copy.30
  13.2 0.0 copy-start.5
  13.2 0.7 compare_convert_fusion.1
  13.9 0.6 slice.37
  15.1 0.8 multiply_bitcast_fusion
  15.9 0.1 bitcast_multiply_fusion.1
  16.0 0.0 copy-done
  16.0 1.0 fusion.44
  17.0 0.0 copy-done.5
  17.0 0.1 broadcast_in_dim.67
  17.1 1.2 fusion.29
  18.4 0.0 collective-permute-start
  18.4 3.1 %collective-permute-done = f32[16,72,256]{2,1,0:T(8,128)S(1)} collective-permute-done((f32[16,72,256]{2,1,0:T(8,128)}, f32[16,72,256]{2,1,0:T(8,128)S(1)}, u32[]{:S(2)}, u32[]{:S(2)}) %collective-permute-start) | collective-permute-done | bytes 1179680 | tf_op jit(solution)/shard_map/ppermute | solution.py:142
  21.4 0.2 exponential_reduce_fusion
  21.6 0.1 broadcast_in_dim.68
  21.7 0.1 broadcast_in_dim.69
  21.8 0.3 select_add_fusion
  22.1 0.1 broadcast_in_dim.70
  22.2 1.2 pad_maximum_fusion
  23.4 0.0 copy-done.1
  23.4 7.6 %all-to-all-start = ((f32[32,40,256]{2,1,0:T(8,128)}), f32[32,40,256]{2,1,0:T(8,128)S(1)}, u32[]{:S(2)}, u32[]{:S(2)}) async-start(f32[32,40,256]{2,1,0:T(8,128)} %pad_maximum_fusion), calls=%async_computation | async-start | bytes 2621440 | tf_op jit(solution)/shard_map/all_to_all | solution.py:164
  31.0 0.0 all-gather.2.cloned.1.call-start
  31.1 17.5 %all-to-all-done = f32[32,40,256]{2,1,0:T(8,128)S(1)} async-done(((f32[32,40,256]{2,1,0:T(8,128)}), f32[32,40,256]{2,1,0:T(8,128)S(1)}, u32[]{:S(2)}, u32[]{:S(2)}) %all-to-all-start) | async-done | bytes 1310752 | tf_op jit(solution)/shard_map/all_to_all | solution.py:164
  48.6 1.1 slice.50
  49.8 0.1 copy.33
  49.8 0.2 select_reduce_fusion
  50.0 2.8 %convolution_bitcast_fusion = f32[16,2,32,256]{3,0,2,1:T(8,128)S(1)} fusion(f32[16,2,32,256]{3,2,1,0:T(8,128)} %slice.50, f32[2,16,16]{2,1,0:T(8,128)S(1)} %select_reduce_fusion, pred[16,16]{1,0:T(8,128)(4,1)S(1)} %iota_compare_fusion.5), kind=kOutput, calls=%fused_computation.17 | convolution fusion | flops 50332160 | bytes 2099456 | tf_op jit(solution)/shard_map/ukd,dupn->kupn/dot_general | solution.py:178
  52.8 0.0 copy-start.2
  52.8 0.6 copy.34
  53.4 20.7 %all_to_all.10 = f32[32,32,256]{2,1,0:T(8,128)S(1)} all-to-all(f32[32,32,256]{2,1,0:T(8,128)S(1)} %bitcast.108), channel_id=1, replica_groups=mesh['ctx'=32,'head'=8] {'ctx'}, dimensions={0} | all-to-all | bytes 2097152 | tf_op jit(solution)/shard_map/all_to_all | solution.py:179
  74.1 0.0 copy-done.2
  74.1 1.4 fusion.36
  75.5 0.6 collective-permute-start.1
  76.1 0.6 pad_maximum_fusion.1
  76.7 2.0 %collective-permute-done.1 = f32[16,64,256]{2,1,0:T(8,128)} collective-permute-done((f32[16,64,256]{2,1,0:T(8,128)}, f32[16,64,256]{2,1,0:T(8,128)}, u32[]{:S(2)}, u32[]{:S(2)}) %collective-permute-start.1) | collective-permute-done | bytes 1048608 | tf_op jit(solution)/shard_map/ppermute | solution.py:183
  78.7 1.9 %maximum_select_fusion = f32[1,32,64,256]{3,2,1,0:T(8,128)S(1)} fusion(f32[1,16,64,256]{3,2,1,0:T(8,128)} %bitcast.27, f32[1,16,64,256]{3,2,1,0:T(8,128)S(1)} %get-tuple-element.13, pred[]{:T(512)S(6)} %eq.45), kind=kLoop, calls=%fused_computation.6 | loop fusion | flops 1572864 | bytes 4194305 | tf_op jit(solution)/shard_map/jit(_where)/select_n | solution.py:187
  80.6 0.0 copy-start.6
  80.6 0.0 copy-start.10
  80.6 0.0 copy-start.12
  80.6 0.0 all-gather.2.cloned.1.call-update
  80.8 0.7 copy.36.low_ref
  81.5 0.6 pad_add_fusion.chunk_ref
  82.1 0.6 iota_add_fusion.high_ref
  82.7 0.1 fusion.46
  82.8 0.1 fusion.58
  82.9 1.1 fusion.22
  84.1 3.6 %fusion.19 = f32[128,1,32,64]{0,3,2,1:T(8,128)} fusion(f32[128,1,32,64]{0,3,2,1:T(8,128)S(1)} %fusion.22, bf16[128,32,64]{0,2,1:T(8,128)(2,1)S(1)} %bitcast.110, f32[32,128]{1,0:T(8,128)S(1)} %copy-done.10, f32[32,128]{1,0:T(8,128)S(1)} %bitcast.115, f32[128,128]{1,0:T(8,128)S(1)} %fusion.58, pred[128,128]{1,0:T(8,128)(4,1)S(1)} %fusion.46, ...), kind=kOutput, calls=%fused_computation.22 | convolution fusion | flops 405798912 | bytes 3260544 | tf_op jit(solution)/shard_map/gjts,sgjp->tgjp/dot_general | solution.py:207
  87.7 1.6 %copy.35 = f32[128,2048]{1,0:T(8,128)S(1)} copy(f32[128,2048]{0,1:T(8,128)} %bitcast.113) | data formatting | bytes 2097152 | tf_op jit(solution)/shard_map/reshape | solution.py:214
  89.3 0.4 multiply_reduce_fusion
  89.7 20.0 %psum.7 = f32[128]{0:T(128)S(1)} all-reduce(f32[128]{0:T(128)S(1)} %multiply_reduce_fusion), channel_id=1, replica_groups=mesh['ctx'=32,'head'=8] {'head'}, use_global_device_ids=true, to_apply=%region_5.6 | all-reduce | flops 128 | bytes 1024 | tf_op jit(solution)/shard_map/psum | solution.py:217
  109.8 0.0 copy-done.11
  109.8 0.4 multiply_convert_fusion
  110.2 0.0 copy-start.3
  110.2 3.8 %fusion.25.query_ref = bf16[128,1024]{1,0:T(8,128)(2,1)} fusion(bf16[128,2048]{1,0:T(8,128)(2,1)S(1)} %multiply_convert_fusion, bf16[1,2048,1024]{2,1,0:T(8,128)(2,1)} %param.20), kind=kOutput, calls=%fused_computation.24 | convolution fusion | flops 537001984 | bytes 4980736 | tf_op jit(solution)/shard_map/tgf,gfo->tgo/dot_general | solution.py:223
  114.0 16.2 %all-gather.2.cloned.1.call-done = bf16[4096,1,256]{2,0,1:T(8,128)(2,1)} async-done(((bf16[128,1,256]{2,0,1:T(8,128)(2,1)}), bf16[4096,1,256]{2,0,1:T(8,128)(2,1)}) %all-gather.2.cloned.1.call-update) | async-done | bytes 2097168 | tf_op jit(solution)/shard_map/all_gather | solution.py:231
  130.2 8.5 %shard_map.131 = bf16[128,1024]{1,0:T(8,128)(2,1)} custom-call(s32[2]{0:T(128)} %pad_add_fusion.chunk_ref, bf16[128,1024]{1,0:T(8,128)(2,1)} %fusion.25.query_ref, bf16[4096,256]{1,0:T(8,128)(2,1)} %bitcast.112, s32[128,1]{1,0:T(8,128)} %copy.36.low_ref, s32[128,1]{1,0:T(8,128)} %iota_add_fusion.high_ref), custom_call_target="tpu_custom_call" | custom-call | tf_op jit(solution)/shard_map/pallas_call | solution.py:85
  (24 shorter events, 0.1 us)
Async XLA Ops:
  7.2 8.9 %copy-start = (bf16[128,256]{1,0:T(8,128)(2,1)S(1)}, bf16[128,256]{1,0:T(8,128)(2,1)}, u32[]{:S(2)}) copy-start(bf16[128,256]{1,0:T(8,128)(2,1)} %param.14) | copy-start | bytes 196612
  13.2 3.8 %copy-start.5 = (bf16[128,2048]{0,1:T(8,128)(2,1)}, bf16[128,2048]{0,1:T(8,128)(2,1)S(1)}, u32[]{:S(2)}) copy-start(bf16[128,2048]{0,1:T(8,128)(2,1)S(1)} %copy.30) | copy-start | bytes 1572868
  18.4 3.1 %collective-permute-start = (f32[16,72,256]{2,1,0:T(8,128)}, f32[16,72,256]{2,1,0:T(8,128)S(1)}, u32[]{:S(2)}, u32[]{:S(2)}) collective-permute-start(f32[16,72,256]{2,1,0:T(8,128)} %get-tuple-element.17), channel_id=1, source_target_pairs={{0,8},{8,0},{16,24},{24,16},{32,40},{40,32},{48,56},{56,48},{64,72... | collective-permute-start | bytes 3538952 | tf_op jit(solution)/shard_map/ppermute | solution.py:142
  21.4 1.9 %copy-start.1 = (f32[16,72,256]{2,1,0:T(8,128)}, f32[16,72,256]{2,1,0:T(8,128)S(1)}, u32[]{:S(2)}) copy-start(f32[16,72,256]{2,1,0:T(8,128)S(1)} %collective-permute-done) | copy-start | bytes 3538948
  23.4 25.3 %all-to-all-start = ((f32[32,40,256]{2,1,0:T(8,128)}), f32[32,40,256]{2,1,0:T(8,128)S(1)}, u32[]{:S(2)}, u32[]{:S(2)}) async-start(f32[32,40,256]{2,1,0:T(8,128)} %pad_maximum_fusion), calls=%async_computation | async-start | bytes 2621440 | tf_op jit(solution)/shard_map/all_to_all | solution.py:164
  31.0 99.2 %all-gather.2.cloned.1.call-start = ((), (), s32[]{:S(2)}) async-start(), calls=%async_computation.2 | async-start | bytes 2162688 | tf_op jit(solution)/shard_map/all_gather | solution.py:231
  52.8 21.3 %copy-start.2 = (f32[16,72,256]{2,1,0:T(8,128)S(1)}, f32[16,72,256]{2,1,0:T(8,128)}, u32[]{:S(2)}) copy-start(f32[16,72,256]{2,1,0:T(8,128)} %copy-done.1) | copy-start | bytes 3538948
  74.1 1.9 %copy-start.8 = (bf16[128,128]{1,0:T(8,128)(2,1)S(1)}, bf16[128,128]{1,0:T(8,128)(2,1)}, u32[]{:S(2)}) copy-start(bf16[128,128]{1,0:T(8,128)(2,1)} %param.22) | copy-start | bytes 98308
  74.1 1.9 %copy-start.9 = (bf16[128,128]{1,0:T(8,128)(2,1)S(1)}, bf16[128,128]{1,0:T(8,128)(2,1)}, u32[]{:S(2)}) copy-start(bf16[128,128]{1,0:T(8,128)(2,1)} %param.21) | copy-start | bytes 98308
  75.5 3.2 %collective-permute-start.1 = (f32[16,64,256]{2,1,0:T(8,128)}, f32[16,64,256]{2,1,0:T(8,128)}, u32[]{:S(2)}, u32[]{:S(2)}) collective-permute-start(f32[16,64,256]{2,1,0:T(8,128)} %get-tuple-element.14), channel_id=1, source_target_pairs={{0,8},{8,0},{16,24},{24,16},{32,40},{40,32},{48,56},{56,48},{64,72... | collective-permute-start | bytes 3145736 | tf_op jit(solution)/shard_map/ppermute | solution.py:183
  78.7 4.1 %copy-start.7 = (bf16[128,256]{1,0:T(8,128)(2,1)S(1)}, bf16[128,256]{1,0:T(8,128)(2,1)}, u32[]{:S(2)}) copy-start(bf16[128,256]{1,0:T(8,128)(2,1)} %param.15) | copy-start | bytes 196612
  80.6 3.5 %copy-start.6 = (bf16[128,2048]{0,1:T(8,128)(2,1)S(1)}, bf16[128,2048]{0,1:T(8,128)(2,1)}, u32[]{:S(2)}) copy-start(bf16[128,2048]{0,1:T(8,128)(2,1)} %copy-done.5) | copy-start | bytes 1572868
  80.6 3.5 %copy-start.10 = (f32[32,128]{1,0:T(8,128)S(1)}, f32[32,128]{1,0:T(8,128)}, u32[]{:S(2)}) copy-start(f32[32,128]{1,0:T(8,128)} %param.16) | copy-start | bytes 49156
  80.6 3.5 %copy-start.12 = (f32[32]{0:T(128)S(1)}, f32[32]{0:T(128)}, u32[]{:S(2)}) copy-start(f32[32]{0:T(128)} %param.18) | copy-start | bytes 388
  87.7 1.6 %copy-start.4 = (bf16[128,2048]{1,0:T(8,128)(2,1)S(1)}, bf16[128,2048]{1,0:T(8,128)(2,1)}, u32[]{:S(2)}) copy-start(bf16[128,2048]{1,0:T(8,128)(2,1)} %param.13) | copy-start | bytes 1572868
  87.7 22.1 %copy-start.11 = (f32[2048]{0:T(1024)S(1)}, f32[2048]{0:T(1024)}, u32[]{:S(2)}) copy-start(f32[2048]{0:T(1024)} %param.19) | copy-start | bytes 24580
  110.2 3.8 %copy-start.3 = (bf16[128,2048]{1,0:T(8,128)(2,1)}, bf16[128,2048]{1,0:T(8,128)(2,1)S(1)}, u32[]{:S(2)}) copy-start(bf16[128,2048]{1,0:T(8,128)(2,1)S(1)} %multiply_convert_fusion) | copy-start | bytes 1572868
Sparse Core Ops, SparseCore 0:
  80.7 49.4 all-gather.1

commit v12 on v9

--- a/solution.py
+++ b/solution.py
@@ -34,33 +34,40 @@
     low = jnp.concatenate([low_ref[...]] * heads, axis=0)
     high = jnp.concatenate([high_ref[...]] * heads, axis=0)
 
-    def chunk_turn(turn, carried):
-        best_old, total_old, accum_old = carried
-        start = pl.multiple_of((chunk_ref[0] + turn) * KEY_CHUNK, KEY_CHUNK)
-        piece = kv_ref[pl.ds(start, KEY_CHUNK), :]
-        key_part = piece[:, :ATT_DIM]
-        value_part = piece[:, ATT_DIM:]
-        scores = lax.dot_general(
-            query_rows, key_part, (((1,), (1,)), ((), ())), preferred_element_type=jnp.float32
-        ) * ATT_DIM ** (-0.5)
-        key_pos = start + lax.broadcasted_iota(jnp.int32, (rows, KEY_CHUNK), 1)
-        visible = (key_pos >= low) & (key_pos <= high)
-        scores = jnp.where(visible, scores, -jnp.inf)
-        best_new = jnp.maximum(best_old, jnp.max(scores, axis=1, keepdims=True))
-        weights = jnp.exp(scores - best_new)
-        rescale = jnp.exp(best_old - best_new)
-        total_new = total_old * rescale + jnp.sum(weights, axis=1, keepdims=True)
-        accum_new = accum_old * rescale + jnp.dot(
-            weights.astype(jnp.bfloat16), value_part, preferred_element_type=jnp.float32
-        )
-        return (best_new, total_new, accum_new)
-
-    initial = (
+    def make_turn(base, masked):
+        def chunk_turn(turn, carried):
+            best_old, total_old, accum_old = carried
+            start = pl.multiple_of((base + turn) * KEY_CHUNK, KEY_CHUNK)
+            piece = kv_ref[pl.ds(start, KEY_CHUNK), :]
+            key_part = piece[:, :ATT_DIM]
+            value_part = piece[:, ATT_DIM:]
+            scores = lax.dot_general(
+                query_rows, key_part, (((1,), (1,)), ((), ())), preferred_element_type=jnp.float32
+            ) * ATT_DIM ** (-0.5)
+            if masked:
+                key_pos = start + lax.broadcasted_iota(jnp.int32, (rows, KEY_CHUNK), 1)
+                visible = (key_pos >= low) & (key_pos <= high)
+                scores = jnp.where(visible, scores, -jnp.inf)
+            best_new = jnp.maximum(best_old, jnp.max(scores, axis=1, keepdims=True))
+            weights = jnp.exp(scores - best_new)
+            rescale = jnp.exp(best_old - best_new)
+            total_new = total_old * rescale + jnp.sum(weights, axis=1, keepdims=True)
+            accum_new = accum_old * rescale + jnp.dot(
+                weights.astype(jnp.bfloat16), value_part, preferred_element_type=jnp.float32
+            )
+            return (best_new, total_new, accum_new)
+
+        return chunk_turn
+
+    carried = (
         jnp.full((rows, 1), NEG_FILL, jnp.float32),
         jnp.zeros((rows, 1), jnp.float32),
         jnp.zeros((rows, ATT_DIM), jnp.float32),
     )
-    _, total, accum = lax.fori_loop(0, chunk_ref[1], chunk_turn, initial)
+    carried = lax.fori_loop(0, chunk_ref[1], make_turn(chunk_ref[0], True), carried)
+    carried = lax.fori_loop(0, chunk_ref[3], make_turn(chunk_ref[2], False), carried)
+    carried = lax.fori_loop(0, chunk_ref[5], make_turn(chunk_ref[4], True), carried)
+    _, total, accum = carried
     result = (accum / total).astype(out_ref.dtype)
     for head in range(heads):
         out_ref[:, head * ATT_DIM : (head + 1) * ATT_DIM] = result[
@@ -70,7 +77,17 @@
 
 def flash_attention(query_rows, kv_rows, low, high, first_chunk, chunk_count):
     tokens = query_rows.shape[0]
-    chunk_info = jnp.stack([first_chunk, chunk_count]).astype(jnp.int32)
+    last_chunk = first_chunk + chunk_count - 1
+    inner_first = jnp.maximum(first_chunk, -(-jnp.max(low) // KEY_CHUNK))
+    inner_last = jnp.minimum(last_chunk, (jnp.min(high) + 1) // KEY_CHUNK - 1)
+    inner_count = jnp.maximum(inner_last - inner_first + 1, 0)
+    has_inner = inner_count > 0
+    front_count = jnp.where(has_inner, inner_first - first_chunk, chunk_count)
+    back_first = jnp.where(has_inner, inner_last + 1, last_chunk + 1)
+    back_count = last_chunk - back_first + 1
+    chunk_info = jnp.stack(
+        [first_chunk, front_count, inner_first, inner_count, back_first, back_count]
+    ).astype(jnp.int32)
     grid_spec = pltpu.PrefetchScalarGridSpec(
         num_scalar_prefetch=1,
         grid=(1,),

time: 136 us -> 138 us (1.015)
  between operations: 17.9 us -> 19.8 us
  transfers between devices with their start and end apart: 5 -> 5, of which waited for: 4 -> 3; matrix products, arithmetic and copies ran while one was open for 12% -> 12% of each run, Pallas kernels for 0% -> 0%
where the time goes in v12:
time: 138 us; the launch traced here: 137 us
  waiting for transfers between devices  34.7 us (25%)
  blocking collectives  20.2 us (15%)
  between operations  19.8 us (14%)
  starting transfers between devices  14.6 us (11%)
  other arithmetic  14 us (10%)
  matrix products  13.6 us (10%)
  Pallas kernels  11 us (8%)
  local copies, waits for them, and re-layouts  9.7 us (7%)
    psum x1, blocking collectives, shards(): square_sum = lax.psum(square_local, 'head')  20.2 us
    all_to_all x1, waiting for transfers between devices, shards(): lax.all_to_all(payload, 'ctx', 0, 0, tiled=True)  17.6 us
    all_to_all x1, waiting for transfers between devices, shards(): lax.all_to_all(incoming_mine.reshape(ctx_count, part_rows, STATE), 'ctx',...  14 us
    pallas_call x1, Pallas kernels, flash_attention(): pl.pallas_call(attention_kernel, grid_spec=grid_spec, out_shape=jax.Shape...  11 us
    all_to_all x1, starting transfers between devices, shards(): lax.all_to_all(payload, 'ctx', 0, 0, tiled=True)  7.6 us
    all_to_all x1, starting transfers between devices, shards(): lax.all_to_all(incoming_mine.reshape(ctx_count, part_rows, STATE), 'ctx',...  6.21 us
    dot_general x1, matrix products, shards(): jnp.einsum('tgf,gfo->tgo', mixer_out.reshape(tok_rows, groups_dev, -1), q...  3.89 us
    dot_general x1, matrix products, shards(): jnp.einsum('gjts,sgjp->tgjp', mixing, input_f32, precision=highest)  3.77 us
  transfers between devices with their start and end apart: 5, of which 3 were waited for; matrix products, arithmetic and copies ran while one was open for 12% of the time, Pallas kernels for 0%

profile of v12, /device:TPU:4, one launch (start us, length us, event | category | flops | bytes accessed | tf_op | source)
XLA Modules:
  0.0 137.5 jit_solution(14020743887185691514)
XLA Ops:
  7.2 0.0 copy-start
  7.2 0.7 iota_add_fusion.1
  7.9 0.7 copy.29
  8.7 0.1 reduce.5
  8.8 1.3 fusion.50
  10.1 0.7 select_reduce_fusion.1
  10.8 0.7 slice.36
  12.1 0.8 fusion.43
  13.0 0.2 slice_reduce_fusion
  13.2 1.3 copy.30
  14.5 0.0 copy-start.5
  14.5 0.7 compare_convert_fusion.1
  15.2 0.6 slice.37
  16.5 1.3 multiply_bitcast_fusion
  17.8 0.1 bitcast_multiply_fusion.1
  17.9 0.0 copy-done
  17.9 1.0 fusion.40
  18.9 0.1 broadcast_in_dim.67
  19.0 1.2 fusion.25
  20.2 0.0 collective-permute-start
  20.2 3.1 %collective-permute-done = f32[16,72,256]{2,1,0:T(8,128)S(1)} collective-permute-done((f32[16,72,256]{2,1,0:T(8,128)}, f32[16,72,256]{2,1,0:T(8,128)S(1)}, u32[]{:S(2)}, u32[]{:S(2)}) %collective-permute-start) | collective-permute-done | bytes 1179680 | tf_op jit(solution)/shard_map/ppermute | solution.py:159
  23.3 0.9 exponential_reduce_fusion
  24.2 0.1 broadcast_in_dim.68
  24.3 0.1 broadcast_in_dim.69
  24.4 0.3 select_add_fusion
  24.6 0.1 broadcast_in_dim.70
  24.7 1.2 pad_maximum_fusion
  25.9 7.6 %all-to-all-start = ((f32[32,40,256]{2,1,0:T(8,128)}), f32[32,40,256]{2,1,0:T(8,128)S(1)}, u32[]{:S(2)}, u32[]{:S(2)}) async-start(f32[32,40,256]{2,1,0:T(8,128)} %pad_maximum_fusion), calls=%async_computation | async-start | bytes 2621440 | tf_op jit(solution)/shard_map/all_to_all | solution.py:181
  33.6 17.6 %all-to-all-done = f32[32,40,256]{2,1,0:T(8,128)S(1)} async-done(((f32[32,40,256]{2,1,0:T(8,128)}), f32[32,40,256]{2,1,0:T(8,128)S(1)}, u32[]{:S(2)}, u32[]{:S(2)}) %all-to-all-start) | async-done | bytes 1310752 | tf_op jit(solution)/shard_map/all_to_all | solution.py:181
  51.2 1.1 slice.50
  52.3 0.1 copy.33
  52.4 0.2 select_reduce_fusion
  52.6 2.8 %convolution_bitcast_fusion = f32[16,2,32,256]{3,0,2,1:T(8,128)S(1)} fusion(f32[16,2,32,256]{3,2,1,0:T(8,128)} %slice.50, f32[2,16,16]{2,1,0:T(8,128)S(1)} %select_reduce_fusion, pred[16,16]{1,0:T(8,128)(4,1)S(1)} %iota_compare_fusion.5), kind=kOutput, calls=%fused_computation.21 | convolution fusion | flops 50332160 | bytes 2099456 | tf_op jit(solution)/shard_map/ukd,dupn->kupn/dot_general | solution.py:195
  55.3 0.0 copy-start.9
  55.3 0.0 copy-start.10
  55.4 0.0 copy-start.2
  55.4 1.6 %copy.34 = f32[16,2,32,256]{3,2,1,0:T(8,128)} copy(f32[16,2,32,256]{3,0,2,1:T(8,128)S(1)} %convolution_bitcast_fusion) | data formatting | bytes 2097152 | tf_op jit(solution)/shard_map/ukd,dupn->kupn/transpose | solution.py:195
  57.0 6.2 %all-to-all-start.1 = ((f32[32,32,256]{2,1,0:T(8,128)}), f32[32,32,256]{2,1,0:T(8,128)S(1)}, u32[]{:S(2)}, u32[]{:S(2)}) async-start(f32[32,32,256]{2,1,0:T(8,128)} %bitcast.22), calls=%async_computation.1 | async-start | bytes 2097152 | tf_op jit(solution)/shard_map/all_to_all | solution.py:196
  63.2 0.0 all-gather.2.cloned.1.call-start
  63.2 0.0 copy-done.9
  63.2 0.0 copy-done.10
  63.3 0.6 pad_maximum_fusion.1
  63.9 0.0 all-gather.2.cloned.1.call-update
  63.9 14.0 %all-to-all-done.1 = f32[32,32,256]{2,1,0:T(8,128)S(1)} async-done(((f32[32,32,256]{2,1,0:T(8,128)}), f32[32,32,256]{2,1,0:T(8,128)S(1)}, u32[]{:S(2)}, u32[]{:S(2)}) %all-to-all-start.1) | async-done | bytes 1048608 | tf_op jit(solution)/shard_map/all_to_all | solution.py:196
  77.9 2.4 %bitcast_select_fusion.1 = (f32[16,64,256]{2,1,0:T(8,128)}, f32[16,64,256]{2,1,0:T(8,128)}) fusion(f32[16]{0:T(128)} %get-tuple-element.2, pred[]{:T(512)S(6)} %eq.45, f32[16,72,256]{2,1,0:T(8,128)S(1)} %copy-done.2, f32[16,72,256]{2,1,0:T(8,128)S(1)} %get-tuple-element.15, f32[16,64,256]{2,1,0:T(8,128)S(1)} %bitcast.100), kind=kLoop, calls=%fused_computation.37 | loop fusion | flops 1310720 | bytes 5242945 | tf_op jit(solution)/shard_map/jit(_where)/select_n | solution.py:203
  80.3 0.7 collective-permute-start.1
  85.1 1.3 copy.36.low_ref
  86.5 0.6 stack.27.chunk_ref
  87.1 0.6 iota_add_fusion.high_ref
  87.7 0.8 fusion.42
  88.5 0.1 fusion.55
  88.6 3.8 %fusion.15 = f32[128,1,32,64]{0,3,2,1:T(8,128)S(1)} fusion(bf16[128,32,64]{0,2,1:T(8,128)(2,1)} %bitcast.101, f32[32,128]{1,0:T(8,128)} %param.16, f32[32,128]{1,0:T(8,128)S(1)} %bitcast.106, f32[128,128]{1,0:T(8,128)S(1)} %fusion.55, pred[128,128]{1,0:T(8,128)(4,1)S(1)} %fusion.42), kind=kOutput, calls=%fused_computation.20 | convolution fusion | flops 404750336 | bytes 1687552 | tf_op jit(solution)/shard_map/gjts,sgjp->tgjp/dot_general | solution.py:216
  92.4 0.0 collective-permute-done.1
  92.4 1.2 fusion.20
  93.6 0.0 copy-start.4
  93.7 0.0 copy-start.12
  93.7 0.3 copy.35
  94.0 0.7 copy-done.4
  94.7 0.4 multiply_reduce_fusion
  95.1 20.2 %psum.7 = f32[128]{0:T(128)S(1)} all-reduce(f32[128]{0:T(128)S(1)} %multiply_reduce_fusion), channel_id=1, replica_groups=mesh['ctx'=32,'head'=8] {'head'}, use_global_device_ids=true, to_apply=%region_5.6 | all-reduce | flops 128 | bytes 1024 | tf_op jit(solution)/shard_map/psum | solution.py:226
  115.3 0.4 multiply_convert_fusion
  115.7 0.0 copy-start.3
  115.7 3.9 %fusion.21.query_ref = bf16[128,1024]{1,0:T(8,128)(2,1)} fusion(bf16[128,2048]{1,0:T(8,128)(2,1)S(1)} %multiply_convert_fusion, bf16[1,2048,1024]{2,1,0:T(8,128)(2,1)} %param.20), kind=kOutput, calls=%fused_computation.28 | convolution fusion | flops 537001984 | bytes 4980736 | tf_op jit(solution)/shard_map/tgf,gfo->tgo/dot_general | solution.py:232
  119.6 11.0 %shard_map.131 = bf16[128,1024]{1,0:T(8,128)(2,1)} custom-call(s32[6]{0:T(128)} %stack.27.chunk_ref, bf16[128,1024]{1,0:T(8,128)(2,1)} %fusion.21.query_ref, bf16[4096,256]{1,0:T(8,128)(2,1)} %bitcast.103, s32[128,1]{1,0:T(8,128)} %copy.36.low_ref, s32[128,1]{1,0:T(8,128)} %iota_add_fusion.high_ref), custom_call_target="tpu_custom_call" | custom-call | tf_op jit(solution)/shard_map/pallas_call | solution.py:102
  (28 shorter events, 0.1 us)
Async XLA Ops:
  7.2 10.7 %copy-start = (bf16[128,256]{1,0:T(8,128)(2,1)S(1)}, bf16[128,256]{1,0:T(8,128)(2,1)}, u32[]{:S(2)}) copy-start(bf16[128,256]{1,0:T(8,128)(2,1)} %param.14) | copy-start | bytes 196612
  10.8 0.7 copy-start.13
  14.5 4.4 %copy-start.5 = (bf16[128,2048]{0,1:T(8,128)(2,1)}, bf16[128,2048]{0,1:T(8,128)(2,1)S(1)}, u32[]{:S(2)}) copy-start(bf16[128,2048]{0,1:T(8,128)(2,1)S(1)} %copy.30) | copy-start | bytes 1572868
  20.2 3.1 %collective-permute-start = (f32[16,72,256]{2,1,0:T(8,128)}, f32[16,72,256]{2,1,0:T(8,128)S(1)}, u32[]{:S(2)}, u32[]{:S(2)}) collective-permute-start(f32[16,72,256]{2,1,0:T(8,128)} %get-tuple-element.14), channel_id=1, source_target_pairs={{0,8},{8,0},{16,24},{24,16},{32,40},{40,32},{48,56},{56,48},{64,72... | collective-permute-start | bytes 3538952 | tf_op jit(solution)/shard_map/ppermute | solution.py:159
  23.2 2.7 %copy-start.1 = (f32[16,72,256]{2,1,0:T(8,128)}, f32[16,72,256]{2,1,0:T(8,128)S(1)}, u32[]{:S(2)}) copy-start(f32[16,72,256]{2,1,0:T(8,128)S(1)} %collective-permute-done) | copy-start | bytes 3538948
  25.9 25.3 %all-to-all-start = ((f32[32,40,256]{2,1,0:T(8,128)}), f32[32,40,256]{2,1,0:T(8,128)S(1)}, u32[]{:S(2)}, u32[]{:S(2)}) async-start(f32[32,40,256]{2,1,0:T(8,128)} %pad_maximum_fusion), calls=%async_computation | async-start | bytes 2621440 | tf_op jit(solution)/shard_map/all_to_all | solution.py:181
  55.3 7.9 %copy-start.9 = (bf16[128,128]{1,0:T(8,128)(2,1)S(1)}, bf16[128,128]{1,0:T(8,128)(2,1)}, u32[]{:S(2)}) copy-start(bf16[128,128]{1,0:T(8,128)(2,1)} %param.22) | copy-start | bytes 98308
  55.3 7.9 %copy-start.10 = (bf16[128,128]{1,0:T(8,128)(2,1)S(1)}, bf16[128,128]{1,0:T(8,128)(2,1)}, u32[]{:S(2)}) copy-start(bf16[128,128]{1,0:T(8,128)(2,1)} %param.21) | copy-start | bytes 98308
  55.4 22.6 %copy-start.2 = (f32[16,72,256]{2,1,0:T(8,128)S(1)}, f32[16,72,256]{2,1,0:T(8,128)}, u32[]{:S(2)}) copy-start(f32[16,72,256]{2,1,0:T(8,128)} %copy-done.1) | copy-start | bytes 3538948
  57.0 21.0 %all-to-all-start.1 = ((f32[32,32,256]{2,1,0:T(8,128)}), f32[32,32,256]{2,1,0:T(8,128)S(1)}, u32[]{:S(2)}, u32[]{:S(2)}) async-start(f32[32,32,256]{2,1,0:T(8,128)} %bitcast.22), calls=%async_computation.1 | async-start | bytes 2097152 | tf_op jit(solution)/shard_map/all_to_all | solution.py:196
  63.2 56.5 %all-gather.2.cloned.1.call-start = ((), (), s32[]{:S(2)}) async-start(), calls=%async_computation.2 | async-start | bytes 2162688 | tf_op jit(solution)/shard_map/all_gather | solution.py:247
  77.9 10.5 %copy-start.8 = (bf16[128,256]{1,0:T(8,128)(2,1)S(1)}, bf16[128,256]{1,0:T(8,128)(2,1)}, u32[]{:S(2)}) copy-start(bf16[128,256]{1,0:T(8,128)(2,1)} %param.15) | copy-start | bytes 196612
  80.3 12.1 %collective-permute-start.1 = (f32[16,64,256]{2,1,0:T(8,128)}, f32[16,64,256]{2,1,0:T(8,128)S(1)}, u32[]{:S(2)}, u32[]{:S(2)}) collective-permute-start(f32[16,64,256]{2,1,0:T(8,128)} %get-tuple-element.11), channel_id=1, source_target_pairs={{0,8},{8,0},{16,24},{24,16},{32,40},{40,32},{48,56},{56,48},{64,72... | collective-permute-start | bytes 3145736 | tf_op jit(solution)/shard_map/ppermute | solution.py:200
  87.1 5.3 %copy-start.6 = (bf16[128,2048]{0,1:T(8,128)(2,1)S(1)}, bf16[128,2048]{0,1:T(8,128)(2,1)}, u32[]{:S(2)}) copy-start(bf16[128,2048]{0,1:T(8,128)(2,1)} %copy-done.5) | copy-start | bytes 1572868
  87.1 5.3 %copy-start.7 = (f32[16,64,256]{2,1,0:T(8,128)S(1)}, f32[16,64,256]{2,1,0:T(8,128)}, u32[]{:S(2)}) copy-start(f32[16,64,256]{2,1,0:T(8,128)} %get-tuple-element.10) | copy-start | bytes 3145732
  87.1 5.3 %copy-start.11 = (f32[128,32]{0,1:T(8,128)S(1)}, f32[128,32]{0,1:T(8,128)}, u32[]{:S(2)}) copy-start(f32[128,32]{0,1:T(8,128)} %get-tuple-element.16) | copy-start | bytes 49156
  87.1 5.4 %copy-start.14 = (f32[32]{0:T(128)S(1)}, f32[32]{0:T(128)}, u32[]{:S(2)}) copy-start(f32[32]{0:T(128)} %param.18) | copy-start | bytes 388
  93.6 1.0 copy-start.4
  93.7 21.7 %copy-start.12 = (f32[2048]{0:T(1024)S(1)}, f32[2048]{0:T(1024)}, u32[]{:S(2)}) copy-start(f32[2048]{0:T(1024)} %param.19) | copy-start | bytes 24580
  115.7 3.9 %copy-start.3 = (bf16[128,2048]{1,0:T(8,128)(2,1)}, bf16[128,2048]{1,0:T(8,128)(2,1)S(1)}, u32[]{:S(2)}) copy-start(bf16[128,2048]{1,0:T(8,128)(2,1)S(1)} %multiply_convert_fusion) | copy-start | bytes 1572868
Sparse Core Ops, SparseCore 0:
  67.2 51.0 all-gather.1

commit v13 on v9

--- a/solution.py
+++ b/solution.py
@@ -164,6 +164,15 @@
     gathered = lax.all_to_all(payload, "ctx", 0, 0, tiled=True).reshape(
         pair_count, 2, part_rows + 8, STATE
     )
+    same_doc = (own_docs[:, None] == own_docs[None, :]) & (row_index[:, None] >= row_index[None, :])
+    log_gap = cum_decay[:, :, :, None] - cum_decay[:, :, None, :]
+    decay_matrix = jnp.exp(jnp.where(same_doc[None, None], log_gap, -jnp.inf))
+    pair_products = jnp.einsum(
+        "tgn,sgn->gts", state_out, state_in, preferred_element_type=jnp.float32
+    )
+    mixing = pair_products[:, None] * decay_matrix * step_rows[:, :, None, :]
+    local_out = jnp.einsum("gjts,sgjp->tgjp", mixing, input_f32, precision=highest)
+    gathered, local_out = lax.optimization_barrier((gathered, local_out))
     states_mine = gathered[:, :, :part_rows, :]
     mine_log = gathered[:, :, part_rows, 0]
     block_row = jnp.arange(pair_count, dtype=jnp.int32)
@@ -189,14 +198,6 @@
         jnp.concatenate([kept, swapped], axis=0),
         jnp.concatenate([swapped, kept], axis=0),
     ).reshape(groups_dev, head_group, HEAD_DIM, STATE)
-    same_doc = (own_docs[:, None] == own_docs[None, :]) & (row_index[:, None] >= row_index[None, :])
-    log_gap = cum_decay[:, :, :, None] - cum_decay[:, :, None, :]
-    decay_matrix = jnp.exp(jnp.where(same_doc[None, None], log_gap, -jnp.inf))
-    pair_products = jnp.einsum(
-        "tgn,sgn->gts", state_out, state_in, preferred_element_type=jnp.float32
-    )
-    mixing = pair_products[:, None] * decay_matrix * step_rows[:, :, None, :]
-    local_out = jnp.einsum("gjts,sgjp->tgjp", mixing, input_f32, precision=highest)
     carry_weight = jnp.exp(cum_decay) * carry_mask[None, None, :]
     carried_out = (
         jnp.einsum("tgn,gjpn->tgjp", state_out.astype(jnp.float32), incoming, precision=highest)

time: 136 us -> 132 us (0.971)
  waiting for transfers between devices: 35.4 us -> 33.5 us
  Pallas kernels: 11.1 us -> 9.4 us
    all_to_all x1, waiting for transfers between devices: 17.6 us -> 13.8 us  [shards(): lax.all_to_all(payload, 'ctx', 0, 0, tiled=True)]
    all_gather x1, waiting for transfers between devices: 0.74 us -> 3.36 us  [shards(): kv_all = lax.all_gather(kv_local, 'ctx', axis=0, tiled=True)]
    dot_general x1, matrix products: 1.2 us -> 3.16 us  [shards(): jnp.einsum('tgn,gjpn->tgjp', state_out.astype(jnp.float32), incoming, pre...]
    pallas_call x1, Pallas kernels: 11.1 us -> 9.4 us  [flash_attention(): pl.pallas_call(attention_kernel, grid_spec=grid_spec, out_shape=jax.Shape...]
  transfers between devices with their start and end apart: 5 -> 5, of which waited for: 4 -> 4; matrix products, arithmetic and copies ran while one was open for 12% -> 14% of each run, Pallas kernels for 0% -> 0%
where the time goes in v13:
time: 132 us; the launch traced here: 131 us
  waiting for transfers between devices  33.5 us (25%)
  blocking collectives  20 us (15%)
  between operations  18 us (14%)
  starting transfers between devices  14.7 us (11%)
  matrix products  14.2 us (11%)
  other arithmetic  13.4 us (10%)
  Pallas kernels  9.4 us (7%)
  local copies, waits for them, and re-layouts  7.88 us (6%)
    psum x1, blocking collectives, shards(): square_sum = lax.psum(square_local, 'head')  20 us
    all_to_all x1, waiting for transfers between devices, shards(): lax.all_to_all(payload, 'ctx', 0, 0, tiled=True)  13.8 us
    all_to_all x1, waiting for transfers between devices, shards(): lax.all_to_all(incoming_mine.reshape(ctx_count, part_rows, STATE), 'ctx',...  13.3 us
    pallas_call x1, Pallas kernels, flash_attention(): pl.pallas_call(attention_kernel, grid_spec=grid_spec, out_shape=jax.Shape...  9.4 us
    all_to_all x1, starting transfers between devices, shards(): lax.all_to_all(payload, 'ctx', 0, 0, tiled=True)  7.73 us
    all_to_all x1, starting transfers between devices, shards(): lax.all_to_all(incoming_mine.reshape(ctx_count, part_rows, STATE), 'ctx',...  6.21 us
    dot_general x1, matrix products, shards(): jnp.einsum('tgf,gfo->tgo', mixer_out.reshape(tok_rows, groups_dev, -1), q...  3.89 us
    dot_general x1, matrix products, shards(): jnp.einsum('gjts,sgjp->tgjp', mixing, input_f32, precision=highest)  3.52 us
  transfers between devices with their start and end apart: 5, of which 4 were waited for; matrix products, arithmetic and copies ran while one was open for 14% of the time, Pallas kernels for 0%

profile of v13, /device:TPU:4, one launch (start us, length us, event | category | flops | bytes accessed | tf_op | source)
XLA Modules:
  0.0 131.0 jit_solution(17779235960448777501)
XLA Ops:
  7.2 0.0 copy-start
  7.2 0.7 copy.30
  8.0 0.1 reduce.3
  8.1 1.3 fusion.51
  10.0 0.6 fusion.48
  10.7 0.6 slice.36
  11.2 0.8 fusion.42
  12.1 0.2 slice_reduce_fusion
  12.3 1.3 %copy.29 = bf16[128,2048]{0,1:T(8,128)(2,1)S(1)} copy(bf16[128,2048]{1,0:T(8,128)(2,1)} %param.12) | data formatting | bytes 1048576 | tf_op args[0]
  13.6 0.0 copy-start.5
  13.6 0.7 compare_convert_fusion.1
  14.3 0.6 slice.37
  15.6 0.8 multiply_bitcast_fusion
  16.4 0.1 bitcast_multiply_fusion.1
  16.4 0.0 copy-done
  16.4 1.0 fusion.40
  17.4 0.0 copy-done.5
  17.4 0.1 broadcast_in_dim.65
  17.6 1.3 fusion.26
  18.8 0.0 collective-permute-start
  18.8 3.1 %collective-permute-done = f32[16,72,256]{2,1,0:T(8,128)S(1)} collective-permute-done((f32[16,72,256]{2,1,0:T(8,128)}, f32[16,72,256]{2,1,0:T(8,128)S(1)}, u32[]{:S(2)}, u32[]{:S(2)}) %collective-permute-start) | collective-permute-done | bytes 1179680 | tf_op jit(solution)/shard_map/ppermute | solution.py:142
  21.9 1.0 exponential_reduce_fusion
  22.9 0.1 broadcast_in_dim.66
  22.9 0.1 broadcast_in_dim.67
  23.0 0.3 select_add_fusion
  23.3 0.1 broadcast_in_dim.68
  23.4 0.0 copy-start.7
  23.4 1.2 pad_maximum_fusion
  24.6 0.0 copy-done.1
  24.6 7.7 %all-to-all-start = ((f32[32,40,256]{2,1,0:T(8,128)}), f32[32,40,256]{2,1,0:T(8,128)S(1)}, u32[]{:S(2)}, u32[]{:S(2)}) async-start(f32[32,40,256]{2,1,0:T(8,128)} %pad_maximum_fusion), calls=%async_computation | async-start | bytes 2621440 | tf_op jit(solution)/shard_map/all_to_all | solution.py:164
  32.4 0.1 fusion.43
  32.5 0.0 copy-done.7
  32.5 0.1 fusion.55
  32.6 0.0 copy-done.6
  32.7 0.0 copy-done.8
  32.7 3.5 %fusion.15 = f32[128,1,32,64]{0,3,2,1:T(8,128)} fusion(bf16[128,32,64]{0,2,1:T(8,128)(2,1)S(1)} %bitcast.98, f32[32,128]{1,0:T(8,128)S(1)} %copy-done.8, f32[32,128]{1,0:T(8,128)S(1)} %bitcast.102, f32[128,128]{1,0:T(8,128)S(1)} %fusion.55, pred[128,128]{1,0:T(8,128)(4,1)S(1)} %fusion.43), kind=kOutput, calls=%fused_computation.20 | convolution fusion | flops 404750336 | bytes 1687552 | tf_op jit(solution)/shard_map/gjts,sgjp->tgjp/dot_general | solution.py:174
  36.2 13.8 %all-to-all-done = f32[32,40,256]{2,1,0:T(8,128)S(1)} async-done(((f32[32,40,256]{2,1,0:T(8,128)}), f32[32,40,256]{2,1,0:T(8,128)S(1)}, u32[]{:S(2)}, u32[]{:S(2)}) %all-to-all-start) | async-done | bytes 1310752 | tf_op jit(solution)/shard_map/all_to_all | solution.py:164
  50.0 0.1 copy.33
  50.1 0.2 select_reduce_fusion
  50.3 1.7 %convolution_bitcast_fusion = f32[16,2,32,256]{3,0,2,1:T(8,128)S(1)} fusion(f32[16,2,40,256]{3,2,1,0:T(8,128)S(1)} %bitcast.93, f32[2,16,16]{2,1,0:T(8,128)S(1)} %select_reduce_fusion, pred[16,16]{1,0:T(8,128)(4,1)S(1)} %iota_compare_fusion.5), kind=kOutput, calls=%fused_computation.21 | convolution fusion | flops 50332160 | bytes 2361600 | tf_op jit(solution)/shard_map/ukd,dupn->kupn/dot_general | solution.py:187
  51.9 1.6 %copy.34 = f32[16,2,32,256]{3,2,1,0:T(8,128)} copy(f32[16,2,32,256]{3,0,2,1:T(8,128)S(1)} %convolution_bitcast_fusion) | data formatting | bytes 2097152 | tf_op jit(solution)/shard_map/ukd,dupn->kupn/transpose | solution.py:187
  53.5 6.2 %all-to-all-start.1 = ((f32[32,32,256]{2,1,0:T(8,128)}), f32[32,32,256]{2,1,0:T(8,128)S(1)}, u32[]{:S(2)}, u32[]{:S(2)}) async-start(f32[32,32,256]{2,1,0:T(8,128)} %bitcast.22), calls=%async_computation.1 | async-start | bytes 2097152 | tf_op jit(solution)/shard_map/all_to_all | solution.py:188
  59.7 0.0 all-gather.2.cloned.1.call-start
  59.8 1.4 %pad_maximum_fusion.1 = bf16[128,1,256]{2,0,1:T(8,128)(2,1)} fusion(bf16[128,1,128]{2,0,1:T(8,128)(2,1)} %bitcast.103, bf16[128,1,128]{2,0,1:T(8,128)(2,1)} %bitcast.104), kind=kLoop, calls=%fused_computation.53 | loop fusion | flops 131072 | bytes 131072 | tf_op jit(solution)/shard_map/concatenate | solution.py:224
  61.2 0.0 all-gather.2.cloned.1.call-update
  61.2 13.3 %all-to-all-done.1 = f32[32,32,256]{2,1,0:T(8,128)S(1)} async-done(((f32[32,32,256]{2,1,0:T(8,128)}), f32[32,32,256]{2,1,0:T(8,128)S(1)}, u32[]{:S(2)}, u32[]{:S(2)}) %all-to-all-start.1) | async-done | bytes 1048608 | tf_op jit(solution)/shard_map/all_to_all | solution.py:188
  74.5 2.4 %bitcast_select_fusion.1 = (f32[16,64,256]{2,1,0:T(8,128)}, f32[16,64,256]{2,1,0:T(8,128)}) fusion(f32[16]{0:T(128)} %get-tuple-element.6, pred[]{:T(512)S(6)} %eq.42, f32[16,72,256]{2,1,0:T(8,128)S(1)} %copy-done.2, f32[16,72,256]{2,1,0:T(8,128)S(1)} %get-tuple-element.18, f32[16,64,256]{2,1,0:T(8,128)S(1)} %bitcast.96), kind=kLoop, calls=%fused_computation.37 | loop fusion | flops 1310720 | bytes 5242945 | tf_op jit(solution)/shard_map/jit(_where)/select_n | solution.py:195
  76.9 0.7 collective-permute-start.1
  79.9 1.3 %copy.36.low_ref = s32[128,1]{1,0:T(8,128)} copy(s32[128,1]{0,1:T(1,128)} %bitcast.109) | data formatting | bytes 1024 | tf_op jit(solution)/shard_map/broadcast_in_dim | solution.py:244
  81.2 0.6 pad_add_fusion.chunk_ref
  81.8 0.6 iota_add_fusion.high_ref
  82.5 0.0 collective-permute-done.1
  82.5 3.2 %fusion.20 = f32[128,1,32,64]{0,3,2,1:T(8,128)S(1)} fusion(f32[128,1,32,64]{0,3,2,1:T(8,128)} %fusion.15, f32[16,64,256]{2,1,0:T(8,128)S(1)} %collective-permute-done.1, f32[16,64,256]{2,1,0:T(8,128)} %get-tuple-element.13, pred[]{:T(512)S(6)} %eq.42, f32[32]{0:T(128)} %param.18, f32[128,32]{0,1:T(8,128)S(1)} %get-tuple-element.19, ...), kind=kOutput, calls=%fused_computation.24 | convolution fusion | flops 808189952 | bytes 4800641 | tf_op jit(solution)/shard_map/tgn,gjpn->tgjp/dot_general | solution.py:203
  85.6 0.0 copy-start.4
  85.6 0.0 copy-start.9
  85.6 0.3 copy.35
  86.0 0.7 copy-done.4
  86.7 0.4 multiply_reduce_fusion
  87.1 20.0 %psum.7 = f32[128]{0:T(128)S(1)} all-reduce(f32[128]{0:T(128)S(1)} %multiply_reduce_fusion), channel_id=1, replica_groups=mesh['ctx'=32,'head'=8] {'head'}, use_global_device_ids=true, to_apply=%region_5.6 | all-reduce | flops 128 | bytes 1024 | tf_op jit(solution)/shard_map/psum | solution.py:210
  107.1 0.4 multiply_convert_fusion
  107.5 0.0 copy-start.3
  107.5 3.9 %fusion.22.query_ref = bf16[128,1024]{1,0:T(8,128)(2,1)} fusion(bf16[128,2048]{1,0:T(8,128)(2,1)S(1)} %multiply_convert_fusion, bf16[1,2048,1024]{2,1,0:T(8,128)(2,1)} %param.20), kind=kOutput, calls=%fused_computation.29 | convolution fusion | flops 537001984 | bytes 4980736 | tf_op jit(solution)/shard_map/tgf,gfo->tgo/dot_general | solution.py:216
  111.4 3.4 %all-gather.2.cloned.1.call-done = bf16[4096,1,256]{2,0,1:T(8,128)(2,1)} async-done(((bf16[128,1,256]{2,0,1:T(8,128)(2,1)}), bf16[4096,1,256]{2,0,1:T(8,128)(2,1)}) %all-gather.2.cloned.1.call-update) | async-done | bytes 2097168 | tf_op jit(solution)/shard_map/all_gather | solution.py:231
  114.8 9.4 %shard_map.131 = bf16[128,1024]{1,0:T(8,128)(2,1)} custom-call(s32[2]{0:T(128)} %pad_add_fusion.chunk_ref, bf16[128,1024]{1,0:T(8,128)(2,1)} %fusion.22.query_ref, bf16[4096,256]{1,0:T(8,128)(2,1)} %bitcast.99, s32[128,1]{1,0:T(8,128)} %copy.36.low_ref, s32[128,1]{1,0:T(8,128)} %iota_add_fusion.high_ref), custom_call_target="tpu_custom_call" | custom-call | tf_op jit(solution)/shard_map/pallas_call | solution.py:85
  (17 shorter events, 0.1 us)
Async XLA Ops:
  7.2 9.3 %copy-start = (bf16[128,256]{1,0:T(8,128)(2,1)S(1)}, bf16[128,256]{1,0:T(8,128)(2,1)}, u32[]{:S(2)}) copy-start(bf16[128,256]{1,0:T(8,128)(2,1)} %param.14) | copy-start | bytes 196612
  13.6 3.8 %copy-start.5 = (bf16[128,2048]{0,1:T(8,128)(2,1)}, bf16[128,2048]{0,1:T(8,128)(2,1)S(1)}, u32[]{:S(2)}) copy-start(bf16[128,2048]{0,1:T(8,128)(2,1)S(1)} %copy.29) | copy-start | bytes 1572868
  18.8 3.1 %collective-permute-start = (f32[16,72,256]{2,1,0:T(8,128)}, f32[16,72,256]{2,1,0:T(8,128)S(1)}, u32[]{:S(2)}, u32[]{:S(2)}) collective-permute-start(f32[16,72,256]{2,1,0:T(8,128)} %get-tuple-element.17), channel_id=1, source_target_pairs={{0,8},{8,0},{16,24},{24,16},{32,40},{40,32},{48,56},{56,48},{64,72... | collective-permute-start | bytes 3538952 | tf_op jit(solution)/shard_map/ppermute | solution.py:142
  21.9 2.7 %copy-start.1 = (f32[16,72,256]{2,1,0:T(8,128)}, f32[16,72,256]{2,1,0:T(8,128)S(1)}, u32[]{:S(2)}) copy-start(f32[16,72,256]{2,1,0:T(8,128)S(1)} %collective-permute-done) | copy-start | bytes 3538948
  23.4 9.1 %copy-start.7 = (bf16[128,256]{1,0:T(8,128)(2,1)S(1)}, bf16[128,256]{1,0:T(8,128)(2,1)}, u32[]{:S(2)}) copy-start(bf16[128,256]{1,0:T(8,128)(2,1)} %param.15) | copy-start | bytes 196612
  24.6 8.1 %copy-start.6 = (bf16[128,2048]{0,1:T(8,128)(2,1)S(1)}, bf16[128,2048]{0,1:T(8,128)(2,1)}, u32[]{:S(2)}) copy-start(bf16[128,2048]{0,1:T(8,128)(2,1)} %copy-done.5) | copy-start | bytes 1572868
  24.6 8.1 %copy-start.8 = (f32[32,128]{1,0:T(8,128)S(1)}, f32[32,128]{1,0:T(8,128)}, u32[]{:S(2)}) copy-start(f32[32,128]{1,0:T(8,128)} %param.16) | copy-start | bytes 49156
  24.6 25.4 %all-to-all-start = ((f32[32,40,256]{2,1,0:T(8,128)}), f32[32,40,256]{2,1,0:T(8,128)S(1)}, u32[]{:S(2)}, u32[]{:S(2)}) async-start(f32[32,40,256]{2,1,0:T(8,128)} %pad_maximum_fusion), calls=%async_computation | async-start | bytes 2621440 | tf_op jit(solution)/shard_map/all_to_all | solution.py:164
  51.9 22.6 %copy-start.2 = (f32[16,72,256]{2,1,0:T(8,128)S(1)}, f32[16,72,256]{2,1,0:T(8,128)}, u32[]{:S(2)}) copy-start(f32[16,72,256]{2,1,0:T(8,128)} %copy-done.1) | copy-start | bytes 3538948
  53.5 21.0 %all-to-all-start.1 = ((f32[32,32,256]{2,1,0:T(8,128)}), f32[32,32,256]{2,1,0:T(8,128)S(1)}, u32[]{:S(2)}, u32[]{:S(2)}) async-start(f32[32,32,256]{2,1,0:T(8,128)} %bitcast.22), calls=%async_computation.1 | async-start | bytes 2097152 | tf_op jit(solution)/shard_map/all_to_all | solution.py:188
  59.7 55.0 %all-gather.2.cloned.1.call-start = ((), (), s32[]{:S(2)}) async-start(), calls=%async_computation.2 | async-start | bytes 2162688 | tf_op jit(solution)/shard_map/all_gather | solution.py:231
  76.9 5.6 %collective-permute-start.1 = (f32[16,64,256]{2,1,0:T(8,128)}, f32[16,64,256]{2,1,0:T(8,128)S(1)}, u32[]{:S(2)}, u32[]{:S(2)}) collective-permute-start(f32[16,64,256]{2,1,0:T(8,128)} %get-tuple-element.14), channel_id=1, source_target_pairs={{0,8},{8,0},{16,24},{24,16},{32,40},{40,32},{48,56},{56,48},{64,72... | collective-permute-start | bytes 3145736 | tf_op jit(solution)/shard_map/ppermute | solution.py:192
  85.6 1.0 copy-start.4
  85.6 21.5 %copy-start.9 = (f32[2048]{0:T(1024)S(1)}, f32[2048]{0:T(1024)}, u32[]{:S(2)}) copy-start(f32[2048]{0:T(1024)} %param.19) | copy-start | bytes 24580
  107.5 3.9 %copy-start.3 = (bf16[128,2048]{1,0:T(8,128)(2,1)}, bf16[128,2048]{1,0:T(8,128)(2,1)S(1)}, u32[]{:S(2)}) copy-start(bf16[128,2048]{1,0:T(8,128)(2,1)S(1)} %multiply_convert_fusion) | copy-start | bytes 1572868
Sparse Core Ops, SparseCore 0:
  63.7 51.0 all-gather.1

commit v14 on v13

--- a/solution.py
+++ b/solution.py
@@ -193,10 +193,8 @@
         jnp.where(first_core, after_early, pair_incoming), "ctx", pair_swap
     )
     kept = jnp.where(first_core, pair_incoming, after_early)
-    incoming = jnp.where(
-        first_core,
-        jnp.concatenate([kept, swapped], axis=0),
-        jnp.concatenate([swapped, kept], axis=0),
+    incoming = lax.dynamic_slice_in_dim(
+        jnp.concatenate([swapped, kept, swapped], axis=0), (1 - core) * half_heads, heads_dev, 0
     ).reshape(groups_dev, head_group, HEAD_DIM, STATE)
     carry_weight = jnp.exp(cum_decay) * carry_mask[None, None, :]
     carried_out = (

time: 132 us -> 134 us (1.015)
  Pallas kernels: 9.4 us -> 11.1 us
    pallas_call x1, Pallas kernels: 9.4 us -> 11.1 us  [flash_attention(): pl.pallas_call(attention_kernel, grid_spec=grid_spec, out_shape=jax.Shape...]
where the time goes in v14:
time: 134 us; the launch traced here: 133 us
  waiting for transfers between devices  33.7 us (25%)
  blocking collectives  20 us (15%)
  between operations  18 us (13%)
  starting transfers between devices  14.7 us (11%)
  matrix products  14 us (10%)
  other arithmetic  13.4 us (10%)
  Pallas kernels  11.1 us (8%)
  local copies, waits for them, and re-layouts  7.88 us (6%)
    psum x1, blocking collectives, shards(): square_sum = lax.psum(square_local, 'head')  20 us
    all_to_all x1, waiting for transfers between devices, shards(): lax.all_to_all(payload, 'ctx', 0, 0, tiled=True)  13.8 us
    all_to_all x1, waiting for transfers between devices, shards(): lax.all_to_all(incoming_mine.reshape(ctx_count, part_rows, STATE), 'ctx',...  13.3 us
    pallas_call x1, Pallas kernels, flash_attention(): pl.pallas_call(attention_kernel, grid_spec=grid_spec, out_shape=jax.Shape...  11.1 us
    all_to_all x1, starting transfers between devices, shards(): lax.all_to_all(payload, 'ctx', 0, 0, tiled=True)  7.73 us
    all_to_all x1, starting transfers between devices, shards(): lax.all_to_all(incoming_mine.reshape(ctx_count, part_rows, STATE), 'ctx',...  6.21 us
    dot_general x1, matrix products, shards(): jnp.einsum('tgf,gfo->tgo', mixer_out.reshape(tok_rows, groups_dev, -1), q...  3.85 us
    dot_general x1, matrix products, shards(): jnp.einsum('gjts,sgjp->tgjp', mixing, input_f32, precision=highest)  3.52 us
  transfers between devices with their start and end apart: 5, of which 4 were waited for; matrix products, arithmetic and copies ran while one was open for 14% of the time, Pallas kernels for 0%

profile of v14, /device:TPU:4, one launch (start us, length us, event | category | flops | bytes accessed | tf_op | source)
XLA Modules:
  0.0 132.8 jit_solution(3113946673362646475)
XLA Ops:
  7.2 0.0 copy-start
  7.2 0.7 copy.30
  8.0 0.1 reduce.3
  8.1 1.3 fusion.57
  10.0 0.6 fusion.53
  10.7 0.6 slice.36
  11.2 0.8 fusion.47
  12.1 0.2 slice_reduce_fusion
  12.3 1.3 copy.29
  13.6 0.0 copy-start.5
  13.6 0.7 compare_convert_fusion.1
  14.3 0.6 slice.37
  15.6 0.8 multiply_bitcast_fusion
  16.4 0.1 bitcast_multiply_fusion.1
  16.4 0.0 copy-done
  16.4 1.0 fusion.45
  17.4 0.0 copy-done.5
  17.4 0.1 broadcast_in_dim.65
  17.6 1.3 fusion.32
  18.8 0.0 collective-permute-start
  18.8 3.1 %collective-permute-done = f32[16,72,256]{2,1,0:T(8,128)S(1)} collective-permute-done((f32[16,72,256]{2,1,0:T(8,128)}, f32[16,72,256]{2,1,0:T(8,128)S(1)}, u32[]{:S(2)}, u32[]{:S(2)}) %collective-permute-start) | collective-permute-done | bytes 1179680 | tf_op jit(solution)/shard_map/ppermute | solution.py:142
  21.9 1.0 exponential_reduce_fusion
  22.9 0.1 broadcast_in_dim.66
  22.9 0.1 broadcast_in_dim.67
  23.0 0.3 select_add_fusion
  23.3 0.1 broadcast_in_dim.68
  23.4 0.0 copy-start.7
  23.4 1.2 pad_maximum_fusion
  24.6 0.0 copy-done.1
  24.6 7.7 %all-to-all-start = ((f32[32,40,256]{2,1,0:T(8,128)}), f32[32,40,256]{2,1,0:T(8,128)S(1)}, u32[]{:S(2)}, u32[]{:S(2)}) async-start(f32[32,40,256]{2,1,0:T(8,128)} %pad_maximum_fusion), calls=%async_computation | async-start | bytes 2621440 | tf_op jit(solution)/shard_map/all_to_all | solution.py:164
  32.4 0.1 fusion.48
  32.5 0.1 fusion.61
  32.6 0.0 copy-done.6
  32.7 3.5 %fusion.12 = f32[128,1,32,64]{0,3,2,1:T(8,128)} fusion(bf16[128,32,64]{0,2,1:T(8,128)(2,1)S(1)} %bitcast.98, f32[32,128]{1,0:T(8,128)S(1)} %copy-done.8, f32[32,128]{1,0:T(8,128)S(1)} %bitcast.102, f32[128,128]{1,0:T(8,128)S(1)} %fusion.61, pred[128,128]{1,0:T(8,128)(4,1)S(1)} %fusion.48), kind=kOutput, calls=%fused_computation.18 | convolution fusion | flops 404750336 | bytes 1687552 | tf_op jit(solution)/shard_map/gjts,sgjp->tgjp/dot_general | solution.py:174
  36.2 13.8 %all-to-all-done = f32[32,40,256]{2,1,0:T(8,128)S(1)} async-done(((f32[32,40,256]{2,1,0:T(8,128)}), f32[32,40,256]{2,1,0:T(8,128)S(1)}, u32[]{:S(2)}, u32[]{:S(2)}) %all-to-all-start) | async-done | bytes 1310752 | tf_op jit(solution)/shard_map/all_to_all | solution.py:164
  50.0 0.1 copy.33
  50.1 0.2 select_reduce_fusion
  50.3 1.7 %convolution_bitcast_fusion = f32[16,2,32,256]{3,0,2,1:T(8,128)S(1)} fusion(f32[16,2,40,256]{3,2,1,0:T(8,128)S(1)} %bitcast.93, f32[2,16,16]{2,1,0:T(8,128)S(1)} %select_reduce_fusion, pred[16,16]{1,0:T(8,128)(4,1)S(1)} %iota_compare_fusion.5), kind=kOutput, calls=%fused_computation.20 | convolution fusion | flops 50332160 | bytes 2361600 | tf_op jit(solution)/shard_map/ukd,dupn->kupn/dot_general | solution.py:187
  51.9 0.0 copy-start.2
  51.9 1.6 %copy.34 = f32[16,2,32,256]{3,2,1,0:T(8,128)} copy(f32[16,2,32,256]{3,0,2,1:T(8,128)S(1)} %convolution_bitcast_fusion) | data formatting | bytes 2097152 | tf_op jit(solution)/shard_map/ukd,dupn->kupn/transpose | solution.py:187
  53.5 6.2 %all-to-all-start.1 = ((f32[32,32,256]{2,1,0:T(8,128)}), f32[32,32,256]{2,1,0:T(8,128)S(1)}, u32[]{:S(2)}, u32[]{:S(2)}) async-start(f32[32,32,256]{2,1,0:T(8,128)} %bitcast.22), calls=%async_computation.1 | async-start | bytes 2097152 | tf_op jit(solution)/shard_map/all_to_all | solution.py:188
  59.7 0.0 all-gather.2.cloned.1.call-start
  59.8 1.4 %pad_maximum_fusion.1 = bf16[128,1,256]{2,0,1:T(8,128)(2,1)} fusion(bf16[128,1,128]{2,0,1:T(8,128)(2,1)} %bitcast.103, bf16[128,1,128]{2,0,1:T(8,128)(2,1)} %bitcast.104), kind=kLoop, calls=%fused_computation.51 | loop fusion | flops 131072 | bytes 131072 | tf_op jit(solution)/shard_map/concatenate | solution.py:222
  61.2 0.0 all-gather.2.cloned.1.call-update
  61.2 13.3 %all-to-all-done.1 = f32[32,32,256]{2,1,0:T(8,128)S(1)} async-done(((f32[32,32,256]{2,1,0:T(8,128)}), f32[32,32,256]{2,1,0:T(8,128)S(1)}, u32[]{:S(2)}, u32[]{:S(2)}) %all-to-all-start.1) | async-done | bytes 1048608 | tf_op jit(solution)/shard_map/all_to_all | solution.py:188
  74.5 2.4 %bitcast_select_fusion = (f32[16,64,256]{2,1,0:T(8,128)}, f32[16,64,256]{2,1,0:T(8,128)}) fusion(f32[16]{0:T(128)} %get-tuple-element.6, pred[]{:T(512)S(6)} %eq.42, f32[16,72,256]{2,1,0:T(8,128)S(1)} %copy-done.2, f32[16,72,256]{2,1,0:T(8,128)S(1)} %get-tuple-element.18, f32[16,64,256]{2,1,0:T(8,128)S(1)} %bitcast.96), kind=kLoop, calls=%fused_computation.35 | loop fusion | flops 1310720 | bytes 5242945 | tf_op jit(solution)/shard_map/jit(_where)/select_n | solution.py:195
  76.9 0.7 collective-permute-start.1
  79.9 1.3 %copy.36.low_ref = s32[128,1]{1,0:T(8,128)} copy(s32[128,1]{0,1:T(1,128)} %bitcast.109) | data formatting | bytes 1024 | tf_op jit(solution)/shard_map/broadcast_in_dim | solution.py:242
  81.2 0.6 pad_add_fusion.chunk_ref
  81.8 0.6 iota_add_fusion.high_ref
  82.5 0.0 collective-permute-done.1
  82.5 3.0 %fusion.24 = f32[128,1,32,64]{0,3,2,1:T(8,128)S(1)} fusion(f32[128,1,32,64]{0,3,2,1:T(8,128)} %fusion.12, s32[]{:T(128)S(6)} %select_n.108, f32[16,64,256]{2,1,0:T(8,128)S(1)} %collective-permute-done.1, f32[16,64,256]{2,1,0:T(8,128)} %get-tuple-element.13, f32[32]{0:T(128)} %param.18, f32[128,32]{0,1:T(8,128)S(1)} %get-tuple-element.19, ...), kind=kOutput, calls=%fused_computation.23 | convolution fusion | flops 807665664 | bytes 4800644 | tf_op jit(solution)/shard_map/tgn,gjpn->tgjp/dot_general | solution.py:201
  85.5 0.0 copy-start.4
  85.5 0.0 copy-start.9
  85.5 0.3 copy.35
  85.9 0.7 copy-done.4
  86.5 0.4 multiply_reduce_fusion
  87.0 20.0 %psum.7 = f32[128]{0:T(128)S(1)} all-reduce(f32[128]{0:T(128)S(1)} %multiply_reduce_fusion), channel_id=1, replica_groups=mesh['ctx'=32,'head'=8] {'head'}, use_global_device_ids=true, to_apply=%region_5.6 | all-reduce | flops 128 | bytes 1024 | tf_op jit(solution)/shard_map/psum | solution.py:208
  107.0 0.4 multiply_convert_fusion
  107.4 0.0 copy-start.3
  107.4 3.9 %fusion.28.query_ref = bf16[128,1024]{1,0:T(8,128)(2,1)} fusion(bf16[128,2048]{1,0:T(8,128)(2,1)S(1)} %multiply_convert_fusion, bf16[1,2048,1024]{2,1,0:T(8,128)(2,1)} %param.20), kind=kOutput, calls=%fused_computation.28 | convolution fusion | flops 537001984 | bytes 4980736 | tf_op jit(solution)/shard_map/tgf,gfo->tgo/dot_general | solution.py:214
  111.3 0.0 copy-done.3
  111.3 3.5 %all-gather.2.cloned.1.call-done = bf16[4096,1,256]{2,0,1:T(8,128)(2,1)} async-done(((bf16[128,1,256]{2,0,1:T(8,128)(2,1)}), bf16[4096,1,256]{2,0,1:T(8,128)(2,1)}) %all-gather.2.cloned.1.call-update) | async-done | bytes 2097168 | tf_op jit(solution)/shard_map/all_gather | solution.py:229
  114.8 11.1 %shard_map.131 = bf16[128,1024]{1,0:T(8,128)(2,1)} custom-call(s32[2]{0:T(128)} %pad_add_fusion.chunk_ref, bf16[128,1024]{1,0:T(8,128)(2,1)} %fusion.28.query_ref, bf16[4096,256]{1,0:T(8,128)(2,1)} %bitcast.99, s32[128,1]{1,0:T(8,128)} %copy.36.low_ref, s32[128,1]{1,0:T(8,128)} %iota_add_fusion.high_ref), custom_call_target="tpu_custom_call" | custom-call | tf_op jit(solution)/shard_map/pallas_call | solution.py:85
  (17 shorter events, 0.1 us)
Async XLA Ops:
  7.2 9.3 %copy-start = (bf16[128,256]{1,0:T(8,128)(2,1)S(1)}, bf16[128,256]{1,0:T(8,128)(2,1)}, u32[]{:S(2)}) copy-start(bf16[128,256]{1,0:T(8,128)(2,1)} %param.14) | copy-start | bytes 196612
  13.6 3.8 %copy-start.5 = (bf16[128,2048]{0,1:T(8,128)(2,1)}, bf16[128,2048]{0,1:T(8,128)(2,1)S(1)}, u32[]{:S(2)}) copy-start(bf16[128,2048]{0,1:T(8,128)(2,1)S(1)} %copy.29) | copy-start | bytes 1572868
  18.8 3.1 %collective-permute-start = (f32[16,72,256]{2,1,0:T(8,128)}, f32[16,72,256]{2,1,0:T(8,128)S(1)}, u32[]{:S(2)}, u32[]{:S(2)}) collective-permute-start(f32[16,72,256]{2,1,0:T(8,128)} %get-tuple-element.17), channel_id=1, source_target_pairs={{0,8},{8,0},{16,24},{24,16},{32,40},{40,32},{48,56},{56,48},{64,72... | collective-permute-start | bytes 3538952 | tf_op jit(solution)/shard_map/ppermute | solution.py:142
  21.9 2.7 %copy-start.1 = (f32[16,72,256]{2,1,0:T(8,128)}, f32[16,72,256]{2,1,0:T(8,128)S(1)}, u32[]{:S(2)}) copy-start(f32[16,72,256]{2,1,0:T(8,128)S(1)} %collective-permute-done) | copy-start | bytes 3538948
  23.4 9.1 %copy-start.7 = (bf16[128,256]{1,0:T(8,128)(2,1)S(1)}, bf16[128,256]{1,0:T(8,128)(2,1)}, u32[]{:S(2)}) copy-start(bf16[128,256]{1,0:T(8,128)(2,1)} %param.15) | copy-start | bytes 196612
  24.6 8.1 %copy-start.6 = (bf16[128,2048]{0,1:T(8,128)(2,1)S(1)}, bf16[128,2048]{0,1:T(8,128)(2,1)}, u32[]{:S(2)}) copy-start(bf16[128,2048]{0,1:T(8,128)(2,1)} %copy-done.5) | copy-start | bytes 1572868
  24.6 8.1 %copy-start.8 = (f32[32,128]{1,0:T(8,128)S(1)}, f32[32,128]{1,0:T(8,128)}, u32[]{:S(2)}) copy-start(f32[32,128]{1,0:T(8,128)} %param.16) | copy-start | bytes 49156
  24.6 25.4 %all-to-all-start = ((f32[32,40,256]{2,1,0:T(8,128)}), f32[32,40,256]{2,1,0:T(8,128)S(1)}, u32[]{:S(2)}, u32[]{:S(2)}) async-start(f32[32,40,256]{2,1,0:T(8,128)} %pad_maximum_fusion), calls=%async_computation | async-start | bytes 2621440 | tf_op jit(solution)/shard_map/all_to_all | solution.py:164
  51.9 22.6 %copy-start.2 = (f32[16,72,256]{2,1,0:T(8,128)S(1)}, f32[16,72,256]{2,1,0:T(8,128)}, u32[]{:S(2)}) copy-start(f32[16,72,256]{2,1,0:T(8,128)} %copy-done.1) | copy-start | bytes 3538948
  53.5 21.0 %all-to-all-start.1 = ((f32[32,32,256]{2,1,0:T(8,128)}), f32[32,32,256]{2,1,0:T(8,128)S(1)}, u32[]{:S(2)}, u32[]{:S(2)}) async-start(f32[32,32,256]{2,1,0:T(8,128)} %bitcast.22), calls=%async_computation.1 | async-start | bytes 2097152 | tf_op jit(solution)/shard_map/all_to_all | solution.py:188
  59.7 55.0 %all-gather.2.cloned.1.call-start = ((), (), s32[]{:S(2)}) async-start(), calls=%async_computation.2 | async-start | bytes 2162688 | tf_op jit(solution)/shard_map/all_gather | solution.py:229
  76.9 5.6 %collective-permute-start.1 = (f32[16,64,256]{2,1,0:T(8,128)}, f32[16,64,256]{2,1,0:T(8,128)S(1)}, u32[]{:S(2)}, u32[]{:S(2)}) collective-permute-start(f32[16,64,256]{2,1,0:T(8,128)} %get-tuple-element.14), channel_id=1, source_target_pairs={{0,8},{8,0},{16,24},{24,16},{32,40},{40,32},{48,56},{56,48},{64,72... | collective-permute-start | bytes 3145736 | tf_op jit(solution)/shard_map/ppermute | solution.py:192
  85.5 1.0 copy-start.4
  85.5 21.5 %copy-start.9 = (f32[2048]{0:T(1024)S(1)}, f32[2048]{0:T(1024)}, u32[]{:S(2)}) copy-start(f32[2048]{0:T(1024)} %param.19) | copy-start | bytes 24580
  107.4 3.9 %copy-start.3 = (bf16[128,2048]{1,0:T(8,128)(2,1)}, bf16[128,2048]{1,0:T(8,128)(2,1)S(1)}, u32[]{:S(2)}) copy-start(bf16[128,2048]{1,0:T(8,128)(2,1)S(1)} %multiply_convert_fusion) | copy-start | bytes 1572868
Sparse Core Ops, SparseCore 0:
  63.7 51.0 all-gather.1

commit v15 on v13

--- a/solution.py
+++ b/solution.py
@@ -15,7 +15,7 @@
 
 EPSILON = 1e-05
 NEG_FILL = -1e30
-KEY_CHUNK = 256
+KEY_CHUNK = 512
 
 
 def segment_ids(positions, doc_lengths):

time: 132 us -> 132 us (level)
  no operation moved by 1% of the time
where the time goes in v15:
time: 132 us; the launch traced here: 130 us
  waiting for transfers between devices  33.5 us (25%)
  blocking collectives  20 us (15%)
  between operations  18 us (14%)
  starting transfers between devices  14.7 us (11%)
  matrix products  14.2 us (11%)
  other arithmetic  13.4 us (10%)
  Pallas kernels  8.56 us (6%)
  local copies, waits for them, and re-layouts  7.88 us (6%)
    psum x1, blocking collectives, shards(): square_sum = lax.psum(square_local, 'head')  20 us
    all_to_all x1, waiting for transfers between devices, shards(): lax.all_to_all(payload, 'ctx', 0, 0, tiled=True)  13.8 us
    all_to_all x1, waiting for transfers between devices, shards(): lax.all_to_all(incoming_mine.reshape(ctx_count, part_rows, STATE), 'ctx',...  13.3 us
    pallas_call x1, Pallas kernels, flash_attention(): pl.pallas_call(attention_kernel, grid_spec=grid_spec, out_shape=jax.Shape...  8.56 us
    all_to_all x1, starting transfers between devices, shards(): lax.all_to_all(payload, 'ctx', 0, 0, tiled=True)  7.73 us
    all_to_all x1, starting transfers between devices, shards(): lax.all_to_all(incoming_mine.reshape(ctx_count, part_rows, STATE), 'ctx',...  6.21 us
    dot_general x1, matrix products, shards(): jnp.einsum('tgf,gfo->tgo', mixer_out.reshape(tok_rows, groups_dev, -1), q...  3.89 us
    dot_general x1, matrix products, shards(): jnp.einsum('gjts,sgjp->tgjp', mixing, input_f32, precision=highest)  3.52 us
  transfers between devices with their start and end apart: 5, of which 4 were waited for; matrix products, arithmetic and copies ran while one was open for 14% of the time, Pallas kernels for 0%

profile of v15, /device:TPU:4, one launch (start us, length us, event | category | flops | bytes accessed | tf_op | source)
XLA Modules:
  0.0 130.2 jit_solution(6694782681108784519)
XLA Ops:
  7.2 0.0 copy-start
  7.2 0.7 copy.30
  8.0 0.1 reduce.3
  8.1 1.3 fusion.51
  10.0 0.6 fusion.48
  10.7 0.6 slice.36
  11.2 0.8 fusion.42
  12.1 0.2 slice_reduce_fusion
  12.3 1.3 %copy.29 = bf16[128,2048]{0,1:T(8,128)(2,1)S(1)} copy(bf16[128,2048]{1,0:T(8,128)(2,1)} %param.12) | data formatting | bytes 1048576 | tf_op args[0]
  13.6 0.0 copy-start.5
  13.6 0.7 compare_convert_fusion.1
  14.3 0.6 slice.37
  15.6 0.8 multiply_bitcast_fusion
  16.4 0.1 bitcast_multiply_fusion.1
  16.4 0.0 copy-done
  16.4 1.0 fusion.40
  17.4 0.0 copy-done.5
  17.4 0.1 broadcast_in_dim.65
  17.6 1.3 fusion.26
  18.8 0.0 collective-permute-start
  18.8 3.1 %collective-permute-done = f32[16,72,256]{2,1,0:T(8,128)S(1)} collective-permute-done((f32[16,72,256]{2,1,0:T(8,128)}, f32[16,72,256]{2,1,0:T(8,128)S(1)}, u32[]{:S(2)}, u32[]{:S(2)}) %collective-permute-start) | collective-permute-done | bytes 1179680 | tf_op jit(solution)/shard_map/ppermute | solution.py:142
  21.9 1.0 exponential_reduce_fusion
  22.9 0.1 broadcast_in_dim.66
  22.9 0.1 broadcast_in_dim.67
  23.0 0.3 select_add_fusion
  23.3 0.1 broadcast_in_dim.68
  23.4 0.0 copy-start.7
  23.4 1.2 pad_maximum_fusion
  24.6 0.0 copy-done.1
  24.6 7.7 %all-to-all-start = ((f32[32,40,256]{2,1,0:T(8,128)}), f32[32,40,256]{2,1,0:T(8,128)S(1)}, u32[]{:S(2)}, u32[]{:S(2)}) async-start(f32[32,40,256]{2,1,0:T(8,128)} %pad_maximum_fusion), calls=%async_computation | async-start | bytes 2621440 | tf_op jit(solution)/shard_map/all_to_all | solution.py:164
  32.4 0.1 fusion.43
  32.5 0.0 copy-done.7
  32.5 0.1 fusion.55
  32.6 0.0 copy-done.6
  32.7 0.0 copy-done.8
  32.7 3.5 %fusion.15 = f32[128,1,32,64]{0,3,2,1:T(8,128)} fusion(bf16[128,32,64]{0,2,1:T(8,128)(2,1)S(1)} %bitcast.98, f32[32,128]{1,0:T(8,128)S(1)} %copy-done.8, f32[32,128]{1,0:T(8,128)S(1)} %bitcast.102, f32[128,128]{1,0:T(8,128)S(1)} %fusion.55, pred[128,128]{1,0:T(8,128)(4,1)S(1)} %fusion.43), kind=kOutput, calls=%fused_computation.20 | convolution fusion | flops 404750336 | bytes 1687552 | tf_op jit(solution)/shard_map/gjts,sgjp->tgjp/dot_general | solution.py:174
  36.2 13.8 %all-to-all-done = f32[32,40,256]{2,1,0:T(8,128)S(1)} async-done(((f32[32,40,256]{2,1,0:T(8,128)}), f32[32,40,256]{2,1,0:T(8,128)S(1)}, u32[]{:S(2)}, u32[]{:S(2)}) %all-to-all-start) | async-done | bytes 1310752 | tf_op jit(solution)/shard_map/all_to_all | solution.py:164
  50.0 0.1 copy.33
  50.1 0.2 select_reduce_fusion
  50.3 1.7 %convolution_bitcast_fusion = f32[16,2,32,256]{3,0,2,1:T(8,128)S(1)} fusion(f32[16,2,40,256]{3,2,1,0:T(8,128)S(1)} %bitcast.93, f32[2,16,16]{2,1,0:T(8,128)S(1)} %select_reduce_fusion, pred[16,16]{1,0:T(8,128)(4,1)S(1)} %iota_compare_fusion.5), kind=kOutput, calls=%fused_computation.21 | convolution fusion | flops 50332160 | bytes 2361600 | tf_op jit(solution)/shard_map/ukd,dupn->kupn/dot_general | solution.py:187
  51.9 1.6 %copy.34 = f32[16,2,32,256]{3,2,1,0:T(8,128)} copy(f32[16,2,32,256]{3,0,2,1:T(8,128)S(1)} %convolution_bitcast_fusion) | data formatting | bytes 2097152 | tf_op jit(solution)/shard_map/ukd,dupn->kupn/transpose | solution.py:187
  53.5 6.2 %all-to-all-start.1 = ((f32[32,32,256]{2,1,0:T(8,128)}), f32[32,32,256]{2,1,0:T(8,128)S(1)}, u32[]{:S(2)}, u32[]{:S(2)}) async-start(f32[32,32,256]{2,1,0:T(8,128)} %bitcast.22), calls=%async_computation.1 | async-start | bytes 2097152 | tf_op jit(solution)/shard_map/all_to_all | solution.py:188
  59.7 0.0 all-gather.2.cloned.1.call-start
  59.8 1.4 %pad_maximum_fusion.1 = bf16[128,1,256]{2,0,1:T(8,128)(2,1)} fusion(bf16[128,1,128]{2,0,1:T(8,128)(2,1)} %bitcast.103, bf16[128,1,128]{2,0,1:T(8,128)(2,1)} %bitcast.104), kind=kLoop, calls=%fused_computation.53 | loop fusion | flops 131072 | bytes 131072 | tf_op jit(solution)/shard_map/concatenate | solution.py:224
  61.2 0.0 all-gather.2.cloned.1.call-update
  61.2 13.3 %all-to-all-done.1 = f32[32,32,256]{2,1,0:T(8,128)S(1)} async-done(((f32[32,32,256]{2,1,0:T(8,128)}), f32[32,32,256]{2,1,0:T(8,128)S(1)}, u32[]{:S(2)}, u32[]{:S(2)}) %all-to-all-start.1) | async-done | bytes 1048608 | tf_op jit(solution)/shard_map/all_to_all | solution.py:188
  74.5 2.4 %bitcast_select_fusion.1 = (f32[16,64,256]{2,1,0:T(8,128)}, f32[16,64,256]{2,1,0:T(8,128)}) fusion(f32[16]{0:T(128)} %get-tuple-element.6, pred[]{:T(512)S(6)} %eq.42, f32[16,72,256]{2,1,0:T(8,128)S(1)} %copy-done.2, f32[16,72,256]{2,1,0:T(8,128)S(1)} %get-tuple-element.18, f32[16,64,256]{2,1,0:T(8,128)S(1)} %bitcast.96), kind=kLoop, calls=%fused_computation.37 | loop fusion | flops 1310720 | bytes 5242945 | tf_op jit(solution)/shard_map/jit(_where)/select_n | solution.py:195
  76.9 0.7 collective-permute-start.1
  79.9 1.3 %copy.36.low_ref = s32[128,1]{1,0:T(8,128)} copy(s32[128,1]{0,1:T(1,128)} %bitcast.109) | data formatting | bytes 1024 | tf_op jit(solution)/shard_map/broadcast_in_dim | solution.py:244
  81.2 0.6 pad_add_fusion.chunk_ref
  81.8 0.6 iota_add_fusion.high_ref
  82.5 0.0 collective-permute-done.1
  82.5 3.2 %fusion.20 = f32[128,1,32,64]{0,3,2,1:T(8,128)S(1)} fusion(f32[128,1,32,64]{0,3,2,1:T(8,128)} %fusion.15, f32[16,64,256]{2,1,0:T(8,128)S(1)} %collective-permute-done.1, f32[16,64,256]{2,1,0:T(8,128)} %get-tuple-element.13, pred[]{:T(512)S(6)} %eq.42, f32[32]{0:T(128)} %param.18, f32[128,32]{0,1:T(8,128)S(1)} %get-tuple-element.19, ...), kind=kOutput, calls=%fused_computation.24 | convolution fusion | flops 808189952 | bytes 4800641 | tf_op jit(solution)/shard_map/tgn,gjpn->tgjp/dot_general | solution.py:203
  85.6 0.0 copy-start.4
  85.6 0.0 copy-start.9
  85.6 0.3 copy.35
  86.0 0.7 copy-done.4
  86.7 0.4 multiply_reduce_fusion
  87.1 20.0 %psum.7 = f32[128]{0:T(128)S(1)} all-reduce(f32[128]{0:T(128)S(1)} %multiply_reduce_fusion), channel_id=1, replica_groups=mesh['ctx'=32,'head'=8] {'head'}, use_global_device_ids=true, to_apply=%region_5.6 | all-reduce | flops 128 | bytes 1024 | tf_op jit(solution)/shard_map/psum | solution.py:210
  107.1 0.4 multiply_convert_fusion
  107.5 0.0 copy-start.3
  107.5 3.9 %fusion.22.query_ref = bf16[128,1024]{1,0:T(8,128)(2,1)} fusion(bf16[128,2048]{1,0:T(8,128)(2,1)S(1)} %multiply_convert_fusion, bf16[1,2048,1024]{2,1,0:T(8,128)(2,1)} %param.20), kind=kOutput, calls=%fused_computation.29 | convolution fusion | flops 537001984 | bytes 4980736 | tf_op jit(solution)/shard_map/tgf,gfo->tgo/dot_general | solution.py:216
  111.4 3.4 %all-gather.2.cloned.1.call-done = bf16[4096,1,256]{2,0,1:T(8,128)(2,1)} async-done(((bf16[128,1,256]{2,0,1:T(8,128)(2,1)}), bf16[4096,1,256]{2,0,1:T(8,128)(2,1)}) %all-gather.2.cloned.1.call-update) | async-done | bytes 2097168 | tf_op jit(solution)/shard_map/all_gather | solution.py:231
  114.8 8.6 %shard_map.131 = bf16[128,1024]{1,0:T(8,128)(2,1)} custom-call(s32[2]{0:T(128)} %pad_add_fusion.chunk_ref, bf16[128,1024]{1,0:T(8,128)(2,1)} %fusion.22.query_ref, bf16[4096,256]{1,0:T(8,128)(2,1)} %bitcast.99, s32[128,1]{1,0:T(8,128)} %copy.36.low_ref, s32[128,1]{1,0:T(8,128)} %iota_add_fusion.high_ref), custom_call_target="tpu_custom_call" | custom-call | tf_op jit(solution)/shard_map/pallas_call | solution.py:85
  (17 shorter events, 0.1 us)
Async XLA Ops:
  7.2 9.3 %copy-start = (bf16[128,256]{1,0:T(8,128)(2,1)S(1)}, bf16[128,256]{1,0:T(8,128)(2,1)}, u32[]{:S(2)}) copy-start(bf16[128,256]{1,0:T(8,128)(2,1)} %param.14) | copy-start | bytes 196612
  13.6 3.8 %copy-start.5 = (bf16[128,2048]{0,1:T(8,128)(2,1)}, bf16[128,2048]{0,1:T(8,128)(2,1)S(1)}, u32[]{:S(2)}) copy-start(bf16[128,2048]{0,1:T(8,128)(2,1)S(1)} %copy.29) | copy-start | bytes 1572868
  18.8 3.1 %collective-permute-start = (f32[16,72,256]{2,1,0:T(8,128)}, f32[16,72,256]{2,1,0:T(8,128)S(1)}, u32[]{:S(2)}, u32[]{:S(2)}) collective-permute-start(f32[16,72,256]{2,1,0:T(8,128)} %get-tuple-element.17), channel_id=1, source_target_pairs={{0,8},{8,0},{16,24},{24,16},{32,40},{40,32},{48,56},{56,48},{64,72... | collective-permute-start | bytes 3538952 | tf_op jit(solution)/shard_map/ppermute | solution.py:142
  21.9 2.7 %copy-start.1 = (f32[16,72,256]{2,1,0:T(8,128)}, f32[16,72,256]{2,1,0:T(8,128)S(1)}, u32[]{:S(2)}) copy-start(f32[16,72,256]{2,1,0:T(8,128)S(1)} %collective-permute-done) | copy-start | bytes 3538948
  23.4 9.1 %copy-start.7 = (bf16[128,256]{1,0:T(8,128)(2,1)S(1)}, bf16[128,256]{1,0:T(8,128)(2,1)}, u32[]{:S(2)}) copy-start(bf16[128,256]{1,0:T(8,128)(2,1)} %param.15) | copy-start | bytes 196612
  24.6 8.1 %copy-start.6 = (bf16[128,2048]{0,1:T(8,128)(2,1)S(1)}, bf16[128,2048]{0,1:T(8,128)(2,1)}, u32[]{:S(2)}) copy-start(bf16[128,2048]{0,1:T(8,128)(2,1)} %copy-done.5) | copy-start | bytes 1572868
  24.6 8.1 %copy-start.8 = (f32[32,128]{1,0:T(8,128)S(1)}, f32[32,128]{1,0:T(8,128)}, u32[]{:S(2)}) copy-start(f32[32,128]{1,0:T(8,128)} %param.16) | copy-start | bytes 49156
  24.6 25.4 %all-to-all-start = ((f32[32,40,256]{2,1,0:T(8,128)}), f32[32,40,256]{2,1,0:T(8,128)S(1)}, u32[]{:S(2)}, u32[]{:S(2)}) async-start(f32[32,40,256]{2,1,0:T(8,128)} %pad_maximum_fusion), calls=%async_computation | async-start | bytes 2621440 | tf_op jit(solution)/shard_map/all_to_all | solution.py:164
  51.9 22.6 %copy-start.2 = (f32[16,72,256]{2,1,0:T(8,128)S(1)}, f32[16,72,256]{2,1,0:T(8,128)}, u32[]{:S(2)}) copy-start(f32[16,72,256]{2,1,0:T(8,128)} %copy-done.1) | copy-start | bytes 3538948
  53.5 21.0 %all-to-all-start.1 = ((f32[32,32,256]{2,1,0:T(8,128)}), f32[32,32,256]{2,1,0:T(8,128)S(1)}, u32[]{:S(2)}, u32[]{:S(2)}) async-start(f32[32,32,256]{2,1,0:T(8,128)} %bitcast.22), calls=%async_computation.1 | async-start | bytes 2097152 | tf_op jit(solution)/shard_map/all_to_all | solution.py:188
  59.7 55.0 %all-gather.2.cloned.1.call-start = ((), (), s32[]{:S(2)}) async-start(), calls=%async_computation.2 | async-start | bytes 2162688 | tf_op jit(solution)/shard_map/all_gather | solution.py:231
  76.9 5.6 %collective-permute-start.1 = (f32[16,64,256]{2,1,0:T(8,128)}, f32[16,64,256]{2,1,0:T(8,128)S(1)}, u32[]{:S(2)}, u32[]{:S(2)}) collective-permute-start(f32[16,64,256]{2,1,0:T(8,128)} %get-tuple-element.14), channel_id=1, source_target_pairs={{0,8},{8,0},{16,24},{24,16},{32,40},{40,32},{48,56},{56,48},{64,72... | collective-permute-start | bytes 3145736 | tf_op jit(solution)/shard_map/ppermute | solution.py:192
  85.6 1.0 copy-start.4
  85.6 21.5 %copy-start.9 = (f32[2048]{0:T(1024)S(1)}, f32[2048]{0:T(1024)}, u32[]{:S(2)}) copy-start(f32[2048]{0:T(1024)} %param.19) | copy-start | bytes 24580
  107.5 3.9 %copy-start.3 = (bf16[128,2048]{1,0:T(8,128)(2,1)}, bf16[128,2048]{1,0:T(8,128)(2,1)S(1)}, u32[]{:S(2)}) copy-start(bf16[128,2048]{1,0:T(8,128)(2,1)S(1)} %multiply_convert_fusion) | copy-start | bytes 1572868
Sparse Core Ops, SparseCore 0:
  63.7 51.0 all-gather.1
